TPU v7x, 512 devices: a whole 4x4x16 slice. The times are simulated.
512 devices in a mesh: seq: 64 (over x, z), tp: 8 (over y, core).
Axes of the slice: x: 4, y: 4, z: 16, core: 2. Of those that a mesh axis runs over, the one named last changes fastest.
Arguments:
- queries: bfloat16 [64, 4, 8192], P('seq', None, 'tp'), may hold values from -40 to 40
- new_keys: bfloat16 [64, 4, 1024], P('seq', None, 'tp'), may hold values from -6 to 6
- new_values: bfloat16 [64, 4, 1024], P('seq', None, 'tp'), may hold values from -6 to 6
- prefix_keys: bfloat16 [8, 12288, 1024], P(None, 'seq', 'tp'), may hold values from -8 to 8
- prefix_values: bfloat16 [8, 12288, 1024], P(None, 'seq', 'tp'), may hold values from -6 to 6
- page_keys: bfloat16 [1024, 64, 1024], P('seq', None, 'tp'), may hold values from -6 to 6
- page_values: bfloat16 [1024, 64, 1024], P('seq', None, 'tp'), may hold values from -6 to 6
- out_weight: bfloat16 [8192, 8192], P('tp', 'seq'), may hold values from -0.5 to 0.5
- group_of: int32 [64], replicated, may hold values from 0 to 7, as said below
- prefix_len: int32 [8], replicated, may hold values from 2 to 12288, as said below
- total_len: int32 [64], replicated, may hold values from 3 to 16384, as said below
- page_owner: int32 [1024], P('seq'), may hold values from 0 to 63, as said below
- page_slot: int32 [1024], P('seq'), may hold values from 0 to 63, as said below
- new_valid: int32 [64, 4], replicated, may hold values from 0 to 1, as said below
Outputs:
- attn_out: bfloat16 [256, 8192], P('tp', 'seq')
Inputs may be any that keep to these rules, and one draw needn't show every extreme that they name: `group_of`: every one of the 8 groups has at least one request. `prefix_len`: some group's prefix holds exactly 12288 tokens. `page_owner`: every request owns at least one page and at most 64 pages; one request owns exactly 64. `page_slot`: the pages of one request carry the slots 0, 1, 2 and so on, each once. A request's pages are full except the one of its highest slot, which holds 1 to 64 tokens; total_len is its group's prefix length plus these tokens. `new_valid`: each row is a run of ones followed by zeros, and its first entry is one.
All inputs are finite; a program needn't handle non-finite values.
Results may differ from a plain program's by a relative error of at most 0.022.
Values may be sent and summed in bfloat16 or wider, within the bound.
No kernel may reach another device: no remote copies, remote signals or barrier semaphores. Data moves between devices by JAX's collectives and lax.ppermute only.
A program may use at most 192 MiB of HBM per device.

v0:
```python
import jax
import jax.numpy as jnp
from jax import lax
from jax.sharding import PartitionSpec as P

HEAD_DIM = 128
HPK = 8
GROUPS = 8
NEW = 4


NEG = -1e30


def merged(part, axis, combine):
    gathered = jax.tree.map(lambda a: lax.all_gather(a, axis), part)

    def take(source):
        return jax.tree.map(lambda a: lax.dynamic_index_in_dim(a, source, 0, False), gathered)

    return lax.fori_loop(
        1, lax.axis_size(axis), lambda source, state: combine(state, take(source)), take(0)
    )


def softmax_part(scores, key_mask):
    masked = jnp.where(key_mask, scores, NEG)
    row_peak = jnp.max(masked, axis=-1)
    weights = jnp.where(key_mask, jnp.exp(masked - row_peak[..., None]), 0.0)
    return (row_peak, jnp.sum(weights, axis=-1), weights.astype(jnp.bfloat16))


def combine(first_part, second_part):
    peak_a, total_a, out_a = first_part
    peak_b, total_b, out_b = second_part
    top_peak = jnp.maximum(peak_a, peak_b)
    factor_a = jnp.exp(peak_a - top_peak)
    factor_b = jnp.exp(peak_b - top_peak)
    return (
        top_peak,
        total_a * factor_a + total_b * factor_b,
        out_a * factor_a[..., None] + out_b * factor_b[..., None],
    )


def local(
    queries,
    new_keys,
    new_values,
    prefix_keys,
    prefix_values,
    page_keys,
    page_values,
    out_weight,
    group_of,
    prefix_len,
    total_len,
    page_owner,
    page_slot,
    new_valid,
):
    req_dev = queries.shape[0]
    seq_count = lax.axis_size("seq")
    requests = req_dev * seq_count
    kv_local = new_keys.shape[2] // HEAD_DIM
    heads_local = kv_local * HPK
    score_scale = HEAD_DIM ** (-0.5)
    seq_idx = lax.axis_index("seq")
    gathered = lax.all_gather(queries, "seq", axis=0, tiled=True)
    query_all = gathered.reshape(requests, NEW, kv_local, HPK, HEAD_DIM)
    group_hot = group_of[:, None] == jnp.arange(GROUPS, dtype=jnp.int32)[None, :]
    own_prefix = jnp.sum(jnp.where(group_hot, prefix_len[None, :], 0), axis=1)
    suffix_len = total_len - own_prefix
    pre_dev = prefix_keys.shape[1]
    positions = seq_idx * pre_dev + jnp.arange(pre_dev, dtype=jnp.int32)
    pre_keys = prefix_keys.reshape(GROUPS, pre_dev, kv_local, HEAD_DIM)
    pre_values = prefix_values.reshape(GROUPS, pre_dev, kv_local, HEAD_DIM)
    partial_value = (
        jnp.full((requests, NEW, kv_local, HPK), NEG, jnp.float32),
        jnp.zeros((requests, NEW, kv_local, HPK), jnp.float32),
        jnp.zeros((requests, NEW, kv_local, HPK, HEAD_DIM), jnp.float32),
    )
    for group_idx in range(GROUPS):
        scores = (
            jnp.einsum(
                "rjkhd,ikd->rjkhi",
                query_all,
                pre_keys[group_idx],
                preferred_element_type=jnp.float32,
            )
            * score_scale
        )
        member = group_hot[:, group_idx]
        live_keys = positions < prefix_len[group_idx]
        key_mask = member[:, None, None, None, None] & live_keys[None, None, None, None, :]
        row_peak, row_total, weights = softmax_part(scores, key_mask)
        values = jnp.einsum(
            "rjkhi,ikd->rjkhd", weights, pre_values[group_idx], preferred_element_type=jnp.float32
        )
        chosen = member[:, None, None, None]
        partial_value = (
            jnp.where(chosen, row_peak, partial_value[0]),
            jnp.where(chosen, row_total, partial_value[1]),
            jnp.where(chosen[..., None], values, partial_value[2]),
        )
    prefix_part = partial_value
    page_count = page_keys.shape[0]
    page_len = page_keys.shape[1]
    key_pages = page_keys.reshape(page_count, page_len, kv_local, HEAD_DIM)
    value_pages = page_values.reshape(page_count, page_len, kv_local, HEAD_DIM)
    owner_hot = page_owner[:, None] == jnp.arange(requests, dtype=jnp.int32)[None, :]
    own_suffix = jnp.sum(jnp.where(owner_hot, suffix_len[None, :], 0), axis=1)
    page_queries = jnp.take(query_all, page_owner, axis=0)
    scores = (
        jnp.einsum("pjkhd,pikd->pjkhi", page_queries, key_pages, preferred_element_type=jnp.float32)
        * score_scale
    )
    offsets = page_slot[:, None] * page_len + jnp.arange(page_len, dtype=jnp.int32)[None, :]
    live_keys = offsets < own_suffix[:, None]
    page_peak, page_total, weights = softmax_part(scores, live_keys[:, None, None, None, :])
    page_out = jnp.einsum(
        "pjkhi,pikd->pjkhd", weights, value_pages, preferred_element_type=jnp.float32
    )
    owner_wide = owner_hot[:, :, None, None, None]
    device_peak = jnp.max(jnp.where(owner_wide, page_peak[:, None], NEG), axis=0)
    page_back = jnp.max(jnp.where(owner_wide, device_peak[None], NEG), axis=1)
    factor = jnp.exp(page_peak - page_back)
    owner_float = owner_hot.astype(jnp.float32)
    suffix_total = jnp.einsum(
        "pr,pjkh->rjkh", owner_float, page_total * factor, precision=lax.Precision.HIGHEST
    )
    suffix_out = jnp.einsum(
        "pr,pjkhd->rjkhd",
        owner_float,
        page_out * factor[..., None],
        precision=lax.Precision.HIGHEST,
    )
    partial_value = combine(prefix_part, (device_peak, suffix_total, suffix_out))
    row_start = seq_idx * req_dev
    local_queries = queries.reshape(req_dev, NEW, kv_local, HPK, HEAD_DIM)
    local_keys = new_keys.reshape(req_dev, NEW, kv_local, HEAD_DIM)
    local_values = new_values.reshape(req_dev, NEW, kv_local, HEAD_DIM)
    valid_local = lax.dynamic_slice_in_dim(new_valid, row_start, req_dev, 0)
    scores = (
        jnp.einsum(
            "rjkhd,rikd->rjkhi", local_queries, local_keys, preferred_element_type=jnp.float32
        )
        * score_scale
    )
    causal = jnp.arange(NEW, dtype=jnp.int32)[None, :] <= jnp.arange(NEW, dtype=jnp.int32)[:, None]
    key_mask = causal[None, :, None, None, :] & (valid_local[:, None, None, None, :] == 1)
    row_peak, row_total, weights = softmax_part(scores, key_mask)
    new_out = jnp.einsum(
        "rjkhi,rikd->rjkhd", weights, local_values, preferred_element_type=jnp.float32
    )
    own_rows = (
        lax.dynamic_slice_in_dim(partial_value[0], row_start, req_dev, 0),
        lax.dynamic_slice_in_dim(partial_value[1], row_start, req_dev, 0),
        lax.dynamic_slice_in_dim(partial_value[2], row_start, req_dev, 0),
    )
    own_part = combine(own_rows, (row_peak, row_total, new_out))
    partial_value = (
        lax.dynamic_update_slice_in_dim(partial_value[0], own_part[0], row_start, 0),
        lax.dynamic_update_slice_in_dim(partial_value[1], own_part[1], row_start, 0),
        lax.dynamic_update_slice_in_dim(partial_value[2], own_part[2], row_start, 0),
    )
    final_peak, final_total, final_out = merged(partial_value, "seq", combine)
    valid_rows = new_valid.astype(jnp.float32)[:, :, None, None, None]
    attention = (final_out / final_total[..., None] * valid_rows).astype(jnp.bfloat16)
    attention = attention.reshape(requests * NEW, heads_local * HEAD_DIM)
    terms = jnp.dot(attention, out_weight, preferred_element_type=jnp.float32)
    summed = lax.psum_scatter(terms.astype(jnp.bfloat16), "tp", scatter_dimension=0, tiled=True)
    return summed


def solution(mesh):
    placed = (
        P("seq", None, "tp"),
        P("seq", None, "tp"),
        P("seq", None, "tp"),
        P(None, "seq", "tp"),
        P(None, "seq", "tp"),
        P("seq", None, "tp"),
        P("seq", None, "tp"),
        P("tp", "seq"),
        P(),
        P(),
        P(),
        P("seq"),
        P("seq"),
        P(),
    )
    return jax.shard_map(
        local, mesh=mesh, in_specs=placed, out_specs=P("tp", "seq"), check_vma=False
    )
```

profile of v0, /device:TPU:1, one launch (start us, length us, event | category | flops | bytes accessed | tf_op | source)
XLA Modules:
  0.0 936.0 jit_solution(16358263161853906716)
XLA Ops:
  12.8 81.7 %all_gather.25 = bf16[64,4,1024]{2,1,0:T(4,128)(2,1)S(1)} all-gather(bf16[1,4,1024]{2,1,0:T(4,128)(2,1)} %param.16), channel_id=1, replica_groups=mesh['seq'=64,'tp'=8] {'seq'}, dimensions={0}, use_global_device_ids=true | all-gather | bytes 532480 | tf_op jit(solution)/shard_map/all_gather | solution.py:69
  101.5 1.9 fusion.11
  104.7 1.9 fusion.10
  106.7 2.0 fusion.9
  125.0 2.3 fusion.58
  127.3 2.4 fusion.57
  129.7 2.3 fusion.56
  132.0 2.3 fusion.55
  134.3 2.3 fusion.54
  136.7 2.3 fusion.53
  139.0 2.3 fusion.52
  145.3 2.4 fusion.72
  160.9 3.2 fusion.150
  166.4 81.5 %all_gather.27 = f32[64,64,4,1,8]{1,4,3,2,0:T(8,128)S(1)} all-gather(f32[1,64,4,1,8]{1,4,3,2,0:T(8,128)S(1)} %bitcast.588), channel_id=1, replica_groups=mesh['seq'=64,'tp'=8] {'seq'}, dimensions={0}, use_global_device_ids=true | all-gather | bytes 532480 | tf_op jit(solution)/shard_map/all_gather | solution.py:16
  247.9 92.0 %all_gather.30 = f32[64,64,4,1,8]{1,4,3,2,0:T(8,128)} all-gather(f32[1,64,4,1,8]{1,4,3,2,0:T(8,128)S(1)} %bitcast.584), channel_id=1, replica_groups=mesh['seq'=64,'tp'=8] {'seq'}, dimensions={0}, use_global_device_ids=true | all-gather | bytes 532480 | tf_op jit(solution)/shard_map/all_gather | solution.py:16
  340.6 367.8 %all-gather.2.cloned.1.call-done = f32[64,64,4,1,8,128]{5,4,3,2,1,0:T(8,128)} async-done(((f32[1,64,4,1,8,128]{5,4,3,2,1,0:T(8,128)}), f32[64,64,4,1,8,128]{5,4,3,2,1,0:T(8,128)}) %all-gather.2.cloned.1.call-update) | async-done | bytes 67108880 | tf_op jit(solution)/shard_map/all_gather | solution.py:16
  709.7 184.2 %while.19 = (s32[]{:T(128)}, f32[64,4,1,8]{0,3,2,1:T(8,128)S(1)}, f32[64,4,1,8]{0,3,2,1:T(8,128)S(1)}, f32[64,4,1,8,128]{4,3,2,1,0:T(8,128)S(1)}, f32[64,64,4,1,...) while((s32[]{:T(128)}, f32[64,4,1,8]{0,3,2,1:T(8,128)S(1)}, ...), condition=%wide.region_25.26_spmd, body=%wide.region_24.25_spmd.sunk | while | flops 800773 | bytes 3301531 | solution.py:21
  710.7 1.9 fusion.182
  713.7 1.9 fusion.182
  716.6 1.9 fusion.182
  719.5 1.9 fusion.182
  722.4 1.9 fusion.182
  725.4 1.9 fusion.182
  728.3 1.9 fusion.182
  731.2 1.9 fusion.182
  734.1 1.9 fusion.182
  737.1 1.9 fusion.182
  740.0 1.9 fusion.182
  742.9 1.9 fusion.182
  745.8 1.9 fusion.182
  748.7 1.9 fusion.182
  751.7 1.9 fusion.182
  754.6 1.9 fusion.182
  757.5 1.9 fusion.182
  760.4 1.9 fusion.182
  763.4 1.9 fusion.182
  766.3 1.9 fusion.182
  769.2 1.9 fusion.182
  778.0 1.9 fusion.182
  783.8 1.9 fusion.182
  798.4 1.9 fusion.182
  818.9 1.9 fusion.182
  833.5 1.9 fusion.182
  839.3 1.9 fusion.182
  854.0 1.9 fusion.182
  874.4 1.9 fusion.182
  889.0 1.9 fusion.182
  895.5 33.7 %reduce-scatter.2.cloned.1.call-done = bf16[32,128]{1,0:T(8,128)(2,1)} async-done(((bf16[256,128]{1,0:T(8,128)(2,1)}), bf16[32,128]{1,0:T(8,128)(2,1)}) %reduce-scatter.2.cloned.1.call-update) | async-done | bytes 8208 | tf_op jit(solution)/shard_map/reduce_scatter | solution.py:172
  (615 shorter events, 176.8 us)
Async XLA Ops:
  6.5 137.5 %copy-start = (bf16[16,64,128]{2,1,0:T(8,128)(2,1)S(1)}, bf16[16,64,128]{2,1,0:T(8,128)(2,1)}, u32[]{:S(2)}) copy-start(bf16[16,64,128]{2,1,0:T(8,128)(2,1)} %param.22) | copy-start | bytes 786436
  6.5 701.8 %all-gather.2.cloned.1.call-start = ((), (), s32[]{:S(2)}) async-start(), calls=%async_computation.1 | async-start | bytes 68157440 | tf_op jit(solution)/shard_map/all_gather | solution.py:16
  94.4 7.0 copy-start.20
  97.9 5.5 copy-start.50
  97.9 6.7 copy-start.54
  97.9 10.8 %copy-start.61 = (pred[64]{0:T(512)(128)(4,1)}, pred[64]{0:T(512)(128)(4,1)S(1)}, u32[]{:S(2)}) copy-start(pred[64]{0:T(512)(128)(4,1)S(1)} %get-tuple-element.261) | copy-start | bytes 196
  98.0 13.3 %copy-start.65 = (pred[64]{0:T(512)(128)(4,1)}, pred[64]{0:T(512)(128)(4,1)S(1)}, u32[]{:S(2)}) copy-start(pred[64]{0:T(512)(128)(4,1)S(1)} %get-tuple-element.262) | copy-start | bytes 196
  98.0 14.6 %copy-start.69 = (pred[64]{0:T(512)(128)(4,1)}, pred[64]{0:T(512)(128)(4,1)S(1)}, u32[]{:S(2)}) copy-start(pred[64]{0:T(512)(128)(4,1)S(1)} %get-tuple-element.263) | copy-start | bytes 196
  98.0 17.2 %copy-start.73 = (pred[64]{0:T(512)(128)(4,1)}, pred[64]{0:T(512)(128)(4,1)S(1)}, u32[]{:S(2)}) copy-start(pred[64]{0:T(512)(128)(4,1)S(1)} %get-tuple-element.264) | copy-start | bytes 196
  98.0 18.7 %copy-start.77 = (pred[64]{0:T(512)(128)(4,1)}, pred[64]{0:T(512)(128)(4,1)S(1)}, u32[]{:S(2)}) copy-start(pred[64]{0:T(512)(128)(4,1)S(1)} %get-tuple-element.257) | copy-start | bytes 196
  103.4 17.9 %copy-start.14 = (f32[64,4,8]{0,2,1:T(8,128)}, f32[64,4,8]{0,2,1:T(8,128)S(1)}, u32[]{:S(2)}) copy-start(f32[64,4,8]{0,2,1:T(8,128)S(1)} %get-tuple-element.277) | copy-start | bytes 24580
  106.6 14.7 %copy-start.17 = (f32[64,4,8]{0,2,1:T(8,128)}, f32[64,4,8]{0,2,1:T(8,128)S(1)}, u32[]{:S(2)}) copy-start(f32[64,4,8]{0,2,1:T(8,128)S(1)} %get-tuple-element.279) | copy-start | bytes 24580
  116.0 4.7 copy-start.48
  116.0 4.7 copy-start.51
  116.0 5.3 copy-start.62
  116.0 5.3 copy-start.66
  116.0 5.3 copy-start.70
  116.0 5.3 copy-start.74
  117.9 7.0 copy-start.60
  141.3 9.4 %copy-start.4 = (bf16[64,4,8,192]{3,0,2,1:T(8,128)(2,1)S(1)}, bf16[64,4,8,192]{3,0,2,1:T(8,128)(2,1)}, u32[]{:S(2)}) copy-start(bf16[64,4,8,192]{3,0,2,1:T(8,128)(2,1)} %get-tuple-element.251) | copy-start | bytes 2359300
  145.3 7.1 copy-start.10
  145.3 7.1 copy-start.52
  160.2 5.2 copy-start.83
  160.2 5.2 copy-start.81
  160.2 5.3 copy-start.34
  160.3 5.4 copy-start.31
  160.3 5.4 copy-start.32
  160.3 5.4 copy-start.37
  160.3 5.4 copy-start.38
  160.3 5.4 copy-start.39
  160.3 5.4 copy-start.40
  160.3 5.4 copy-start.41
  160.3 5.4 copy-start.42
  160.3 5.4 copy-start.43
  160.3 5.4 copy-start.44
  160.4 5.4 copy-start.49
  160.4 5.4 copy-start.53
  160.4 5.4 copy-start.57
  160.4 5.4 copy-start.64
  160.4 5.4 copy-start.68
  160.4 5.4 copy-start.72
  160.4 5.4 copy-start.76
  160.4 5.4 copy-start.80
  160.4 5.4 copy-start.84
  160.5 5.7 copy-start.16
  160.5 5.7 copy-start.19
  165.3 763.9 %reduce-scatter.2.cloned.1.call-start = ((), (), s32[]{:S(2)}) async-start(), calls=%async_computation.2 | async-start | bytes 73728 | tf_op jit(solution)/shard_map/reduce_scatter | solution.py:172
  709.7 184.9 %copy-start.90 = (bf16[1024,128]{1,0:T(8,128)(2,1)S(1)}, bf16[1024,128]{1,0:T(8,128)(2,1)}, u32[]{:S(2)}) copy-start(bf16[1024,128]{1,0:T(8,128)(2,1)} %param.23) | copy-start | bytes 786436
  (46 other events, 111.5 us)
Sparse Core Ops, SparseCore 0:
  165.4 542.8 all-gather.1
  895.6 33.5 reduce-scatter.1
where the time goes:
time: 943 us; the launch traced here: 936 us
  waiting for transfers between devices  401 us (43%)
  blocking collectives  255 us (27%)
  other arithmetic  209 us (22%)
  local copies, waits for them, and re-layouts  29.1 us (3%)
  matrix products  23.3 us (2%)
  between operations  14.7 us (2%)
    all_gather x1, waiting for transfers between devices, merged(): gathered = jax.tree.map(lambda a: lax.all_gather(a, axis), part)  368 us
    all_gather x2, blocking collectives, merged(): gathered = jax.tree.map(lambda a: lax.all_gather(a, axis), part)  174 us
    add x63, other arithmetic, combine(): out_a * factor_a[..., None] + out_b * factor_b[..., None]  119 us
    all_gather x1, blocking collectives, local(): gathered = lax.all_gather(queries, 'seq', axis=0, tiled=True)  81.7 us
    mul x63, other arithmetic, combine(): out_b * factor_b[..., None]  46.8 us
    reduce_scatter x1, waiting for transfers between devices, local(): lax.psum_scatter(terms.astype(jnp.bfloat16), 'tp', scatter_dimension=0, t...  33.7 us
  transfers between devices with their start and end apart: 2, of which 2 were waited for; matrix products, arithmetic and copies ran while one was open for 0% of the time, Pallas kernels for 0%

commit v1 on v0

v1 whole, which is shorter than its diff:
```python
import jax
import jax.numpy as jnp
from jax import lax
from jax.sharding import PartitionSpec as P

HEAD_DIM = 128
HPK = 8
GROUPS = 8
NEW = 4


NEG = -1e30


def local(
    queries,
    new_keys,
    new_values,
    prefix_keys,
    prefix_values,
    page_keys,
    page_values,
    out_weight,
    group_of,
    prefix_len,
    total_len,
    page_owner,
    page_slot,
    new_valid,
):
    req_dev = queries.shape[0]
    seq_count = lax.axis_size("seq")
    requests = req_dev * seq_count
    kv_local = new_keys.shape[2] // HEAD_DIM
    heads_local = kv_local * HPK
    score_scale = HEAD_DIM ** (-0.5)
    seq_idx = lax.axis_index("seq")
    gathered = lax.all_gather(queries, "seq", axis=0, tiled=True)
    query_all = gathered.reshape(requests, NEW, kv_local, HPK, HEAD_DIM)

    group_hot = group_of[:, None] == jnp.arange(GROUPS, dtype=jnp.int32)[None, :]
    own_prefix = jnp.sum(jnp.where(group_hot, prefix_len[None, :], 0), axis=1)
    suffix_len = total_len - own_prefix

    pre_dev = prefix_keys.shape[1]
    page_count = page_keys.shape[0]
    page_len = page_keys.shape[1]
    keys = jnp.concatenate(
        [
            prefix_keys.reshape(GROUPS * pre_dev, kv_local, HEAD_DIM),
            page_keys.reshape(page_count * page_len, kv_local, HEAD_DIM),
            new_keys.reshape(req_dev * NEW, kv_local, HEAD_DIM),
        ],
        axis=0,
    )
    values = jnp.concatenate(
        [
            prefix_values.reshape(GROUPS * pre_dev, kv_local, HEAD_DIM),
            page_values.reshape(page_count * page_len, kv_local, HEAD_DIM),
            new_values.reshape(req_dev * NEW, kv_local, HEAD_DIM),
        ],
        axis=0,
    )

    req_ids = jnp.arange(requests, dtype=jnp.int32)
    positions = seq_idx * pre_dev + jnp.arange(pre_dev, dtype=jnp.int32)
    pre_live = positions[None, :] < prefix_len[:, None]
    pre_mask = group_hot[:, :, None] & pre_live[None, :, :]
    pre_mask = pre_mask.reshape(requests, 1, GROUPS * pre_dev)
    pre_mask = jnp.broadcast_to(pre_mask, (requests, NEW, GROUPS * pre_dev))
    owner_hot = req_ids[:, None] == page_owner[None, :]
    offsets = page_slot[:, None] * page_len + jnp.arange(page_len, dtype=jnp.int32)[None, :]
    page_live = offsets[None, :, :] < suffix_len[:, None, None]
    page_mask = (owner_hot[:, :, None] & page_live).reshape(requests, 1, page_count * page_len)
    page_mask = jnp.broadcast_to(page_mask, (requests, NEW, page_count * page_len))
    new_owner = seq_idx * req_dev + jnp.arange(req_dev, dtype=jnp.int32)
    tok = jnp.arange(NEW, dtype=jnp.int32)
    causal = tok[None, :] <= tok[:, None]
    new_live = new_valid == 1
    new_mask = (
        (req_ids[:, None, None, None] == new_owner[None, None, :, None])
        & causal[None, :, None, :]
        & new_live[:, None, None, :]
    ).reshape(requests, NEW, req_dev * NEW)
    key_mask = jnp.concatenate([pre_mask, page_mask, new_mask], axis=2)
    key_mask = key_mask[:, :, None, None, :]

    scores = (
        jnp.einsum("rjkhd,nkd->rjkhn", query_all, keys, preferred_element_type=jnp.float32)
        * score_scale
    )
    masked = jnp.where(key_mask, scores, NEG)
    row_peak = jnp.max(masked, axis=-1)
    weights = jnp.where(key_mask, jnp.exp(masked - row_peak[..., None]), 0.0)
    row_total = jnp.sum(weights, axis=-1)
    out = jnp.einsum(
        "rjkhn,nkd->rjkhd", weights.astype(jnp.bfloat16), values, preferred_element_type=jnp.float32
    )

    top_peak = lax.pmax(row_peak, "seq")
    factor = jnp.exp(row_peak - top_peak)
    final_total, final_out = lax.psum((row_total * factor, out * factor[..., None]), "seq")
    valid_rows = new_valid.astype(jnp.float32)[:, :, None, None, None]
    attention = (final_out / final_total[..., None] * valid_rows).astype(jnp.bfloat16)
    attention = attention.reshape(requests * NEW, heads_local * HEAD_DIM)
    terms = jnp.dot(attention, out_weight, preferred_element_type=jnp.float32)
    summed = lax.psum_scatter(terms.astype(jnp.bfloat16), "tp", scatter_dimension=0, tiled=True)
    return summed


def solution(mesh):
    placed = (
        P("seq", None, "tp"),
        P("seq", None, "tp"),
        P("seq", None, "tp"),
        P(None, "seq", "tp"),
        P(None, "seq", "tp"),
        P("seq", None, "tp"),
        P("seq", None, "tp"),
        P("tp", "seq"),
        P(),
        P(),
        P(),
        P("seq"),
        P("seq"),
        P(),
    )
    return jax.shard_map(
        local, mesh=mesh, in_specs=placed, out_specs=P("tp", "seq"), check_vma=False
    )
```

time: 943 us -> 739 us (0.78)
  blocking collectives: 255 us -> 523 us
  waiting for transfers between devices: 401 us -> 161 us
  other arithmetic: 209 us -> 13.4 us
  local copies, waits for them, and re-layouts: 29.1 us -> 10.2 us
    all_gather x1 -> x0, waiting for transfers between devices: 368 us -> none  [merged(): gathered = jax.tree.map(lambda a: lax.all_gather(a, axis), part)]
    pmax x0 -> x1, blocking collectives: none -> 222 us  [local(): top_peak = lax.pmax(row_peak, 'seq')]
    psum x0 -> x1, blocking collectives: none -> 220 us  [local(): lax.psum((row_total * factor, out * factor[..., None]), 'seq')]
    all_gather x2 -> x0, blocking collectives: 174 us -> none  [merged(): gathered = jax.tree.map(lambda a: lax.all_gather(a, axis), part)]
    add x63 -> x2, other arithmetic: 119 us -> 0.01 us  [the longest x1 0.01 us: local(): page_slot[:, None] * page_len]
    psum x0 -> x1, waiting for transfers between devices: none -> 116 us  [local(): lax.psum((row_total * factor, out * factor[..., None]), 'seq')]
    mul x127 -> x0, other arithmetic: 49.2 us -> none  [the longest x63 46.8 us: combine(): out_b * factor_b[..., None]]
    another operation x8 -> x0, other arithmetic: 17.7 us -> none
where the time goes in v1:
time: 739 us; the launch traced here: 738 us
  blocking collectives  523 us (71%)
  waiting for transfers between devices  161 us (22%)
  matrix products  16.7 us (2%)
  between operations  13.7 us (2%)
  other arithmetic  13.4 us (2%)
  local copies, waits for them, and re-layouts  10.2 us (1%)
    pmax x1, blocking collectives, local(): top_peak = lax.pmax(row_peak, 'seq')  222 us
    psum x1, blocking collectives, local(): lax.psum((row_total * factor, out * factor[..., None]), 'seq')  220 us
    psum x1, waiting for transfers between devices, local(): lax.psum((row_total * factor, out * factor[..., None]), 'seq')  116 us
    all_gather x1, blocking collectives, local(): gathered = lax.all_gather(queries, 'seq', axis=0, tiled=True)  81.7 us
    reduce_scatter x1, waiting for transfers between devices, local(): lax.psum_scatter(terms.astype(jnp.bfloat16), 'tp', scatter_dimension=0, t...  44.8 us
  transfers between devices with their start and end apart: 2, of which 2 were waited for; matrix products, arithmetic and copies ran while one was open for 0% of the time, Pallas kernels for 0%

profile of v1, /device:TPU:1, one launch (start us, length us, event | category | flops | bytes accessed | tf_op | source)
XLA Modules:
  0.0 738.2 jit_solution(732492033588366109)
XLA Ops:
  6.5 0.0 copy-start
  6.5 0.0 all-reduce.2.cloned.1.call-start
  6.5 0.8 broadcast_reduce_fusion.1
  7.3 0.7 iota_compare_fusion.1
  8.1 0.8 select_reduce_fusion
  9.0 0.1 lt.39
  9.0 0.1 lt.41
  9.1 0.1 and.61
  9.3 0.3 and.62
  9.5 0.7 broadcast_compare_fusion
  10.2 0.1 copy.20
  10.3 0.7 iota_compare_fusion
  11.0 0.2 and.65
  11.2 0.2 and.66
  11.4 0.7 broadcast_multiply_fusion
  12.1 0.1 broadcast_reduce_fusion
  12.2 0.1 add.40
  12.2 0.1 add.42
  12.3 81.7 %all_gather.3 = bf16[64,4,1024]{2,1,0:T(4,128)(2,1)S(1)} all-gather(bf16[1,4,1024]{2,1,0:T(4,128)(2,1)} %param.14), channel_id=1, replica_groups=mesh['seq'=64,'tp'=8] {'seq'}, dimensions={0}, use_global_device_ids=true | all-gather | bytes 532480 | tf_op jit(solution)/shard_map/all_gather | solution.py:38
  94.0 0.2 reshape.221
  94.2 0.1 broadcast_and_fusion
  94.3 0.7 sub.14
  94.9 0.1 and_and_fusion
  95.0 0.1 compare_and_fusion
  95.2 0.1 broadcast_in_dim.30
  95.3 0.1 broadcast_in_dim.33
  95.4 0.1 pad_add_fusion
  95.4 0.0 copy-start.3
  95.4 0.0 copy-start.4
  95.4 0.0 copy-start.5
  95.5 5.5 fusion
  100.9 0.0 copy-start.1
  100.9 7.3 copy-done.1
  108.2 7.2 fusion.1
  115.5 222.0 %pmax.7 = f32[64,4,1,8]{0,3,1,2:T(8,128)S(1)} all-reduce(f32[64,4,1,8]{0,3,1,2:T(8,128)S(1)} %bitcast.79), channel_id=1, replica_groups=mesh['seq'=64,'tp'=8] {'seq'}, use_global_device_ids=true, to_apply=%region_2.3 | all-reduce | flops 2048 | bytes 16384 | tf_op jit(solution)/shard_map/pmax | solution.py:100
  337.4 0.0 copy-done.3
  337.5 0.0 copy-start.2
  337.5 10.4 %fusion.13 = f32[64,4,1,8,128]{4,0,3,1,2:T(8,128)} fusion(f32[2564,64,4,8]{0,1,3,2:T(8,128)} %copy-done.1, f32[64,4,8]{0,2,1:T(8,128)S(1)} %get-tuple-element.7, pred[64,4,2564]{2,0,1:T(8,128)(4,1)S(1)} %pad_add_fusion, bf16[4,1,128]{2,0,1:T(4,128)(2,1)S(1)} %bitcast.85, bf16[1024,1,128]{2,0,1:T(8,128)(2,1)S(1)} %bitcast.83, ...), kind=kOutput, calls=%fused_computation.11 | convolution fusion | flops 1372761088 | bytes 23382016 | tf_op jit(solution)/shard_map/rjkhn,nkd->rjkhd/dot_general | solution.py:96
  347.8 0.0 all-reduce.2.cloned.1.call-update
  347.9 0.0 reduce-scatter.2.cloned.1.call-start
  347.9 0.0 copy-done.2
  347.9 219.7 %psum.15 = f32[64,4,8]{0,2,1:T(8,128)S(1)} all-reduce(f32[64,4,8]{0,2,1:T(8,128)S(1)} %get-tuple-element.5), channel_id=1, replica_groups=mesh['seq'=64,'tp'=8] {'seq'}, use_global_device_ids=true, to_apply=%region_5.6 | all-reduce | flops 2048 | bytes 16384 | tf_op jit(solution)/shard_map/psum | solution.py:102
  567.6 116.0 %all-reduce.2.cloned.1.call-done = f32[64,4,1,8,128]{4,0,3,1,2:T(8,128)} async-done(((f32[64,4,1,8,128]{4,0,3,1,2:T(8,128)}), f32[64,4,1,8,128]{4,0,3,1,2:T(8,128)}) %all-reduce.2.cloned.1.call-update) | async-done | bytes 1048592 | tf_op jit(solution)/shard_map/psum | solution.py:102
  683.6 1.6 multiply_convert_fusion
  685.3 0.3 copy.23
  685.6 0.9 convolution_convert_fusion
  686.5 0.0 reduce-scatter.2.cloned.1.call-update
  686.6 44.8 %reduce-scatter.2.cloned.1.call-done = bf16[32,128]{1,0:T(8,128)(2,1)} async-done(((bf16[256,128]{1,0:T(8,128)(2,1)}), bf16[32,128]{1,0:T(8,128)(2,1)}) %reduce-scatter.2.cloned.1.call-update) | async-done | bytes 8208 | tf_op jit(solution)/shard_map/reduce_scatter | solution.py:107
  (12 shorter events, 0.1 us)
Async XLA Ops:
  6.5 679.1 %copy-start = (bf16[1024,128]{1,0:T(8,128)(2,1)S(1)}, bf16[1024,128]{1,0:T(8,128)(2,1)}, u32[]{:S(2)}) copy-start(bf16[1024,128]{1,0:T(8,128)(2,1)} %param.21) | copy-start | bytes 786436
  6.5 677.1 %all-reduce.2.cloned.1.call-start = ((), (), s32[]{:S(2)}) async-start(), calls=%async_computation.1 | async-start | bytes 2097152 | tf_op jit(solution)/shard_map/psum | solution.py:102
  95.4 242.0 %copy-start.3 = (bf16[8,192,128]{2,1,0:T(8,128)(2,1)S(1)}, bf16[8,192,128]{2,1,0:T(8,128)(2,1)}, u32[]{:S(2)}) copy-start(bf16[8,192,128]{2,1,0:T(8,128)(2,1)} %param.18) | copy-start | bytes 1179652
  95.4 242.0 %copy-start.4 = (bf16[16,64,128]{2,1,0:T(8,128)(2,1)S(1)}, bf16[16,64,128]{2,1,0:T(8,128)(2,1)}, u32[]{:S(2)}) copy-start(bf16[16,64,128]{2,1,0:T(8,128)(2,1)} %param.20) | copy-start | bytes 786436
  95.4 242.0 %copy-start.5 = (bf16[1,4,128]{2,1,0:T(4,128)(2,1)S(1)}, bf16[1,4,128]{2,1,0:T(4,128)(2,1)}, u32[]{:S(2)}) copy-start(bf16[1,4,128]{2,1,0:T(4,128)(2,1)} %param.16) | copy-start | bytes 3076
  100.9 7.3 copy-start.1
  337.5 10.5 %copy-start.2 = (s32[64,4]{0,1:T(4,128)S(1)}, s32[64,4]{0,1:T(4,128)}, u32[]{:S(2)}) copy-start(s32[64,4]{0,1:T(4,128)} %param.27) | copy-start | bytes 3076
  347.9 383.5 %reduce-scatter.2.cloned.1.call-start = ((), (), s32[]{:S(2)}) async-start(), calls=%async_computation.2 | async-start | bytes 73728 | tf_op jit(solution)/shard_map/reduce_scatter | solution.py:107
Sparse Core Ops, SparseCore 0:
  348.0 335.6 all-reduce.1
  686.7 44.6 reduce-scatter.1

commit v2 on v1

--- a/solution.py
+++ b/solution.py
@@ -1,7 +1,7 @@
 import jax
 import jax.numpy as jnp
 from jax import lax
-from jax.sharding import PartitionSpec as P
+from jax.sharding import Mesh, PartitionSpec as P
 
 HEAD_DIM = 128
 HPK = 8
@@ -10,6 +10,19 @@
 
 
 NEG = -1e30
+SEQ = ("sx", "sz")
+
+
+def gather_rows(block):
+    block = lax.all_gather(block, "sz", axis=0, tiled=True)
+    return lax.all_gather(block, "sx", axis=0, tiled=True)
+
+
+def inner_size(devices):
+    try:
+        return len({d.coords[2] for d in devices})
+    except Exception:
+        return 1
 
 
 def local(
@@ -29,13 +42,13 @@
     new_valid,
 ):
     req_dev = queries.shape[0]
-    seq_count = lax.axis_size("seq")
+    seq_count = lax.axis_size(SEQ)
     requests = req_dev * seq_count
     kv_local = new_keys.shape[2] // HEAD_DIM
     heads_local = kv_local * HPK
     score_scale = HEAD_DIM ** (-0.5)
-    seq_idx = lax.axis_index("seq")
-    gathered = lax.all_gather(queries, "seq", axis=0, tiled=True)
+    seq_idx = lax.axis_index(SEQ)
+    gathered = gather_rows(queries)
     query_all = gathered.reshape(requests, NEW, kv_local, HPK, HEAD_DIM)
 
     group_hot = group_of[:, None] == jnp.arange(GROUPS, dtype=jnp.int32)[None, :]
@@ -97,34 +110,57 @@
         "rjkhn,nkd->rjkhd", weights.astype(jnp.bfloat16), values, preferred_element_type=jnp.float32
     )
 
-    top_peak = lax.pmax(row_peak, "seq")
-    factor = jnp.exp(row_peak - top_peak)
-    final_total, final_out = lax.psum((row_total * factor, out * factor[..., None]), "seq")
-    valid_rows = new_valid.astype(jnp.float32)[:, :, None, None, None]
+    flat_out = out.reshape(requests, -1)
+    stats = jnp.concatenate(
+        [row_peak.reshape(requests, -1), row_total.reshape(requests, -1)], axis=1
+    )
+    packed = jnp.concatenate([flat_out, stats], axis=1)
+    received = lax.all_to_all(packed, SEQ, 0, 0, tiled=True)
+    received = received.reshape(seq_count, req_dev, -1)
+    n_out = flat_out.shape[1]
+    n_stat = row_peak.size // requests
+    shape_rows = (seq_count, req_dev, NEW, kv_local, HPK)
+    part_out = received[:, :, :n_out].reshape(shape_rows + (HEAD_DIM,))
+    part_peak = received[:, :, n_out : n_out + n_stat].reshape(shape_rows)
+    part_total = received[:, :, n_out + n_stat :].reshape(shape_rows)
+    top_peak = jnp.max(part_peak, axis=0)
+    factor = jnp.exp(part_peak - top_peak[None])
+    final_total = jnp.sum(part_total * factor, axis=0)
+    final_out = jnp.sum(part_out * factor[..., None], axis=0)
+    row_start = seq_idx * req_dev
+    valid_local = lax.dynamic_slice_in_dim(new_valid, row_start, req_dev, 0)
+    valid_rows = valid_local.astype(jnp.float32)[:, :, None, None, None]
     attention = (final_out / final_total[..., None] * valid_rows).astype(jnp.bfloat16)
-    attention = attention.reshape(requests * NEW, heads_local * HEAD_DIM)
+    attention = attention.reshape(req_dev * NEW, heads_local * HEAD_DIM)
+    attention = gather_rows(attention)
     terms = jnp.dot(attention, out_weight, preferred_element_type=jnp.float32)
     summed = lax.psum_scatter(terms.astype(jnp.bfloat16), "tp", scatter_dimension=0, tiled=True)
     return summed
 
 
 def solution(mesh):
+    grid = mesh.devices
+    n_seq, n_tp = grid.shape
+    inner = inner_size(list(grid[:, 0]))
+    if inner < 1 or n_seq % inner:
+        inner = 1
+    mesh = Mesh(grid.reshape(n_seq // inner, inner, n_tp), ("sx", "sz", "tp"))
     placed = (
-        P("seq", None, "tp"),
-        P("seq", None, "tp"),
-        P("seq", None, "tp"),
-        P(None, "seq", "tp"),
-        P(None, "seq", "tp"),
-        P("seq", None, "tp"),
-        P("seq", None, "tp"),
-        P("tp", "seq"),
+        P(SEQ, None, "tp"),
+        P(SEQ, None, "tp"),
+        P(SEQ, None, "tp"),
+        P(None, SEQ, "tp"),
+        P(None, SEQ, "tp"),
+        P(SEQ, None, "tp"),
+        P(SEQ, None, "tp"),
+        P("tp", SEQ),
         P(),
         P(),
         P(),
-        P("seq"),
-        P("seq"),
+        P(SEQ),
+        P(SEQ),
         P(),
     )
     return jax.shard_map(
-        local, mesh=mesh, in_specs=placed, out_specs=P("tp", "seq"), check_vma=False
+        local, mesh=mesh, in_specs=placed, out_specs=P("tp", SEQ), check_vma=False
     )

time: 739 us -> 235 us (0.32)
  blocking collectives: 523 us -> 72.9 us
  waiting for transfers between devices: 161 us -> 94.3 us
  starting transfers between devices: 0.04 us -> 9.48 us
    pmax x1 -> x0, blocking collectives: 222 us -> none  [local(): top_peak = lax.pmax(row_peak, 'seq')]
    psum x1 -> x0, blocking collectives: 220 us -> none  [local(): lax.psum((row_total * factor, out * factor[..., None]), 'seq')]
    psum x1 -> x0, waiting for transfers between devices: 116 us -> none  [local(): lax.psum((row_total * factor, out * factor[..., None]), 'seq')]
    all_to_all x0 -> x1, waiting for transfers between devices: none -> 43.8 us  [local(): received = lax.all_to_all(packed, SEQ, 0, 0, tiled=True)]
    all_to_all x0 -> x1, starting transfers between devices: none -> 9.44 us  [local(): received = lax.all_to_all(packed, SEQ, 0, 0, tiled=True)]
    all_gather x1 -> x4, blocking collectives: 81.7 us -> 72.9 us  [the longest x2 52.8 us: gather_rows(): block = lax.all_gather(block, 'sz', axis=0, tiled=True)]
where the time goes in v2:
time: 235 us; the launch traced here: 234 us
  waiting for transfers between devices  94.3 us (40%)
  blocking collectives  72.9 us (31%)
  matrix products  15.9 us (7%)
  local copies, waits for them, and re-layouts  14 us (6%)
  other arithmetic  13.7 us (6%)
  between operations  13.7 us (6%)
  starting transfers between devices  9.48 us (4%)
    all_gather x2, blocking collectives, gather_rows(): block = lax.all_gather(block, 'sz', axis=0, tiled=True)  52.8 us
    reduce_scatter x1, waiting for transfers between devices, local(): lax.psum_scatter(terms.astype(jnp.bfloat16), 'tp', scatter_dimension=0, t...  50.4 us
    all_to_all x1, waiting for transfers between devices, local(): received = lax.all_to_all(packed, SEQ, 0, 0, tiled=True)  43.8 us
    all_gather x2, blocking collectives, gather_rows(): return lax.all_gather(block, 'sx', axis=0, tiled=True)  20.2 us
    dot_general x1, matrix products, local(): jnp.einsum('rjkhn,nkd->rjkhd', weights.astype(jnp.bfloat16), values, pref...  9.51 us
    all_to_all x1, starting transfers between devices, local(): received = lax.all_to_all(packed, SEQ, 0, 0, tiled=True)  9.44 us
    unnamed x16, local copies, waits for them, and re-layouts  7.58 us
    reduce_sum x1, other arithmetic, local(): row_total = jnp.sum(weights, axis=-1)  7.21 us
  transfers between devices with their start and end apart: 2, of which 2 were waited for; matrix products, arithmetic and copies ran while one was open for 0% of the time, Pallas kernels for 0%

profile of v2, /device:TPU:1, one launch (start us, length us, event | category | flops | bytes accessed | tf_op | source)
XLA Modules:
  0.0 233.9 jit_solution(11599162332830723495)
XLA Ops:
  6.5 0.8 iota_compare_fusion.1
  7.3 0.8 select_reduce_fusion
  8.2 0.8 broadcast_reduce_fusion.1
  9.0 0.7 broadcast_multiply_fusion
  9.6 0.7 broadcast_compare_fusion
  10.3 0.1 lt.42
  10.4 0.1 copy.33
  10.5 0.1 broadcast_reduce_fusion
  10.7 0.7 iota_compare_fusion
  11.3 0.1 lt.44
  11.5 0.1 and.62
  11.6 0.3 and.63
  11.9 0.2 and.66
  12.1 0.2 and.67
  12.3 30.1 %all_gather.12 = bf16[16,4,1024]{2,1,0:T(4,128)(2,1)S(1)} all-gather(bf16[1,4,1024]{2,1,0:T(4,128)(2,1)} %param.14), channel_id=1, replica_groups=mesh['sx'=4,'sz'=16,'tp'=8] {'sz'}, dimensions={0}, use_global_device_ids=true | all-gather | bytes 139264 | tf_op jit(solution)/shard_map/all_gather | solution.py:17
  42.4 10.2 %all_gather.13 = bf16[64,4,1024]{2,1,0:T(4,128)(2,1)S(1)} all-gather(bf16[16,4,1024]{2,1,0:T(4,128)(2,1)S(1)} %all_gather.12), channel_id=1, replica_groups=mesh['sx'=4,'sz'=16,'tp'=8] {'sx'}, dimensions={0}, use_global_device_ids=true | all-gather | bytes 655360 | tf_op jit(solution)/shard_map/all_gather | solution.py:18
  52.6 0.2 reshape.287
  52.8 0.7 sub.33
  53.6 0.1 and_and_fusion
  53.7 0.1 compare_and_fusion
  53.9 0.1 broadcast_in_dim.30
  54.1 5.5 %fusion = (f32[64,4,8]{0,2,1:T(8,128)S(1)}, f32[2564,64,4,8]{0,1,3,2:T(8,128)S(1)}) fusion(pred[64,4,2564]{2,0,1:T(8,128)(4,1)S(1)} %pad_add_fusion, bf16[64,4,8,128]{3,2,1,0:T(8,128)(2,1)S(1)} %reshape.287, bf16[4,1,128]{2,0,1:T(4,128)(2,1)} %bitcast.80, bf16[1024,1,128]{2,0,1:T(8,128)(2,1)} %bitcast.78, bf16[1536,1,128]{2,0,1:T(8,128)(2,1)} %bitcast.76), kind=kOutput, calls=%fused_computation.2 | convolution fusion | flops 1361994752 | bytes 22849536 | tf_op jit(solution)/shard_map/rjkhd,nkd->rjkhn/dot_general | solution.py:102
  59.6 7.3 %copy-done.1 = f32[2564,64,4,8]{0,1,3,2:T(8,128)} copy-done((f32[2564,64,4,8]{0,1,3,2:T(8,128)}, f32[2564,64,4,8]{0,1,3,2:T(8,128)S(1)}, u32[]{:S(2)}) %copy-start.1) | copy-done | bytes 21004312
  66.9 7.2 %fusion.1 = f32[64,4,8]{0,2,1:T(8,128)S(1)} fusion(f32[2564,64,4,8]{0,1,3,2:T(8,128)S(1)} %get-tuple-element.9, f32[64,4,8]{0,2,1:T(8,128)S(1)} %get-tuple-element.8, pred[64,4,2564]{2,0,1:T(8,128)(4,1)S(1)} %pad_add_fusion), kind=kLoop, calls=%fused_computation.3 | loop fusion | flops 26253312 | bytes 21677056 | tf_op jit(solution)/shard_map/reduce_sum | solution.py:108
  74.1 9.5 %fusion.7 = f32[64,4,1,8,128]{4,0,3,1,2:T(8,128)S(1)} fusion(f32[2564,64,4,8]{0,1,3,2:T(8,128)} %copy-done.1, f32[64,4,8]{0,2,1:T(8,128)S(1)} %get-tuple-element.8, pred[64,4,2564]{2,0,1:T(8,128)(4,1)S(1)} %pad_add_fusion, bf16[4,1,128]{2,0,1:T(4,128)(2,1)S(1)} %bitcast.81, bf16[1024,1,128]{2,0,1:T(8,128)(2,1)S(1)} %bitcast.79, ...), kind=kOutput, calls=%fused_computation.9 | convolution fusion | flops 1372498944 | bytes 23373824 | tf_op jit(solution)/shard_map/rjkhn,nkd->rjkhd/dot_general | solution.py:109
  83.6 0.6 copy.36
  84.3 0.2 reshape.279
  84.5 0.1 copy.38
  84.5 0.1 copy.37
  84.6 0.2 concatenate.15
  84.9 2.1 copy.39
  87.0 9.4 %all-to-all-start = ((f32[64,1,4160]{2,1,0:T(1,128)}), f32[64,1,4160]{2,1,0:T(1,128)S(1)}, u32[]{:S(2)}, u32[]{:S(2)}) async-start(f32[64,1,4160]{2,1,0:T(1,128)} %copy.39), calls=%async_computation | async-start | bytes 2162688 | tf_op jit(solution)/shard_map/all_to_all | solution.py:118
  96.5 0.2 convert_reduce_fusion
  96.7 43.8 %all-to-all-done = f32[64,1,4160]{2,1,0:T(1,128)S(1)} async-done(((f32[64,1,4160]{2,1,0:T(1,128)}), f32[64,1,4160]{2,1,0:T(1,128)S(1)}, u32[]{:S(2)}, u32[]{:S(2)}) %all-to-all-start) | async-done | bytes 1064992 | tf_op jit(solution)/shard_map/all_to_all | solution.py:118
  140.5 0.1 fusion.28
  140.7 0.1 sub.36
  140.8 0.2 multiply_reduce_fusion
  141.0 0.1 fusion.21
  141.1 0.1 div.15
  141.2 0.1 broadcast_bitcast_fusion
  141.3 0.1 copy.41
  141.4 0.3 mul.61
  141.7 1.1 fusion.10
  142.9 0.1 fusion.22
  143.0 22.7 %all-gather = bf16[16,4,1024]{2,1,0:T(4,128)(2,1)S(1)} all-gather(bf16[1,4,1024]{2,1,0:T(4,128)(2,1)S(1)} %fusion.22), channel_id=1, replica_groups=mesh['sx'=4,'sz'=16,'tp'=8] {'sz'}, dimensions={0}, use_global_device_ids=true | all-gather | bytes 139264 | tf_op jit(solution)/shard_map/all_gather | solution.py:17
  165.7 9.9 %all_gather.15 = bf16[256,1024]{1,0:T(8,128)(2,1)S(1)} all-gather(bf16[64,1024]{1,0:T(8,128)(2,1)S(1)} %reshape.284), channel_id=1, replica_groups=mesh['sx'=4,'sz'=16,'tp'=8] {'sx'}, dimensions={0}, use_global_device_ids=true | all-gather | bytes 655360 | tf_op jit(solution)/shard_map/all_gather | solution.py:18
  175.6 0.9 convolution_convert_fusion
  176.6 50.4 %reduce-scatter.2.cloned.1.call-done = bf16[32,128]{1,0:T(8,128)(2,1)} async-done(((bf16[256,128]{1,0:T(8,128)(2,1)}), bf16[32,128]{1,0:T(8,128)(2,1)}) %reduce-scatter.2.cloned.1.call-update) | async-done | bytes 8208 | tf_op jit(solution)/shard_map/reduce_scatter | solution.py:137
  (29 shorter events, 0.6 us)
Async XLA Ops:
  6.5 169.1 %copy-start = (bf16[1024,128]{1,0:T(8,128)(2,1)S(1)}, bf16[1024,128]{1,0:T(8,128)(2,1)}, u32[]{:S(2)}) copy-start(bf16[1024,128]{1,0:T(8,128)(2,1)} %param.21) | copy-start | bytes 786436
  54.0 20.1 %copy-start.3 = (bf16[8,192,128]{2,1,0:T(8,128)(2,1)S(1)}, bf16[8,192,128]{2,1,0:T(8,128)(2,1)}, u32[]{:S(2)}) copy-start(bf16[8,192,128]{2,1,0:T(8,128)(2,1)} %param.18) | copy-start | bytes 1179652
  54.0 20.0 %copy-start.4 = (bf16[16,64,128]{2,1,0:T(8,128)(2,1)S(1)}, bf16[16,64,128]{2,1,0:T(8,128)(2,1)}, u32[]{:S(2)}) copy-start(bf16[16,64,128]{2,1,0:T(8,128)(2,1)} %param.20) | copy-start | bytes 786436
  54.1 20.0 %copy-start.5 = (bf16[1,4,128]{2,1,0:T(4,128)(2,1)S(1)}, bf16[1,4,128]{2,1,0:T(4,128)(2,1)}, u32[]{:S(2)}) copy-start(bf16[1,4,128]{2,1,0:T(4,128)(2,1)} %param.16) | copy-start | bytes 3076
  59.5 7.3 %copy-start.1 = (f32[2564,64,4,8]{0,1,3,2:T(8,128)}, f32[2564,64,4,8]{0,1,3,2:T(8,128)S(1)}, u32[]{:S(2)}) copy-start(f32[2564,64,4,8]{0,1,3,2:T(8,128)S(1)} %get-tuple-element.9) | copy-start | bytes 63012868
  74.1 22.4 %copy-start.2 = (s32[64,4]{0,1:T(4,128)S(1)}, s32[64,4]{0,1:T(4,128)}, u32[]{:S(2)}) copy-start(s32[64,4]{0,1:T(4,128)} %param.27) | copy-start | bytes 3076
  87.0 53.5 %all-to-all-start = ((f32[64,1,4160]{2,1,0:T(1,128)}), f32[64,1,4160]{2,1,0:T(1,128)S(1)}, u32[]{:S(2)}, u32[]{:S(2)}) async-start(f32[64,1,4160]{2,1,0:T(1,128)} %copy.39), calls=%async_computation | async-start | bytes 2162688 | tf_op jit(solution)/shard_map/all_to_all | solution.py:118
  96.4 130.6 %reduce-scatter.2.cloned.1.call-start = ((), (), s32[]{:S(2)}) async-start(), calls=%async_computation.2 | async-start | bytes 73728 | tf_op jit(solution)/shard_map/reduce_scatter | solution.py:137
Sparse Core Ops, SparseCore 0:
  176.7 50.2 reduce-scatter.1

commit v3 on v2

--- a/solution.py
+++ b/solution.py
@@ -9,13 +9,30 @@
 NEW = 4
 
 
-NEG = -1e30
+NEG = -(2.0**100)
 SEQ = ("sx", "sz")
 
 
 def gather_rows(block):
-    block = lax.all_gather(block, "sz", axis=0, tiled=True)
+    inner = lax.axis_size("sz")
+    copies = jnp.broadcast_to(block[None], (inner,) + block.shape)
+    block = lax.all_to_all(copies, "sz", 0, 0, tiled=True)
+    block = block.reshape((inner * block.shape[1],) + block.shape[2:])
     return lax.all_gather(block, "sx", axis=0, tiled=True)
+
+
+def merge(parts, n_out, n_stat):
+    part_out = parts[..., :n_out]
+    part_peak = parts[..., n_out : n_out + n_stat]
+    part_total = parts[..., n_out + n_stat :]
+    top_peak = jnp.max(part_peak, axis=0)
+    factor = jnp.exp(part_peak - top_peak[None])
+    total = jnp.sum(part_total * factor, axis=0)
+    lead = factor.shape[:-1]
+    rows = factor.reshape(lead + (n_stat, 1))
+    out = parts[..., :n_out].reshape(lead + (n_stat, n_out // n_stat)) * rows
+    out = jnp.sum(out, axis=0).reshape(out.shape[1:-2] + (n_out,))
+    return out, top_peak, total
 
 
 def inner_size(devices):
@@ -111,22 +128,25 @@
     )
 
     flat_out = out.reshape(requests, -1)
-    stats = jnp.concatenate(
-        [row_peak.reshape(requests, -1), row_total.reshape(requests, -1)], axis=1
-    )
-    packed = jnp.concatenate([flat_out, stats], axis=1)
-    received = lax.all_to_all(packed, SEQ, 0, 0, tiled=True)
-    received = received.reshape(seq_count, req_dev, -1)
+    peak = row_peak.reshape(requests, -1)
+    near_peak = peak.astype(jnp.bfloat16).astype(jnp.float32)
+    shift = jnp.exp(peak - near_peak)
+    n_stat = peak.shape[1]
     n_out = flat_out.shape[1]
-    n_stat = row_peak.size // requests
-    shape_rows = (seq_count, req_dev, NEW, kv_local, HPK)
-    part_out = received[:, :, :n_out].reshape(shape_rows + (HEAD_DIM,))
-    part_peak = received[:, :, n_out : n_out + n_stat].reshape(shape_rows)
-    part_total = received[:, :, n_out + n_stat :].reshape(shape_rows)
-    top_peak = jnp.max(part_peak, axis=0)
-    factor = jnp.exp(part_peak - top_peak[None])
-    final_total = jnp.sum(part_total * factor, axis=0)
-    final_out = jnp.sum(part_out * factor[..., None], axis=0)
+    flat_out = (flat_out.reshape(requests, n_stat, -1) * shift[..., None]).reshape(requests, n_out)
+    total = row_total.reshape(requests, -1) * shift
+    packed = jnp.concatenate([flat_out, near_peak, total], axis=1).astype(jnp.bfloat16)
+    outer = lax.axis_size("sx")
+    inner = lax.axis_size("sz")
+    width = packed.shape[1]
+    packed = packed.reshape(outer, inner, req_dev, width).transpose(1, 0, 2, 3)
+    received = lax.all_to_all(packed, "sz", 0, 0, tiled=True).astype(jnp.float32)
+    stage_out, stage_peak, stage_total = merge(received, n_out, n_stat)
+    packed = jnp.concatenate([stage_out, stage_peak, stage_total], axis=-1)
+    received = lax.all_to_all(packed, "sx", 0, 0, tiled=True)
+    final_out, _, final_total = merge(received, n_out, n_stat)
+    final_out = final_out.reshape(req_dev, NEW, kv_local, HPK, HEAD_DIM)
+    final_total = final_total.reshape(req_dev, NEW, kv_local, HPK)
     row_start = seq_idx * req_dev
     valid_local = lax.dynamic_slice_in_dim(new_valid, row_start, req_dev, 0)
     valid_rows = valid_local.astype(jnp.float32)[:, :, None, None, None]
@@ -134,8 +154,10 @@
     attention = attention.reshape(req_dev * NEW, heads_local * HEAD_DIM)
     attention = gather_rows(attention)
     terms = jnp.dot(attention, out_weight, preferred_element_type=jnp.float32)
-    summed = lax.psum_scatter(terms.astype(jnp.bfloat16), "tp", scatter_dimension=0, tiled=True)
-    return summed
+    n_tp = lax.axis_size("tp")
+    blocks = lax.all_to_all(terms, "tp", 0, 0, tiled=True)
+    blocks = blocks.reshape((n_tp, blocks.shape[0] // n_tp) + blocks.shape[1:])
+    return jnp.sum(blocks, axis=0).astype(jnp.bfloat16)
 
 
 def solution(mesh):

time: 235 us -> 167 us (0.71)
  waiting for transfers between devices: 94.3 us -> 9.28 us
  blocking collectives: 72.9 us -> 92.3 us
  between operations: 13.7 us -> 0.35 us
  starting transfers between devices: 9.48 us -> 19 us
  local copies, waits for them, and re-layouts: 14 us -> 7.9 us
  matrix products: 15.9 us -> 20.3 us
  other arithmetic: 13.7 us -> 17.5 us
    all_to_all x0 -> x3, blocking collectives: none -> 71.7 us  [the longest x1 37.3 us: local(): lax.all_to_all(packed, 'sz', 0, 0, tiled=True).astype(jnp.float32)]
    all_gather x2 -> x0, blocking collectives: 52.8 us -> none  [gather_rows(): block = lax.all_gather(block, 'sz', axis=0, tiled=True)]
    reduce_scatter x1 -> x0, waiting for transfers between devices: 50.4 us -> none  [local(): lax.psum_scatter(terms.astype(jnp.bfloat16), 'tp', scatter_dimension=0, t...]
    all_to_all x1 -> x2, waiting for transfers between devices: 43.8 us -> 9.28 us  [the longest x1 5.03 us: gather_rows(): block = lax.all_to_all(copies, 'sz', 0, 0, tiled=True)]
    all_to_all x1 -> x2, starting transfers between devices: 9.44 us -> 19 us  [the longest x1 15.7 us: gather_rows(): block = lax.all_to_all(copies, 'sz', 0, 0, tiled=True)]
    unnamed x16 -> x11, local copies, waits for them, and re-layouts: 7.58 us -> 0.1 us
    dot_general x1, matrix products: 5.47 us -> 10.5 us  [local(): jnp.einsum('rjkhd,nkd->rjkhn', query_all, keys, preferred_element_type=jn...]
    reduce_sum x1, other arithmetic: 7.21 us -> 11.2 us  [local(): row_total = jnp.sum(weights, axis=-1)]
  transfers between devices with their start and end apart: 2 -> 2, of which waited for: 2 -> 2; matrix products, arithmetic and copies ran while one was open for 0% -> 4% of each run, Pallas kernels for 0% -> 0%
where the time goes in v3:
time: 167 us
  blocking collectives  92.3 us (55%)
  matrix products  20.3 us (12%)
  starting transfers between devices  19 us (11%)
  other arithmetic  17.5 us (10%)
  waiting for transfers between devices  9.28 us (6%)
  local copies, waits for them, and re-layouts  7.9 us (5%)
    all_to_all x1, blocking collectives, local(): lax.all_to_all(packed, 'sz', 0, 0, tiled=True).astype(jnp.float32)  37.3 us
    all_gather x2, blocking collectives, gather_rows(): return lax.all_gather(block, 'sx', axis=0, tiled=True)  20.6 us
    all_to_all x1, blocking collectives, gather_rows(): block = lax.all_to_all(copies, 'sz', 0, 0, tiled=True)  17.8 us
    all_to_all x1, blocking collectives, local(): blocks = lax.all_to_all(terms, 'tp', 0, 0, tiled=True)  16.6 us
    all_to_all x1, starting transfers between devices, gather_rows(): block = lax.all_to_all(copies, 'sz', 0, 0, tiled=True)  15.7 us
    reduce_sum x1, other arithmetic, local(): row_total = jnp.sum(weights, axis=-1)  11.2 us
    dot_general x1, matrix products, local(): jnp.einsum('rjkhd,nkd->rjkhn', query_all, keys, preferred_element_type=jn...  10.5 us
    dot_general x1, matrix products, local(): jnp.einsum('rjkhn,nkd->rjkhd', weights.astype(jnp.bfloat16), values, pref...  9.54 us
  transfers between devices with their start and end apart: 2, of which 2 were waited for; matrix products, arithmetic and copies ran while one was open for 4% of the time, Pallas kernels for 0%

profile of v3, /device:TPU:1, one launch (start us, length us, event | category | flops | bytes accessed | tf_op | source)
XLA Modules:
  0.0 166.7 jit_solution(6012672266476342557)
XLA Ops:
  0.0 1.4 broadcast_in_dim.46
  1.4 15.7 %all-to-all-start = ((bf16[16,1,4,1024]{3,2,1,0:T(4,128)(2,1)}), bf16[16,1,4,1024]{3,2,1,0:T(4,128)(2,1)S(1)}, u32[]{:S(2)}, u32[]{:S(2)}) async-start(bf16[16,1,4,1024]{3,2,1,0:T(4,128)(2,1)} %broadcast_in_dim.46), calls=%async_computation | async-start | bytes 262144 | tf_op jit(solution)/shard_map/all_to_all | solution.py:19
  17.2 0.7 iota_compare_fusion.1
  17.9 0.8 select_reduce_fusion
  18.8 0.8 broadcast_reduce_fusion.1
  19.5 0.7 broadcast_multiply_fusion
  20.2 0.7 broadcast_compare_fusion
  21.0 0.1 copy.37
  21.1 0.1 broadcast_reduce_fusion
  21.3 0.7 iota_compare_fusion
  22.1 0.1 and.62
  22.2 0.3 and.63
  22.5 0.2 and.66
  22.7 0.2 and.67
  22.9 0.7 sub.42
  23.6 0.1 compare_and_fusion
  23.9 0.1 broadcast_in_dim.36
  24.1 5.0 %all-to-all-done = bf16[16,1,4,1024]{3,2,1,0:T(4,128)(2,1)S(1)} async-done(((bf16[16,1,4,1024]{3,2,1,0:T(4,128)(2,1)}), bf16[16,1,4,1024]{3,2,1,0:T(4,128)(2,1)S(1)}, u32[]{:S(2)}, u32[]{:S(2)}) %all-to-all-start) | async-done | bytes 131104 | tf_op jit(solution)/shard_map/all_to_all | solution.py:19
  29.1 10.2 %all-gather = bf16[64,1,4,1024]{3,2,1,0:T(4,128)(2,1)S(1)} all-gather(bf16[16,1,4,1024]{3,2,1,0:T(4,128)(2,1)S(1)} %all-to-all-done), channel_id=2, replica_groups=mesh['sx'=4,'sz'=16,'tp'=8] {'sx'}, dimensions={0}, use_global_device_ids=true | all-gather | bytes 655360 | tf_op jit(solution)/shard_map/all_gather | solution.py:21
  39.4 0.2 reshape.388
  39.6 10.5 %fusion = (f32[64,4,8]{0,2,1:T(8,128)S(1)}, f32[2564,64,4,8]{0,1,3,2:T(8,128)}) fusion(pred[64,4,2564]{2,0,1:T(8,128)(4,1)S(1)} %pad_add_fusion, bf16[64,4,8,128]{3,2,1,0:T(8,128)(2,1)S(1)} %reshape.388, bf16[4,1,128]{2,0,1:T(4,128)(2,1)} %bitcast.103, bf16[1024,1,128]{2,0,1:T(8,128)(2,1)} %bitcast.101, bf16[1536,1,128]{2,0,1:T(8,128)(2,1)} %bitcast.99), kind=kOutput, calls=%fused_computation.2 | convolution fusion | flops 1361994752 | bytes 22849536 | tf_op jit(solution)/shard_map/rjkhd,nkd->rjkhn/dot_general | solution.py:119
  50.1 0.1 reshape.380
  50.2 11.2 %fusion.1 = f32[64,4,8]{0,2,1:T(8,128)S(1)} fusion(f32[2564,64,4,8]{0,1,3,2:T(8,128)} %get-tuple-element.12, f32[64,4,8]{0,2,1:T(8,128)S(1)} %get-tuple-element.11, pred[64,4,2564]{2,0,1:T(8,128)(4,1)S(1)} %pad_add_fusion), kind=kLoop, calls=%fused_computation.3 | loop fusion | flops 26253312 | bytes 21677056 | tf_op jit(solution)/shard_map/reduce_sum | solution.py:125
  61.5 9.5 %fusion.7 = f32[64,4,1,8,128]{4,0,3,1,2:T(8,128)S(1)} fusion(f32[2564,64,4,8]{0,1,3,2:T(8,128)} %get-tuple-element.12, f32[64,4,8]{0,2,1:T(8,128)S(1)} %get-tuple-element.11, pred[64,4,2564]{2,0,1:T(8,128)(4,1)S(1)} %pad_add_fusion, bf16[4,1,128]{2,0,1:T(4,128)(2,1)S(1)} %bitcast.104, bf16[1024,1,128]{2,0,1:T(8,128)(2,1)S(1)} %bitcast.102, ...), kind=kOutput, calls=%fused_computation.9 | convolution fusion | flops 1372498944 | bytes 23373824 | tf_op jit(solution)/shard_map/rjkhn,nkd->rjkhd/dot_general | solution.py:126
  71.0 0.6 copy.40
  71.6 0.2 reshape_reshape.6
  72.0 0.1 reshape.381
  72.2 0.3 mul.107
  72.5 0.2 mul.108
  72.7 0.1 fusion.20
  72.8 0.2 concatenate.35
  73.1 0.2 copy.45
  73.3 37.3 %all_to_all.29 = bf16[16,4,1,4160]{3,1,2,0:T(4,128)(2,1)S(1)} all-to-all(bf16[16,4,1,4160]{3,1,2,0:T(4,128)(2,1)S(1)} %copy.45), channel_id=1, replica_groups=mesh['sx'=4,'sz'=16,'tp'=8] {'sz'}, dimensions={0} | all-to-all | bytes 1064960 | tf_op jit(solution)/shard_map/all_to_all | solution.py:143
  110.7 0.1 fusion.23
  110.8 0.3 mul.112
  111.1 0.4 mul.113
  111.5 0.3 fusion.10
  111.8 0.8 concatenate.36
  112.6 3.3 %all-to-all-start.2 = ((f32[4,1,4160]{2,1,0:T(1,128)}), f32[4,1,4160]{2,1,0:T(1,128)S(1)}, u32[]{:S(2)}, u32[]{:S(2)}) async-start(f32[4,1,4160]{2,1,0:T(1,128)} %concatenate.36), calls=%async_computation.2 | async-start | bytes 135168 | tf_op jit(solution)/shard_map/all_to_all | solution.py:146
  115.9 0.2 convert_reduce_fusion
  116.1 4.3 %all-to-all-done.2 = f32[4,1,4160]{2,1,0:T(1,128)S(1)} async-done(((f32[4,1,4160]{2,1,0:T(1,128)}), f32[4,1,4160]{2,1,0:T(1,128)S(1)}, u32[]{:S(2)}, u32[]{:S(2)}) %all-to-all-start.2) | async-done | bytes 66592 | tf_op jit(solution)/shard_map/all_to_all | solution.py:146
  120.4 0.1 fusion.27
  120.7 0.1 fusion.22
  120.9 17.8 %all_to_all.30 = bf16[16,4,1024]{2,1,0:T(4,128)(2,1)S(1)} all-to-all(bf16[16,4,1024]{2,1,0:T(4,128)(2,1)S(1)} %broadcast_in_dim.49), channel_id=1, replica_groups=mesh['sx'=4,'sz'=16,'tp'=8] {'sz'}, dimensions={0} | all-to-all | bytes 262144 | tf_op jit(solution)/shard_map/all_to_all | solution.py:19
  138.8 10.4 %all_gather.7 = bf16[256,1024]{1,0:T(8,128)(2,1)S(1)} all-gather(bf16[64,1024]{1,0:T(8,128)(2,1)S(1)} %reshape.383), channel_id=1, replica_groups=mesh['sx'=4,'sz'=16,'tp'=8] {'sx'}, dimensions={0}, use_global_device_ids=true | all-gather | bytes 655360 | tf_op jit(solution)/shard_map/all_gather | solution.py:21
  149.2 0.3 fusion.33
  149.5 16.6 %all_to_all.31 = f32[8,32,128]{2,1,0:T(8,128)S(1)} all-to-all(f32[8,32,128]{2,1,0:T(8,128)S(1)} %bitcast.93), channel_id=1, replica_groups=mesh['sx'=4,'sz'=16,'tp'=8] {'tp'}, dimensions={0} | all-to-all | bytes 262144 | tf_op jit(solution)/shard_map/all_to_all | solution.py:158
  166.1 0.6 reduce_sum.72
  (41 shorter events, 1.4 us)
Async XLA Ops:
  0.0 149.2 %copy-start = (bf16[1024,128]{1,0:T(8,128)(2,1)S(1)}, bf16[1024,128]{1,0:T(8,128)(2,1)}, u32[]{:S(2)}) copy-start(bf16[1024,128]{1,0:T(8,128)(2,1)} %param.21) | copy-start | bytes 786436
  1.4 27.7 %all-to-all-start = ((bf16[16,1,4,1024]{3,2,1,0:T(4,128)(2,1)}), bf16[16,1,4,1024]{3,2,1,0:T(4,128)(2,1)S(1)}, u32[]{:S(2)}, u32[]{:S(2)}) async-start(bf16[16,1,4,1024]{3,2,1,0:T(4,128)(2,1)} %broadcast_in_dim.46), calls=%async_computation | async-start | bytes 262144 | tf_op jit(solution)/shard_map/all_to_all | solution.py:19
  39.6 21.9 %copy-start.2 = (bf16[8,192,128]{2,1,0:T(8,128)(2,1)S(1)}, bf16[8,192,128]{2,1,0:T(8,128)(2,1)}, u32[]{:S(2)}) copy-start(bf16[8,192,128]{2,1,0:T(8,128)(2,1)} %param.18) | copy-start | bytes 1179652
  39.6 21.8 %copy-start.3 = (bf16[16,64,128]{2,1,0:T(8,128)(2,1)S(1)}, bf16[16,64,128]{2,1,0:T(8,128)(2,1)}, u32[]{:S(2)}) copy-start(bf16[16,64,128]{2,1,0:T(8,128)(2,1)} %param.20) | copy-start | bytes 786436
  39.6 21.8 %copy-start.4 = (bf16[1,4,128]{2,1,0:T(4,128)(2,1)S(1)}, bf16[1,4,128]{2,1,0:T(4,128)(2,1)}, u32[]{:S(2)}) copy-start(bf16[1,4,128]{2,1,0:T(4,128)(2,1)} %param.16) | copy-start | bytes 3076
  61.4 54.4 %copy-start.1 = (s32[64,4]{0,1:T(4,128)S(1)}, s32[64,4]{0,1:T(4,128)}, u32[]{:S(2)}) copy-start(s32[64,4]{0,1:T(4,128)} %param.27) | copy-start | bytes 3076
  112.6 7.7 %all-to-all-start.2 = ((f32[4,1,4160]{2,1,0:T(1,128)}), f32[4,1,4160]{2,1,0:T(1,128)S(1)}, u32[]{:S(2)}, u32[]{:S(2)}) async-start(f32[4,1,4160]{2,1,0:T(1,128)} %concatenate.36), calls=%async_computation.2 | async-start | bytes 135168 | tf_op jit(solution)/shard_map/all_to_all | solution.py:146

commit v4 on v3

--- a/solution.py
+++ b/solution.py
@@ -139,11 +139,11 @@
     outer = lax.axis_size("sx")
     inner = lax.axis_size("sz")
     width = packed.shape[1]
-    packed = packed.reshape(outer, inner, req_dev, width).transpose(1, 0, 2, 3)
-    received = lax.all_to_all(packed, "sz", 0, 0, tiled=True).astype(jnp.float32)
+    packed = packed.reshape(outer, inner, req_dev, width)
+    received = lax.all_to_all(packed, "sx", 0, 0, tiled=True).astype(jnp.float32)
     stage_out, stage_peak, stage_total = merge(received, n_out, n_stat)
     packed = jnp.concatenate([stage_out, stage_peak, stage_total], axis=-1)
-    received = lax.all_to_all(packed, "sx", 0, 0, tiled=True)
+    received = lax.all_to_all(packed, "sz", 0, 0, tiled=True)
     final_out, _, final_total = merge(received, n_out, n_stat)
     final_out = final_out.reshape(req_dev, NEW, kv_local, HPK, HEAD_DIM)
     final_total = final_total.reshape(req_dev, NEW, kv_local, HPK)

time: 167 us -> 157 us (0.940)
  blocking collectives: 92.3 us -> 69.1 us
  waiting for transfers between devices: 9.28 us -> 17.7 us
  starting transfers between devices: 19 us -> 22.6 us
    all_to_all x1, blocking collectives: 37.3 us -> 10.2 us  [local(): lax.all_to_all(packed, 'sx', 0, 0, tiled=True).astype(jnp.float32)]
    all_to_all x1, waiting for transfers between devices: 4.25 us -> 12.7 us  [local(): received = lax.all_to_all(packed, 'sz', 0, 0, tiled=True)]
    all_to_all x1, blocking collectives: 16.6 us -> 20.2 us  [local(): blocks = lax.all_to_all(terms, 'tp', 0, 0, tiled=True)]
    all_to_all x1, starting transfers between devices: 3.28 us -> 6.9 us  [local(): received = lax.all_to_all(packed, 'sz', 0, 0, tiled=True)]
where the time goes in v4:
time: 157 us; the launch traced here: 156 us
  blocking collectives  69.1 us (44%)
  starting transfers between devices  22.6 us (14%)
  matrix products  20.3 us (13%)
  waiting for transfers between devices  17.7 us (11%)
  other arithmetic  17.4 us (11%)
  local copies, waits for them, and re-layouts  8.8 us (6%)
    all_gather x2, blocking collectives, gather_rows(): return lax.all_gather(block, 'sx', axis=0, tiled=True)  20.7 us
    all_to_all x1, blocking collectives, local(): blocks = lax.all_to_all(terms, 'tp', 0, 0, tiled=True)  20.2 us
    all_to_all x1, blocking collectives, gather_rows(): block = lax.all_to_all(copies, 'sz', 0, 0, tiled=True)  18 us
    all_to_all x1, starting transfers between devices, gather_rows(): block = lax.all_to_all(copies, 'sz', 0, 0, tiled=True)  15.7 us
    all_to_all x1, waiting for transfers between devices, local(): received = lax.all_to_all(packed, 'sz', 0, 0, tiled=True)  12.7 us
    reduce_sum x1, other arithmetic, local(): row_total = jnp.sum(weights, axis=-1)  11.2 us
    dot_general x1, matrix products, local(): jnp.einsum('rjkhd,nkd->rjkhn', query_all, keys, preferred_element_type=jn...  10.5 us
    all_to_all x1, blocking collectives, local(): lax.all_to_all(packed, 'sx', 0, 0, tiled=True).astype(jnp.float32)  10.2 us
  transfers between devices with their start and end apart: 2, of which 2 were waited for; matrix products, arithmetic and copies ran while one was open for 4% of the time, Pallas kernels for 0%

profile of v4, /device:TPU:1, one launch (start us, length us, event | category | flops | bytes accessed | tf_op | source)
XLA Modules:
  0.0 156.4 jit_solution(2093377535693647264)
XLA Ops:
  0.0 1.4 broadcast_in_dim.46
  1.4 15.7 %all-to-all-start = ((bf16[16,1,4,1024]{3,2,1,0:T(4,128)(2,1)}), bf16[16,1,4,1024]{3,2,1,0:T(4,128)(2,1)S(1)}, u32[]{:S(2)}, u32[]{:S(2)}) async-start(bf16[16,1,4,1024]{3,2,1,0:T(4,128)(2,1)} %broadcast_in_dim.46), calls=%async_computation | async-start | bytes 262144 | tf_op jit(solution)/shard_map/all_to_all | solution.py:19
  17.2 0.7 iota_compare_fusion.1
  17.9 0.8 select_reduce_fusion
  18.8 0.8 broadcast_reduce_fusion.1
  19.5 0.7 broadcast_multiply_fusion
  20.2 0.7 broadcast_compare_fusion
  21.0 0.1 copy.35
  21.1 0.1 broadcast_reduce_fusion
  21.3 0.7 iota_compare_fusion
  22.1 0.1 and.62
  22.2 0.3 and.63
  22.5 0.2 and.66
  22.7 0.2 and.67
  22.9 0.7 sub.42
  23.6 0.1 compare_and_fusion
  23.9 0.1 broadcast_in_dim.36
  24.1 5.0 %all-to-all-done = bf16[16,1,4,1024]{3,2,1,0:T(4,128)(2,1)S(1)} async-done(((bf16[16,1,4,1024]{3,2,1,0:T(4,128)(2,1)}), bf16[16,1,4,1024]{3,2,1,0:T(4,128)(2,1)S(1)}, u32[]{:S(2)}, u32[]{:S(2)}) %all-to-all-start) | async-done | bytes 131104 | tf_op jit(solution)/shard_map/all_to_all | solution.py:19
  29.1 10.2 %all-gather = bf16[64,1,4,1024]{3,2,1,0:T(4,128)(2,1)S(1)} all-gather(bf16[16,1,4,1024]{3,2,1,0:T(4,128)(2,1)S(1)} %all-to-all-done), channel_id=2, replica_groups=mesh['sx'=4,'sz'=16,'tp'=8] {'sx'}, dimensions={0}, use_global_device_ids=true | all-gather | bytes 655360 | tf_op jit(solution)/shard_map/all_gather | solution.py:21
  39.4 0.2 reshape.388
  39.6 10.5 %fusion = (f32[64,4,8]{0,2,1:T(8,128)S(1)}, f32[2564,64,4,8]{0,1,3,2:T(8,128)}) fusion(pred[64,4,2564]{2,0,1:T(8,128)(4,1)S(1)} %pad_add_fusion, bf16[64,4,8,128]{3,2,1,0:T(8,128)(2,1)S(1)} %reshape.388, bf16[4,1,128]{2,0,1:T(4,128)(2,1)} %bitcast.99, bf16[1024,1,128]{2,0,1:T(8,128)(2,1)} %bitcast.97, bf16[1536,1,128]{2,0,1:T(8,128)(2,1)} %bitcast.95), kind=kOutput, calls=%fused_computation.2 | convolution fusion | flops 1361994752 | bytes 22849536 | tf_op jit(solution)/shard_map/rjkhd,nkd->rjkhn/dot_general | solution.py:119
  50.1 0.1 reshape.380
  50.2 11.2 %fusion.1 = f32[64,4,8]{0,2,1:T(8,128)S(1)} fusion(f32[2564,64,4,8]{0,1,3,2:T(8,128)} %get-tuple-element.12, f32[64,4,8]{0,2,1:T(8,128)S(1)} %get-tuple-element.11, pred[64,4,2564]{2,0,1:T(8,128)(4,1)S(1)} %pad_add_fusion), kind=kLoop, calls=%fused_computation.3 | loop fusion | flops 26253312 | bytes 21677056 | tf_op jit(solution)/shard_map/reduce_sum | solution.py:125
  61.5 9.5 %fusion.7 = f32[64,4,1,8,128]{4,0,3,1,2:T(8,128)S(1)} fusion(f32[2564,64,4,8]{0,1,3,2:T(8,128)} %get-tuple-element.12, f32[64,4,8]{0,2,1:T(8,128)S(1)} %get-tuple-element.11, pred[64,4,2564]{2,0,1:T(8,128)(4,1)S(1)} %pad_add_fusion, bf16[4,1,128]{2,0,1:T(4,128)(2,1)S(1)} %bitcast.100, bf16[1024,1,128]{2,0,1:T(8,128)(2,1)S(1)} %bitcast.98, ...), kind=kOutput, calls=%fused_computation.9 | convolution fusion | flops 1372498944 | bytes 23373824 | tf_op jit(solution)/shard_map/rjkhn,nkd->rjkhd/dot_general | solution.py:126
  71.0 0.6 copy.38
  71.6 0.2 reshape_reshape.6
  72.0 0.1 reshape.381
  72.2 0.3 mul.107
  72.5 0.2 mul.108
  72.7 0.1 fusion.20
  72.8 0.2 concatenate.35
  73.1 10.2 %all_to_all.29 = bf16[4,16,1,4160]{3,1,2,0:T(8,128)(2,1)S(1)} all-to-all(bf16[4,16,1,4160]{3,1,2,0:T(8,128)(2,1)S(1)} %bitcast.88), channel_id=1, replica_groups=mesh['sx'=4,'sz'=16,'tp'=8] {'sx'}, dimensions={0} | all-to-all | bytes 1064960 | tf_op jit(solution)/shard_map/all_to_all | solution.py:143
  83.5 0.3 mul.112
  83.8 0.2 mul.113
  84.0 0.1 fusion.10
  84.1 0.3 reshape.382
  84.4 1.8 %concatenate.36 = f32[16,1,4160]{2,1,0:T(1,128)} concatenate(f32[16,1,4096]{2,1,0:T(1,128)S(1)} %reshape.382, f32[16,1,32]{2,1,0:T(1,128)S(1)} %bitcast.91, f32[16,1,32]{2,1,0:T(1,128)S(1)} %bitcast.92), dimensions={2} | concatenate | bytes 532480 | tf_op jit(solution)/shard_map/concatenate | solution.py:145
  86.2 6.9 %all-to-all-start.2 = ((f32[16,1,4160]{2,1,0:T(1,128)}), f32[16,1,4160]{2,1,0:T(1,128)S(1)}, u32[]{:S(2)}, u32[]{:S(2)}) async-start(f32[16,1,4160]{2,1,0:T(1,128)} %concatenate.36), calls=%async_computation.2 | async-start | bytes 540672 | tf_op jit(solution)/shard_map/all_to_all | solution.py:146
  93.1 0.2 convert_reduce_fusion
  93.3 12.7 %all-to-all-done.2 = f32[16,1,4160]{2,1,0:T(1,128)S(1)} async-done(((f32[16,1,4160]{2,1,0:T(1,128)}), f32[16,1,4160]{2,1,0:T(1,128)S(1)}, u32[]{:S(2)}, u32[]{:S(2)}) %all-to-all-start.2) | async-done | bytes 266272 | tf_op jit(solution)/shard_map/all_to_all | solution.py:146
  106.0 0.1 fusion.27
  106.3 0.1 mul.117
  106.4 0.3 fusion.22
  106.8 18.0 %all_to_all.30 = bf16[16,4,1024]{2,1,0:T(4,128)(2,1)S(1)} all-to-all(bf16[16,4,1024]{2,1,0:T(4,128)(2,1)S(1)} %broadcast_in_dim.49), channel_id=1, replica_groups=mesh['sx'=4,'sz'=16,'tp'=8] {'sz'}, dimensions={0} | all-to-all | bytes 262144 | tf_op jit(solution)/shard_map/all_to_all | solution.py:19
  124.8 10.5 %all_gather.7 = bf16[256,1024]{1,0:T(8,128)(2,1)S(1)} all-gather(bf16[64,1024]{1,0:T(8,128)(2,1)S(1)} %reshape.383), channel_id=1, replica_groups=mesh['sx'=4,'sz'=16,'tp'=8] {'sx'}, dimensions={0}, use_global_device_ids=true | all-gather | bytes 655360 | tf_op jit(solution)/shard_map/all_gather | solution.py:21
  135.3 0.3 fusion.33
  135.6 20.2 %all_to_all.31 = f32[8,32,128]{2,1,0:T(8,128)S(1)} all-to-all(f32[8,32,128]{2,1,0:T(8,128)S(1)} %bitcast.90), channel_id=1, replica_groups=mesh['sx'=4,'sz'=16,'tp'=8] {'tp'}, dimensions={0} | all-to-all | bytes 262144 | tf_op jit(solution)/shard_map/all_to_all | solution.py:158
  155.8 0.6 reduce_sum.72
  (40 shorter events, 1.4 us)
Async XLA Ops:
  0.0 135.3 %copy-start = (bf16[1024,128]{1,0:T(8,128)(2,1)S(1)}, bf16[1024,128]{1,0:T(8,128)(2,1)}, u32[]{:S(2)}) copy-start(bf16[1024,128]{1,0:T(8,128)(2,1)} %param.21) | copy-start | bytes 786436
  1.4 27.7 %all-to-all-start = ((bf16[16,1,4,1024]{3,2,1,0:T(4,128)(2,1)}), bf16[16,1,4,1024]{3,2,1,0:T(4,128)(2,1)S(1)}, u32[]{:S(2)}, u32[]{:S(2)}) async-start(bf16[16,1,4,1024]{3,2,1,0:T(4,128)(2,1)} %broadcast_in_dim.46), calls=%async_computation | async-start | bytes 262144 | tf_op jit(solution)/shard_map/all_to_all | solution.py:19
  39.6 21.9 %copy-start.2 = (bf16[8,192,128]{2,1,0:T(8,128)(2,1)S(1)}, bf16[8,192,128]{2,1,0:T(8,128)(2,1)}, u32[]{:S(2)}) copy-start(bf16[8,192,128]{2,1,0:T(8,128)(2,1)} %param.18) | copy-start | bytes 1179652
  39.6 21.8 %copy-start.3 = (bf16[16,64,128]{2,1,0:T(8,128)(2,1)S(1)}, bf16[16,64,128]{2,1,0:T(8,128)(2,1)}, u32[]{:S(2)}) copy-start(bf16[16,64,128]{2,1,0:T(8,128)(2,1)} %param.20) | copy-start | bytes 786436
  39.6 21.8 %copy-start.4 = (bf16[1,4,128]{2,1,0:T(4,128)(2,1)S(1)}, bf16[1,4,128]{2,1,0:T(4,128)(2,1)}, u32[]{:S(2)}) copy-start(bf16[1,4,128]{2,1,0:T(4,128)(2,1)} %param.16) | copy-start | bytes 3076
  61.4 31.6 %copy-start.1 = (s32[64,4]{0,1:T(4,128)S(1)}, s32[64,4]{0,1:T(4,128)}, u32[]{:S(2)}) copy-start(s32[64,4]{0,1:T(4,128)} %param.27) | copy-start | bytes 3076
  86.2 19.8 %all-to-all-start.2 = ((f32[16,1,4160]{2,1,0:T(1,128)}), f32[16,1,4160]{2,1,0:T(1,128)S(1)}, u32[]{:S(2)}, u32[]{:S(2)}) async-start(f32[16,1,4160]{2,1,0:T(1,128)} %concatenate.36), calls=%async_computation.2 | async-start | bytes 540672 | tf_op jit(solution)/shard_map/all_to_all | solution.py:146

commit v5 on v4

--- a/solution.py
+++ b/solution.py
@@ -19,6 +19,13 @@
     block = lax.all_to_all(copies, "sz", 0, 0, tiled=True)
     block = block.reshape((inner * block.shape[1],) + block.shape[2:])
     return lax.all_gather(block, "sx", axis=0, tiled=True)
+
+
+def softmax_part(scores, key_mask):
+    masked = jnp.where(key_mask, scores, NEG)
+    row_peak = jnp.max(masked, axis=-1)
+    weights = jnp.where(key_mask, jnp.exp(masked - row_peak[..., None]), 0.0)
+    return (row_peak, jnp.sum(weights, axis=-1), weights.astype(jnp.bfloat16))
 
 
 def merge(parts, n_out, n_stat):
@@ -75,56 +82,70 @@
     pre_dev = prefix_keys.shape[1]
     page_count = page_keys.shape[0]
     page_len = page_keys.shape[1]
-    keys = jnp.concatenate(
-        [
-            prefix_keys.reshape(GROUPS * pre_dev, kv_local, HEAD_DIM),
-            page_keys.reshape(page_count * page_len, kv_local, HEAD_DIM),
-            new_keys.reshape(req_dev * NEW, kv_local, HEAD_DIM),
-        ],
-        axis=0,
-    )
-    values = jnp.concatenate(
-        [
-            prefix_values.reshape(GROUPS * pre_dev, kv_local, HEAD_DIM),
-            page_values.reshape(page_count * page_len, kv_local, HEAD_DIM),
-            new_values.reshape(req_dev * NEW, kv_local, HEAD_DIM),
-        ],
-        axis=0,
-    )
-
     req_ids = jnp.arange(requests, dtype=jnp.int32)
+
+    pre_k = prefix_keys.reshape(GROUPS, pre_dev, kv_local, HEAD_DIM)
+    pre_v = prefix_values.reshape(GROUPS, pre_dev, kv_local, HEAD_DIM)
+    req_keys = jnp.take(pre_k, group_of, axis=0)
+    req_values = jnp.take(pre_v, group_of, axis=0)
     positions = seq_idx * pre_dev + jnp.arange(pre_dev, dtype=jnp.int32)
-    pre_live = positions[None, :] < prefix_len[:, None]
-    pre_mask = group_hot[:, :, None] & pre_live[None, :, :]
-    pre_mask = pre_mask.reshape(requests, 1, GROUPS * pre_dev)
-    pre_mask = jnp.broadcast_to(pre_mask, (requests, NEW, GROUPS * pre_dev))
-    owner_hot = req_ids[:, None] == page_owner[None, :]
+    pre_live = positions[None, :] < own_prefix[:, None]
+    scores = (
+        jnp.einsum("rjkhd,rpkd->rjkhp", query_all, req_keys, preferred_element_type=jnp.float32)
+        * score_scale
+    )
+    pre_peak, pre_total, weights = softmax_part(scores, pre_live[:, None, None, None, :])
+    pre_out = jnp.einsum(
+        "rjkhp,rpkd->rjkhd", weights, req_values, preferred_element_type=jnp.float32
+    )
+
+    page_q = jnp.take(query_all, page_owner, axis=0)
+    key_pages = page_keys.reshape(page_count, page_len, kv_local, HEAD_DIM)
+    value_pages = page_values.reshape(page_count, page_len, kv_local, HEAD_DIM)
+    own_suffix = jnp.take(suffix_len, page_owner)
     offsets = page_slot[:, None] * page_len + jnp.arange(page_len, dtype=jnp.int32)[None, :]
-    page_live = offsets[None, :, :] < suffix_len[:, None, None]
-    page_mask = (owner_hot[:, :, None] & page_live).reshape(requests, 1, page_count * page_len)
-    page_mask = jnp.broadcast_to(page_mask, (requests, NEW, page_count * page_len))
-    new_owner = seq_idx * req_dev + jnp.arange(req_dev, dtype=jnp.int32)
+    page_live = offsets < own_suffix[:, None]
+    scores = (
+        jnp.einsum("qjkhd,qikd->qjkhi", page_q, key_pages, preferred_element_type=jnp.float32)
+        * score_scale
+    )
+    page_peak, page_total, weights = softmax_part(scores, page_live[:, None, None, None, :])
+    page_out = jnp.einsum(
+        "qjkhi,qikd->qjkhd", weights, value_pages, preferred_element_type=jnp.float32
+    )
+
+    row_start = seq_idx * req_dev
+    valid_local = lax.dynamic_slice_in_dim(new_valid, row_start, req_dev, 0)
+    local_q = queries.reshape(req_dev, NEW, kv_local, HPK, HEAD_DIM)
+    local_k = new_keys.reshape(req_dev, NEW, kv_local, HEAD_DIM)
+    local_v = new_values.reshape(req_dev, NEW, kv_local, HEAD_DIM)
     tok = jnp.arange(NEW, dtype=jnp.int32)
     causal = tok[None, :] <= tok[:, None]
-    new_live = new_valid == 1
-    new_mask = (
-        (req_ids[:, None, None, None] == new_owner[None, None, :, None])
-        & causal[None, :, None, :]
-        & new_live[:, None, None, :]
-    ).reshape(requests, NEW, req_dev * NEW)
-    key_mask = jnp.concatenate([pre_mask, page_mask, new_mask], axis=2)
-    key_mask = key_mask[:, :, None, None, :]
-
+    new_mask = causal[None, :, None, None, :] & (valid_local[:, None, None, None, :] == 1)
     scores = (
-        jnp.einsum("rjkhd,nkd->rjkhn", query_all, keys, preferred_element_type=jnp.float32)
+        jnp.einsum("rjkhd,rikd->rjkhi", local_q, local_k, preferred_element_type=jnp.float32)
         * score_scale
     )
-    masked = jnp.where(key_mask, scores, NEG)
-    row_peak = jnp.max(masked, axis=-1)
-    weights = jnp.where(key_mask, jnp.exp(masked - row_peak[..., None]), 0.0)
-    row_total = jnp.sum(weights, axis=-1)
-    out = jnp.einsum(
-        "rjkhn,nkd->rjkhd", weights.astype(jnp.bfloat16), values, preferred_element_type=jnp.float32
+    new_peak, new_total, weights = softmax_part(scores, new_mask)
+    new_out = jnp.einsum(
+        "rjkhi,rikd->rjkhd", weights, local_v, preferred_element_type=jnp.float32
+    )
+
+    ex_owner = jnp.concatenate([page_owner, row_start + jnp.arange(req_dev, dtype=jnp.int32)])
+    ex_peak = jnp.concatenate([page_peak, new_peak], axis=0)
+    ex_total = jnp.concatenate([page_total, new_total], axis=0)
+    ex_out = jnp.concatenate([page_out, new_out], axis=0)
+    ex_hot = ex_owner[None, :] == req_ids[:, None]
+    ex_top = jnp.max(jnp.where(ex_hot[:, :, None, None, None], ex_peak[None], NEG), axis=1)
+    row_peak = jnp.maximum(pre_peak, ex_top)
+    pre_factor = jnp.exp(pre_peak - row_peak)
+    ex_factor = jnp.exp(ex_peak - jnp.take(row_peak, ex_owner, axis=0))
+    hot = ex_hot.astype(jnp.float32)
+    row_total = pre_total * pre_factor + jnp.einsum(
+        "re,ejkh->rjkh", hot, ex_total * ex_factor, precision=lax.Precision.HIGHEST
+    )
+    out = pre_out * pre_factor[..., None] + jnp.einsum(
+        "re,ejkhd->rjkhd", hot, ex_out * ex_factor[..., None], precision=lax.Precision.HIGHEST
     )
 
     flat_out = out.reshape(requests, -1)
@@ -147,8 +168,6 @@
     final_out, _, final_total = merge(received, n_out, n_stat)
     final_out = final_out.reshape(req_dev, NEW, kv_local, HPK, HEAD_DIM)
     final_total = final_total.reshape(req_dev, NEW, kv_local, HPK)
-    row_start = seq_idx * req_dev
-    valid_local = lax.dynamic_slice_in_dim(new_valid, row_start, req_dev, 0)
     valid_rows = valid_local.astype(jnp.float32)[:, :, None, None, None]
     attention = (final_out / final_total[..., None] * valid_rows).astype(jnp.bfloat16)
     attention = attention.reshape(req_dev * NEW, heads_local * HEAD_DIM)

time: 157 us -> 169 us (1.076)
  local copies, waits for them, and re-layouts: 8.8 us -> 26.2 us
  waiting for transfers between devices: 17.7 us -> 12.7 us
  matrix products: 20.3 us -> 15.6 us
  starting transfers between devices: 22.6 us -> 27.1 us
    reduce_sum x1 -> x3, other arithmetic: 11.2 us -> 2.07 us  [softmax_part(): return (row_peak, jnp.sum(weights, axis=-1), weights.astype(jnp.bfloat16))]
    gather x0 -> x5, local copies, waits for them, and re-layouts: none -> 7.09 us  [the longest x1 2.65 us: local(): req_keys = jnp.take(pre_k, group_of, axis=0)]
    dot_general x2 -> x7, matrix products: 20 us -> 13.8 us  [the longest x1 4.35 us: local(): jnp.einsum('rjkhp,rpkd->rjkhd', weights, req_values, preferred_element_ty...]
    all_to_all x1, waiting for transfers between devices: 5.03 us -> 0.01 us  [gather_rows(): block = lax.all_to_all(copies, 'sz', 0, 0, tiled=True)]
    all_to_all x1, starting transfers between devices: 6.9 us -> 11.3 us  [local(): received = lax.all_to_all(packed, 'sz', 0, 0, tiled=True)]
    concatenate x1 -> x3, local copies, waits for them, and re-layouts: 0.23 us -> 3.1 us  [local(): jnp.concatenate([flat_out, near_peak, total], axis=1).astype(jnp.bfloat16)]
    select_n x0 -> x4, other arithmetic: none -> 2.74 us  [the longest x2 1.35 us: local(): own_suffix = jnp.take(suffix_len, page_owner)]
    mul x3, local copies, waits for them, and re-layouts: 0.65 us -> 2.86 us  [merge(): out = parts[..., :n_out].reshape(lead + (n_stat, n_out // n_stat)) * rows]
  transfers between devices with their start and end apart: 2 -> 2, of which waited for: 2 -> 1; matrix products, arithmetic and copies ran while one was open for 4% -> 10% of each run, Pallas kernels for 0% -> 0%
where the time goes in v5:
time: 169 us; the launch traced here: 168 us
  blocking collectives  69.7 us (41%)
  starting transfers between devices  27.1 us (16%)
  local copies, waits for them, and re-layouts  26.2 us (16%)
  other arithmetic  16 us (9%)
  matrix products  15.6 us (9%)
  waiting for transfers between devices  12.7 us (8%)
    all_gather x2, blocking collectives, gather_rows(): return lax.all_gather(block, 'sx', axis=0, tiled=True)  22.1 us
    all_to_all x1, blocking collectives, local(): blocks = lax.all_to_all(terms, 'tp', 0, 0, tiled=True)  20.2 us
    all_to_all x1, blocking collectives, gather_rows(): block = lax.all_to_all(copies, 'sz', 0, 0, tiled=True)  18 us
    all_to_all x1, starting transfers between devices, gather_rows(): block = lax.all_to_all(copies, 'sz', 0, 0, tiled=True)  15.7 us
    all_to_all x1, waiting for transfers between devices, local(): received = lax.all_to_all(packed, 'sz', 0, 0, tiled=True)  12.7 us
    all_to_all x1, starting transfers between devices, local(): received = lax.all_to_all(packed, 'sz', 0, 0, tiled=True)  11.3 us
    all_to_all x1, blocking collectives, local(): lax.all_to_all(packed, 'sx', 0, 0, tiled=True).astype(jnp.float32)  9.39 us
    dot_general x1, matrix products, local(): jnp.einsum('rjkhp,rpkd->rjkhd', weights, req_values, preferred_element_ty...  4.35 us
  transfers between devices with their start and end apart: 2, of which 1 were waited for; matrix products, arithmetic and copies ran while one was open for 10% of the time, Pallas kernels for 0%

profile of v5, /device:TPU:1, one launch (start us, length us, event | category | flops | bytes accessed | tf_op | source)
XLA Modules:
  0.0 167.5 jit_solution(1492917407485410836)
XLA Ops:
  0.0 1.4 broadcast_in_dim.170
  1.4 15.7 %all-to-all-start = ((bf16[16,1,4,1024]{3,2,1,0:T(4,128)(2,1)}), bf16[16,1,4,1024]{3,2,1,0:T(4,128)(2,1)S(1)}, u32[]{:S(2)}, u32[]{:S(2)}) async-start(bf16[16,1,4,1024]{3,2,1,0:T(4,128)(2,1)} %broadcast_in_dim.170), calls=%async_computation | async-start | bytes 262144 | tf_op jit(solution)/shard_map/all_to_all | solution.py:19
  17.2 0.7 compare_select_fusion
  17.8 1.2 compare_and_fusion
  19.0 0.9 compare_reduce_fusion
  20.0 0.7 compare_select_fusion.3
  20.6 0.8 select_reduce_fusion.1
  21.4 0.7 compare_and_fusion.1
  22.1 0.7 fusion.74
  22.9 0.8 convolution_multiply_fusion.1
  23.9 0.7 sub.80
  24.6 0.7 gather_fusion
  25.2 0.7 broadcast_select_fusion
  26.0 1.5 convolution_bitcast_fusion
  27.6 2.7 %gather_fusion.4 = bf16[64,192,128]{2,1,0:T(8,128)(2,1)} fusion(bf16[8,192,128]{2,1,0:T(8,128)(2,1)S(1)} %copy-done, s32[1024]{0:T(1024)S(1)} %pad_clamp_fusion.2), kind=kCustom, calls=%fused_computation.1.clone | custom fusion | bytes 6291712 | tf_op jit(solution)/shard_map/jit(_take)/gather | solution.py:89
  30.2 2.6 %gather_fusion.3 = bf16[64,192,128]{2,1,0:T(8,128)(2,1)} fusion(bf16[8,192,128]{2,1,0:T(8,128)(2,1)S(1)} %copy-done.1, s32[1024]{0:T(1024)S(1)} %pad_clamp_fusion.2), kind=kCustom, calls=%fused_computation.clone | custom fusion | bytes 6291712 | tf_op jit(solution)/shard_map/jit(_take)/gather | solution.py:90
  33.0 11.6 %all-gather = bf16[64,1,4,1024]{3,2,1,0:T(4,128)(2,1)S(1)} all-gather(bf16[16,1,4,1024]{3,2,1,0:T(4,128)(2,1)S(1)} %all-to-all-done), channel_id=2, replica_groups=mesh['sx'=4,'sz'=16,'tp'=8] {'sx'}, dimensions={0}, use_global_device_ids=true | all-gather | bytes 655360 | tf_op jit(solution)/shard_map/all_gather | solution.py:21
  44.9 0.6 gather_fusion.1
  46.2 4.1 %bitcast_reduce_fusion = (f32[64,4,8]{2,1,0:T(4,128)S(1)}, f32[64,192,4,8]{1,3,2,0:T(8,128)S(1)}) fusion(pred[64,192]{1,0:T(8,128)(4,1)S(1)} %broadcast_compare_fusion, bf16[64,4,8,128]{3,2,1,0:T(8,128)(2,1)S(1)} %reshape.632, bf16[64,192,128]{2,1,0:T(8,128)(2,1)} %gather_fusion.4, pred[64]{0:T(512)(128)(4,1)S(1)} %copy-done.17), kind=kOutput, calls=%fused_computation.14 | convolution fusion | flops 103413760 | bytes 5263424 | tf_op jit(solution)/shard_map/rjkhd,rpkd->rjkhp/dot_general | solution.py:94
  50.5 0.8 fusion.59
  51.4 0.6 subtract_exponential_fusion.1
  52.0 0.7 max.45
  53.1 0.6 gather_fusion.2
  53.7 0.7 maximum_multiply_fusion.1
  54.4 0.7 copy.102
  55.1 1.7 %fusion.10 = f32[64,4,8]{2,1,0:T(4,128)} fusion(f32[64,192,4,8]{1,3,2,0:T(8,128)S(1)} %get-tuple-element.25, f32[64,4,8]{2,1,0:T(4,128)S(1)} %get-tuple-element.24, pred[64,192]{1,0:T(8,128)(4,1)S(1)} %broadcast_compare_fusion), kind=kLoop, calls=%fused_computation.20 | loop fusion | flops 1964032 | bytes 1601536 | tf_op jit(solution)/shard_map/reduce_sum | solution.py:28
  56.7 1.7 %copy.101 = f32[64,4,8]{0,2,1:T(8,128)} copy(f32[64,4,8]{2,1,0:T(4,128)} %fusion.10) | data formatting | bytes 16384 | tf_op jit(solution)/shard_map/reduce_sum | solution.py:28
  58.5 1.5 copy.95
  60.0 1.6 fusion.27
  61.5 1.4 reshape.640
  62.9 1.6 fusion.55
  64.5 1.4 copy.103
  65.9 1.4 copy.104
  67.4 1.4 fusion.40
  68.8 0.9 maximum_multiply_fusion
  69.7 1.3 fusion.38
  71.0 4.3 %fusion.21 = f32[64,4,1,8,128]{4,3,1,0,2:T(8,128)} fusion(bf16[64,192,128]{2,1,0:T(8,128)(2,1)S(1)} %copy-done.2, pred[64]{0:T(512)(128)(4,1)S(1)} %copy-done.18, f32[64,192,4,8]{1,3,2,0:T(8,128)} %copy-done.3, f32[64,4,8,128]{3,0,2,1:T(8,128)S(1)} %fusion.38, f32[64,4,8]{2,1,0:T(4,128)S(1)} %copy-done.6, pred[64,192]{1,0:T(8,128)(4,1)S(1)} %broadcast_compare_fusion, ...), kind=kOutput, calls=%fused_computation.25 | convolution fusion | flops 104726528 | bytes 6844480 | tf_op jit(solution)/shard_map/rjkhp,rpkd->rjkhd/dot_general | solution.py:98
  75.4 1.4 reshape_reshape.6
  78.4 9.4 %all_to_all.29 = bf16[4,16,1,4160]{3,1,2,0:T(8,128)(2,1)S(1)} all-to-all(bf16[4,16,1,4160]{3,1,2,0:T(8,128)(2,1)S(1)} %concatenate.95), channel_id=1, replica_groups=mesh['sx'=4,'sz'=16,'tp'=8] {'sx'}, dimensions={0} | all-to-all | bytes 1064960 | tf_op jit(solution)/shard_map/all_to_all | solution.py:164
  88.0 1.3 mul.181
  89.3 1.4 mul.182
  91.1 1.8 %concatenate.96 = f32[16,1,4160]{2,1,0:T(1,128)} concatenate(f32[16,1,4096]{2,1,0:T(1,128)S(1)} %reshape.641, f32[16,1,32]{2,1,0:T(1,128)S(1)} %bitcast.215, f32[16,1,32]{2,1,0:T(1,128)S(1)} %bitcast.216), dimensions={2} | concatenate | bytes 532480 | tf_op jit(solution)/shard_map/concatenate | solution.py:166
  92.9 11.3 %all-to-all-start.2 = ((f32[16,1,4160]{2,1,0:T(1,128)}), f32[16,1,4160]{2,1,0:T(1,128)S(1)}, u32[]{:S(2)}, u32[]{:S(2)}) async-start(f32[16,1,4160]{2,1,0:T(1,128)} %concatenate.96), calls=%async_computation.2 | async-start | bytes 540672 | tf_op jit(solution)/shard_map/all_to_all | solution.py:167
  104.4 12.7 %all-to-all-done.2 = f32[16,1,4160]{2,1,0:T(1,128)S(1)} async-done(((f32[16,1,4160]{2,1,0:T(1,128)}), f32[16,1,4160]{2,1,0:T(1,128)S(1)}, u32[]{:S(2)}, u32[]{:S(2)}) %all-to-all-start.2) | async-done | bytes 266272 | tf_op jit(solution)/shard_map/all_to_all | solution.py:167
  118.0 18.0 %all_to_all.30 = bf16[16,4,1024]{2,1,0:T(4,128)(2,1)S(1)} all-to-all(bf16[16,4,1024]{2,1,0:T(4,128)(2,1)S(1)} %broadcast_in_dim.189), channel_id=1, replica_groups=mesh['sx'=4,'sz'=16,'tp'=8] {'sz'}, dimensions={0} | all-to-all | bytes 262144 | tf_op jit(solution)/shard_map/all_to_all | solution.py:19
  135.9 10.5 %all_gather.7 = bf16[256,1024]{1,0:T(8,128)(2,1)S(1)} all-gather(bf16[64,1024]{1,0:T(8,128)(2,1)S(1)} %reshape.642), channel_id=1, replica_groups=mesh['sx'=4,'sz'=16,'tp'=8] {'sx'}, dimensions={0}, use_global_device_ids=true | all-gather | bytes 655360 | tf_op jit(solution)/shard_map/all_gather | solution.py:21
  146.7 20.2 %all_to_all.31 = f32[8,32,128]{2,1,0:T(8,128)S(1)} all-to-all(f32[8,32,128]{2,1,0:T(8,128)S(1)} %bitcast.213), channel_id=1, replica_groups=mesh['sx'=4,'sz'=16,'tp'=8] {'tp'}, dimensions={0} | all-to-all | bytes 262144 | tf_op jit(solution)/shard_map/all_to_all | solution.py:177
  166.9 0.6 reduce_sum.92
  (81 shorter events, 5.6 us)
Async XLA Ops:
  0.0 27.6 %copy-start = (bf16[8,192,128]{2,1,0:T(8,128)(2,1)S(1)}, bf16[8,192,128]{2,1,0:T(8,128)(2,1)}, u32[]{:S(2)}) copy-start(bf16[8,192,128]{2,1,0:T(8,128)(2,1)} %param.19) | copy-start | bytes 1179652
  1.4 31.6 %all-to-all-start = ((bf16[16,1,4,1024]{3,2,1,0:T(4,128)(2,1)}), bf16[16,1,4,1024]{3,2,1,0:T(4,128)(2,1)S(1)}, u32[]{:S(2)}, u32[]{:S(2)}) async-start(bf16[16,1,4,1024]{3,2,1,0:T(4,128)(2,1)} %broadcast_in_dim.170), calls=%async_computation | async-start | bytes 262144 | tf_op jit(solution)/shard_map/all_to_all | solution.py:19
  22.1 10.7 %copy-start.15 = (s32[17]{0:T(128)}, s32[17]{0:T(128)S(1)}, u32[]{:S(2)}) copy-start(s32[17]{0:T(128)S(1)} %get-tuple-element.13) | copy-start | bytes 208
  26.0 26.8 %copy-start.14 = (pred[16,64]{1,0:T(8,128)(4,1)}, pred[16,64]{1,0:T(8,128)(4,1)S(1)}, u32[]{:S(2)}) copy-start(pred[16,64]{1,0:T(8,128)(4,1)S(1)} %add_compare_fusion) | copy-start | bytes 3076
  27.6 2.7 %copy-start.1 = (bf16[8,192,128]{2,1,0:T(8,128)(2,1)S(1)}, bf16[8,192,128]{2,1,0:T(8,128)(2,1)}, u32[]{:S(2)}) copy-start(bf16[8,192,128]{2,1,0:T(8,128)(2,1)} %param.20) | copy-start | bytes 1179652
  30.2 15.2 %copy-start.9 = (bf16[16,64,128]{2,1,0:T(8,128)(2,1)S(1)}, bf16[16,64,128]{2,1,0:T(8,128)(2,1)}, u32[]{:S(2)}) copy-start(bf16[16,64,128]{2,1,0:T(8,128)(2,1)} %param.21) | copy-start | bytes 786436
  32.9 13.3 %copy-start.17 = (pred[64]{0:T(512)(128)(4,1)S(1)}, pred[64]{0:T(512)(128)(4,1)}, u32[]{:S(2)}) copy-start(pred[64]{0:T(512)(128)(4,1)} %compare_and_fusion) | copy-start | bytes 196
  45.9 6.9 %copy-start.4 = (f32[16,4,1,8,64]{4,3,1,0,2:T(8,128)}, f32[16,4,1,8,64]{4,3,1,0,2:T(8,128)S(1)}, u32[]{:S(2)}) copy-start(f32[16,4,1,8,64]{4,3,1,0,2:T(8,128)S(1)} %get-tuple-element.23) | copy-start | bytes 393220
  45.9 7.8 %copy-start.7 = (f32[16,4,8]{2,1,0:T(4,128)}, f32[16,4,8]{2,1,0:T(4,128)S(1)}, u32[]{:S(2)}) copy-start(f32[16,4,8]{2,1,0:T(4,128)S(1)} %get-tuple-element.22) | copy-start | bytes 6148
  50.2 4.8 %copy-start.3 = (f32[64,192,4,8]{1,3,2,0:T(8,128)}, f32[64,192,4,8]{1,3,2,0:T(8,128)S(1)}, u32[]{:S(2)}) copy-start(f32[64,192,4,8]{1,3,2,0:T(8,128)S(1)} %get-tuple-element.25) | copy-start | bytes 4718596
  50.2 4.8 %copy-start.5 = (f32[64,4,8]{2,1,0:T(4,128)}, f32[64,4,8]{2,1,0:T(4,128)S(1)}, u32[]{:S(2)}) copy-start(f32[64,4,8]{2,1,0:T(4,128)S(1)} %get-tuple-element.24) | copy-start | bytes 24580
  56.7 14.2 %copy-start.2 = (bf16[64,192,128]{2,1,0:T(8,128)(2,1)S(1)}, bf16[64,192,128]{2,1,0:T(8,128)(2,1)}, u32[]{:S(2)}) copy-start(bf16[64,192,128]{2,1,0:T(8,128)(2,1)} %gather_fusion.3) | copy-start | bytes 9437188
  67.4 3.6 %copy-start.6 = (f32[64,4,8]{2,1,0:T(4,128)S(1)}, f32[64,4,8]{2,1,0:T(4,128)}, u32[]{:S(2)}) copy-start(f32[64,4,8]{2,1,0:T(4,128)} %copy-done.5) | copy-start | bytes 24580
  67.4 3.6 %copy-start.10 = (f32[64,4,8]{2,1,0:T(4,128)S(1)}, f32[64,4,8]{2,1,0:T(4,128)}, u32[]{:S(2)}) copy-start(f32[64,4,8]{2,1,0:T(4,128)} %copy.95) | copy-start | bytes 24580
  67.4 3.6 %copy-start.18 = (pred[64]{0:T(512)(128)(4,1)S(1)}, pred[64]{0:T(512)(128)(4,1)}, u32[]{:S(2)}) copy-start(pred[64]{0:T(512)(128)(4,1)} %compare_and_fusion) | copy-start | bytes 196
  75.4 1.4 copy-start.13
  77.2 0.7 copy-start.11
  77.5 0.7 copy-start.12
  90.7 13.5 %copy-start.16 = (s32[64,4]{0,1:T(4,128)S(1)}, s32[64,4]{0,1:T(4,128)}, u32[]{:S(2)}) copy-start(s32[64,4]{0,1:T(4,128)} %param.29) | copy-start | bytes 3076
  90.8 55.6 %copy-start.8 = (bf16[1024,128]{1,0:T(8,128)(2,1)S(1)}, bf16[1024,128]{1,0:T(8,128)(2,1)}, u32[]{:S(2)}) copy-start(bf16[1024,128]{1,0:T(8,128)(2,1)} %param.23) | copy-start | bytes 786436
  92.9 24.2 %all-to-all-start.2 = ((f32[16,1,4160]{2,1,0:T(1,128)}), f32[16,1,4160]{2,1,0:T(1,128)S(1)}, u32[]{:S(2)}, u32[]{:S(2)}) async-start(f32[16,1,4160]{2,1,0:T(1,128)} %concatenate.96), calls=%async_computation.2 | async-start | bytes 540672 | tf_op jit(solution)/shard_map/all_to_all | solution.py:167

commit v6 on v4

--- a/solution.py
+++ b/solution.py
@@ -1,6 +1,10 @@
+import functools
+
 import jax
 import jax.numpy as jnp
 from jax import lax
+from jax.experimental import pallas as pl
+from jax.experimental.pallas import tpu as pltpu
 from jax.sharding import Mesh, PartitionSpec as P
 
 HEAD_DIM = 128
@@ -19,6 +23,51 @@
     block = lax.all_to_all(copies, "sz", 0, 0, tiled=True)
     block = block.reshape((inner * block.shape[1],) + block.shape[2:])
     return lax.all_gather(block, "sx", axis=0, tiled=True)
+
+
+def attend_kernel(scale, q_ref, k_ref, v_ref, keep_ref, o_ref, m_ref, l_ref):
+    scores = lax.dot_general(
+        q_ref[...], k_ref[0], (((1,), (1,)), ((), ())), preferred_element_type=jnp.float32
+    )
+    scores = scores * scale
+    keep = keep_ref[...] > 0.5
+    masked = jnp.where(keep, scores, NEG)
+    peak = jnp.max(masked, axis=1, keepdims=True)
+    weights = jnp.where(keep, jnp.exp(masked - peak), 0.0)
+    total = jnp.sum(weights, axis=1, keepdims=True)
+    o_ref[...] = jnp.dot(
+        weights.astype(jnp.bfloat16), v_ref[0], preferred_element_type=jnp.float32
+    )
+    m_ref[...] = jnp.broadcast_to(peak, m_ref.shape)
+    l_ref[...] = jnp.broadcast_to(total, l_ref.shape)
+
+
+def attend(query_all, keys, values, key_mask, scale):
+    requests, new, kv, hpk, dim = query_all.shape
+    n_keys = keys.shape[0]
+    padded = -(-n_keys // 128) * 128
+    rows = requests * new
+    pad = ((0, padded - n_keys), (0, 0), (0, 0))
+    keys_t = jnp.pad(keys, pad).transpose(1, 0, 2)
+    values_t = jnp.pad(values, pad).transpose(1, 0, 2)
+    keep = jnp.pad(key_mask, ((0, 0), (0, 0), (0, padded - n_keys)))
+    keep = keep.reshape(rows, padded).astype(jnp.float32)
+    q_rows = query_all.transpose(2, 3, 0, 1, 4).reshape(kv * hpk * rows, dim)
+    row_block = pl.BlockSpec((rows, dim), lambda i: (i, 0))
+    kv_block = pl.BlockSpec((1, padded, dim), lambda i: (i // hpk, 0, 0))
+    stat = jax.ShapeDtypeStruct((kv * hpk * rows, dim), jnp.float32)
+    out, peak, total = pl.pallas_call(
+        functools.partial(attend_kernel, scale),
+        grid=(kv * hpk,),
+        in_specs=[row_block, kv_block, kv_block, pl.BlockSpec((rows, padded), lambda i: (0, 0))],
+        out_specs=[row_block, row_block, row_block],
+        out_shape=[stat, stat, stat],
+        compiler_params=pltpu.CompilerParams(vmem_limit_bytes=48 * 1024 * 1024),
+    )(q_rows, keys_t, values_t, keep)
+    out = out.reshape(kv, hpk, requests, new, dim).transpose(2, 3, 0, 1, 4)
+    peak = peak[:, 0].reshape(kv, hpk, requests, new).transpose(2, 3, 0, 1)
+    total = total[:, 0].reshape(kv, hpk, requests, new).transpose(2, 3, 0, 1)
+    return out, peak, total
 
 
 def merge(parts, n_out, n_stat):
@@ -113,19 +162,7 @@
         & new_live[:, None, None, :]
     ).reshape(requests, NEW, req_dev * NEW)
     key_mask = jnp.concatenate([pre_mask, page_mask, new_mask], axis=2)
-    key_mask = key_mask[:, :, None, None, :]
-
-    scores = (
-        jnp.einsum("rjkhd,nkd->rjkhn", query_all, keys, preferred_element_type=jnp.float32)
-        * score_scale
-    )
-    masked = jnp.where(key_mask, scores, NEG)
-    row_peak = jnp.max(masked, axis=-1)
-    weights = jnp.where(key_mask, jnp.exp(masked - row_peak[..., None]), 0.0)
-    row_total = jnp.sum(weights, axis=-1)
-    out = jnp.einsum(
-        "rjkhn,nkd->rjkhd", weights.astype(jnp.bfloat16), values, preferred_element_type=jnp.float32
-    )
+    out, row_peak, row_total = attend(query_all, keys, values, key_mask, score_scale)
 
     flat_out = out.reshape(requests, -1)
     peak = row_peak.reshape(requests, -1)

time: 157 us -> 152 us (0.968)
  matrix products: 20.3 us -> 0.29 us
  Pallas kernels: 0 us -> 16.8 us
  other arithmetic: 17.4 us -> 9.48 us
  local copies, waits for them, and re-layouts: 8.8 us -> 15.4 us
  waiting for transfers between devices: 17.7 us -> 12.7 us
  starting transfers between devices: 22.6 us -> 27.1 us
    dot_general x2 -> x0, matrix products: 20 us -> none  [the longest x1 10.5 us: local(): jnp.einsum('rjkhd,nkd->rjkhn', query_all, keys, preferred_element_type=jn...]
    pallas_call x0 -> x1, Pallas kernels: none -> 16.8 us  [attend(): pl.pallas_call(functools.partial(attend_kernel, scale), grid=(kv * hpk,),...]
    reduce_sum x1 -> x0, other arithmetic: 11.2 us -> none  [local(): row_total = jnp.sum(weights, axis=-1)]
    all_to_all x1, waiting for transfers between devices: 5.03 us -> 0.01 us  [gather_rows(): block = lax.all_to_all(copies, 'sz', 0, 0, tiled=True)]
    all_to_all x1, starting transfers between devices: 6.9 us -> 11.3 us  [local(): received = lax.all_to_all(packed, 'sz', 0, 0, tiled=True)]
    convert_element_type x0 -> x1, local copies, waits for them, and re-layouts: none -> 4.12 us  [attend(): keep = keep.reshape(rows, padded).astype(jnp.float32)]
    convert_element_type x0 -> x1, other arithmetic: none -> 2.28 us  [attend(): keep = keep.reshape(rows, padded).astype(jnp.float32)]
  transfers between devices with their start and end apart: 2 -> 2, of which waited for: 2 -> 1; matrix products, arithmetic and copies ran while one was open for 4% -> 10% of each run, Pallas kernels for 0% -> 0%
where the time goes in v6:
time: 152 us
  blocking collectives  69.7 us (46%)
  starting transfers between devices  27.1 us (18%)
  Pallas kernels  16.8 us (11%)
  local copies, waits for them, and re-layouts  15.4 us (10%)
  waiting for transfers between devices  12.7 us (8%)
  other arithmetic  9.48 us (6%)
    all_gather x2, blocking collectives, gather_rows(): return lax.all_gather(block, 'sx', axis=0, tiled=True)  22.1 us
    all_to_all x1, blocking collectives, local(): blocks = lax.all_to_all(terms, 'tp', 0, 0, tiled=True)  20.2 us
    all_to_all x1, blocking collectives, gather_rows(): block = lax.all_to_all(copies, 'sz', 0, 0, tiled=True)  18 us
    pallas_call x1, Pallas kernels, attend(): pl.pallas_call(functools.partial(attend_kernel, scale), grid=(kv * hpk,),...  16.8 us
    all_to_all x1, starting transfers between devices, gather_rows(): block = lax.all_to_all(copies, 'sz', 0, 0, tiled=True)  15.7 us
    all_to_all x1, waiting for transfers between devices, local(): received = lax.all_to_all(packed, 'sz', 0, 0, tiled=True)  12.7 us
    all_to_all x1, starting transfers between devices, local(): received = lax.all_to_all(packed, 'sz', 0, 0, tiled=True)  11.3 us
    all_to_all x1, blocking collectives, local(): lax.all_to_all(packed, 'sx', 0, 0, tiled=True).astype(jnp.float32)  9.39 us
  transfers between devices with their start and end apart: 2, of which 1 were waited for; matrix products, arithmetic and copies ran while one was open for 10% of the time, Pallas kernels for 0%

profile of v6, /device:TPU:1, one launch (start us, length us, event | category | flops | bytes accessed | tf_op | source)
XLA Modules:
  0.0 151.8 jit_solution(3363803245080686417)
XLA Ops:
  0.0 1.4 broadcast_in_dim.23
  1.4 15.7 %all-to-all-start = ((bf16[16,1,4,1024]{3,2,1,0:T(4,128)(2,1)}), bf16[16,1,4,1024]{3,2,1,0:T(4,128)(2,1)S(1)}, u32[]{:S(2)}, u32[]{:S(2)}) async-start(bf16[16,1,4,1024]{3,2,1,0:T(4,128)(2,1)} %broadcast_in_dim.23), calls=%async_computation | async-start | bytes 262144 | tf_op jit(solution)/shard_map/all_to_all | solution.py:23
  17.2 0.7 iota_compare_fusion.2
  17.9 0.8 select_reduce_fusion
  18.8 0.8 broadcast_reduce_fusion.1
  19.6 0.7 broadcast_multiply_fusion
  20.2 0.7 broadcast_compare_fusion
  21.3 0.7 iota_compare_fusion.1
  22.1 0.1 and.62
  22.2 0.3 and.63
  22.5 0.2 and.66
  22.7 0.2 and.67
  22.9 0.7 sub.34
  23.7 0.1 and_and_fusion
  23.9 0.2 broadcast_in_dim.27
  24.2 0.4 broadcast_in_dim.24
  24.5 0.8 pad_add_fusion
  25.4 2.3 %pad_convert_fusion = f32[64,4,2688]{2,1,0:T(4,128)} fusion(pred[64,4,2564]{2,1,0:T(4,128)(4,1)S(1)} %pad_add_fusion), kind=kLoop, calls=%fused_computation.1 | loop fusion | flops 688128 | bytes 3408896 | tf_op jit(solution)/shard_map/convert_element_type | solution.py:54
  27.8 4.1 %reshape.365.keep_ref = f32[256,2688]{1,0:T(8,128)} reshape(f32[64,4,2688]{2,1,0:T(4,128)} %pad_convert_fusion) | data formatting | bytes 5505024 | tf_op jit(solution)/shard_map/convert_element_type | solution.py:54
  32.0 11.6 %all-gather = bf16[64,1,4,1024]{3,2,1,0:T(4,128)(2,1)S(1)} all-gather(bf16[16,1,4,1024]{3,2,1,0:T(4,128)(2,1)S(1)} %all-to-all-done), channel_id=2, replica_groups=mesh['sx'=4,'sz'=16,'tp'=8] {'sx'}, dimensions={0}, use_global_device_ids=true | all-gather | bytes 655360 | tf_op jit(solution)/shard_map/all_gather | solution.py:25
  43.7 0.2 reshape.368
  44.0 0.4 copy.39
  44.4 16.8 %shard_map.136 = (f32[2048,128]{1,0:T(8,128)S(1)}, f32[2048,128]{1,0:T(8,128)S(1)}, f32[2048,128]{1,0:T(8,128)S(1)}) custom-call(bf16[2048,128]{1,0:T(8,128)(2,1)S(1)} %bitcast.64, bf16[1,2688,128]{2,1,0:T(8,128)(2,1)S(1)} %fusion.9.k_ref, bf16[1,2688,128]{2,1,0:T(8,128)(2,1)S(1)} %fusion.12.v_ref, f32[256,2688]{1,0:T(8,128)} %reshape.365.keep_ref), custom_call_target="tpu_custom_call" | custom-call | tf_op jit(solution)/shard_map/pallas_call | solution.py:59
  61.2 0.6 slice_reduce_fusion
  61.8 0.3 reshape_squeeze.6
  62.0 0.1 copy.44
  62.2 0.1 copy.42
  62.3 0.6 copy.57
  62.9 0.2 reshape_reshape.6
  63.1 0.3 reshape_squeeze.7
  63.4 0.1 copy.46
  64.0 0.3 mul.91
  64.3 0.2 mul.92
  64.7 0.2 concatenate.35
  64.9 9.4 %all_to_all.29 = bf16[4,16,1,4160]{3,1,2,0:T(8,128)(2,1)S(1)} all-to-all(bf16[4,16,1,4160]{3,1,2,0:T(8,128)(2,1)S(1)} %bitcast.69), channel_id=1, replica_groups=mesh['sx'=4,'sz'=16,'tp'=8] {'sx'}, dimensions={0} | all-to-all | bytes 1064960 | tf_op jit(solution)/shard_map/all_to_all | solution.py:180
  74.5 0.3 mul.96
  74.8 0.2 mul.97
  75.1 0.3 reshape.363
  75.4 1.8 %concatenate.36 = f32[16,1,4160]{2,1,0:T(1,128)} concatenate(f32[16,1,4096]{2,1,0:T(1,128)S(1)} %reshape.363, f32[16,1,32]{2,1,0:T(1,128)S(1)} %bitcast.78, f32[16,1,32]{2,1,0:T(1,128)S(1)} %bitcast.79), dimensions={2} | concatenate | bytes 532480 | tf_op jit(solution)/shard_map/concatenate | solution.py:182
  77.2 11.3 %all-to-all-start.2 = ((f32[16,1,4160]{2,1,0:T(1,128)}), f32[16,1,4160]{2,1,0:T(1,128)S(1)}, u32[]{:S(2)}, u32[]{:S(2)}) async-start(f32[16,1,4160]{2,1,0:T(1,128)} %concatenate.36), calls=%async_computation.2 | async-start | bytes 540672 | tf_op jit(solution)/shard_map/all_to_all | solution.py:183
  88.5 0.2 convert_reduce_fusion
  88.7 12.7 %all-to-all-done.2 = f32[16,1,4160]{2,1,0:T(1,128)S(1)} async-done(((f32[16,1,4160]{2,1,0:T(1,128)}), f32[16,1,4160]{2,1,0:T(1,128)S(1)}, u32[]{:S(2)}, u32[]{:S(2)}) %all-to-all-start.2) | async-done | bytes 266272 | tf_op jit(solution)/shard_map/all_to_all | solution.py:183
  101.8 0.3 fusion.14
  102.2 18.0 %all_to_all.30 = bf16[16,4,1024]{2,1,0:T(4,128)(2,1)S(1)} all-to-all(bf16[16,4,1024]{2,1,0:T(4,128)(2,1)S(1)} %broadcast_in_dim.28), channel_id=1, replica_groups=mesh['sx'=4,'sz'=16,'tp'=8] {'sz'}, dimensions={0} | all-to-all | bytes 262144 | tf_op jit(solution)/shard_map/all_to_all | solution.py:23
  120.2 10.5 %all_gather.7 = bf16[256,1024]{1,0:T(8,128)(2,1)S(1)} all-gather(bf16[64,1024]{1,0:T(8,128)(2,1)S(1)} %reshape.364), channel_id=1, replica_groups=mesh['sx'=4,'sz'=16,'tp'=8] {'sx'}, dimensions={0}, use_global_device_ids=true | all-gather | bytes 655360 | tf_op jit(solution)/shard_map/all_gather | solution.py:25
  130.7 0.3 fusion.20
  131.0 20.2 %all_to_all.31 = f32[8,32,128]{2,1,0:T(8,128)S(1)} all-to-all(f32[8,32,128]{2,1,0:T(8,128)S(1)} %bitcast.73), channel_id=1, replica_groups=mesh['sx'=4,'sz'=16,'tp'=8] {'tp'}, dimensions={0} | all-to-all | bytes 262144 | tf_op jit(solution)/shard_map/all_to_all | solution.py:195
  151.2 0.6 reduce_sum.62
  (56 shorter events, 2.4 us)
Async XLA Ops:
  0.0 130.7 %copy-start = (bf16[1024,128]{1,0:T(8,128)(2,1)S(1)}, bf16[1024,128]{1,0:T(8,128)(2,1)}, u32[]{:S(2)}) copy-start(bf16[1024,128]{1,0:T(8,128)(2,1)} %param.21) | copy-start | bytes 786436
  1.4 30.6 %all-to-all-start = ((bf16[16,1,4,1024]{3,2,1,0:T(4,128)(2,1)}), bf16[16,1,4,1024]{3,2,1,0:T(4,128)(2,1)S(1)}, u32[]{:S(2)}, u32[]{:S(2)}) async-start(bf16[16,1,4,1024]{3,2,1,0:T(4,128)(2,1)} %broadcast_in_dim.23), calls=%async_computation | async-start | bytes 262144 | tf_op jit(solution)/shard_map/all_to_all | solution.py:23
  25.4 2.3 %copy-start.1 = (bf16[8,192,128]{2,1,0:T(8,128)(2,1)S(1)}, bf16[8,192,128]{2,1,0:T(8,128)(2,1)}, u32[]{:S(2)}) copy-start(bf16[8,192,128]{2,1,0:T(8,128)(2,1)} %param.17) | copy-start | bytes 1179652
  25.4 2.3 %copy-start.3 = (bf16[16,64,128]{2,1,0:T(8,128)(2,1)S(1)}, bf16[16,64,128]{2,1,0:T(8,128)(2,1)}, u32[]{:S(2)}) copy-start(bf16[16,64,128]{2,1,0:T(8,128)(2,1)} %param.19) | copy-start | bytes 786436
  25.4 2.3 %copy-start.6 = (bf16[1,4,128]{2,1,0:T(4,128)(2,1)S(1)}, bf16[1,4,128]{2,1,0:T(4,128)(2,1)}, u32[]{:S(2)}) copy-start(bf16[1,4,128]{2,1,0:T(4,128)(2,1)} %param.15) | copy-start | bytes 3076
  27.8 4.2 %copy-start.2 = (bf16[8,192,128]{2,1,0:T(8,128)(2,1)S(1)}, bf16[8,192,128]{2,1,0:T(8,128)(2,1)}, u32[]{:S(2)}) copy-start(bf16[8,192,128]{2,1,0:T(8,128)(2,1)} %param.18) | copy-start | bytes 1179652
  27.8 4.2 %copy-start.4 = (bf16[16,64,128]{2,1,0:T(8,128)(2,1)S(1)}, bf16[16,64,128]{2,1,0:T(8,128)(2,1)}, u32[]{:S(2)}) copy-start(bf16[16,64,128]{2,1,0:T(8,128)(2,1)} %param.20) | copy-start | bytes 786436
  27.8 4.1 %copy-start.7 = (bf16[1,4,128]{2,1,0:T(4,128)(2,1)S(1)}, bf16[1,4,128]{2,1,0:T(4,128)(2,1)}, u32[]{:S(2)}) copy-start(bf16[1,4,128]{2,1,0:T(4,128)(2,1)} %param.16) | copy-start | bytes 3076
  75.1 13.4 %copy-start.5 = (s32[64,4]{0,1:T(4,128)S(1)}, s32[64,4]{0,1:T(4,128)}, u32[]{:S(2)}) copy-start(s32[64,4]{0,1:T(4,128)} %param.27) | copy-start | bytes 3076
  77.2 24.2 %all-to-all-start.2 = ((f32[16,1,4160]{2,1,0:T(1,128)}), f32[16,1,4160]{2,1,0:T(1,128)S(1)}, u32[]{:S(2)}, u32[]{:S(2)}) async-start(f32[16,1,4160]{2,1,0:T(1,128)} %concatenate.36), calls=%async_computation.2 | async-start | bytes 540672 | tf_op jit(solution)/shard_map/all_to_all | solution.py:183

commit v7 on v6

--- a/solution.py
+++ b/solution.py
@@ -33,7 +33,7 @@
     keep = keep_ref[...] > 0.5
     masked = jnp.where(keep, scores, NEG)
     peak = jnp.max(masked, axis=1, keepdims=True)
-    weights = jnp.where(keep, jnp.exp(masked - peak), 0.0)
+    weights = jnp.exp(masked - jnp.maximum(peak, 0.5 * NEG))
     total = jnp.sum(weights, axis=1, keepdims=True)
     o_ref[...] = jnp.dot(
         weights.astype(jnp.bfloat16), v_ref[0], preferred_element_type=jnp.float32
@@ -51,7 +51,7 @@
     keys_t = jnp.pad(keys, pad).transpose(1, 0, 2)
     values_t = jnp.pad(values, pad).transpose(1, 0, 2)
     keep = jnp.pad(key_mask, ((0, 0), (0, 0), (0, padded - n_keys)))
-    keep = keep.reshape(rows, padded).astype(jnp.float32)
+    keep = keep.reshape(rows, padded).astype(jnp.bfloat16)
     q_rows = query_all.transpose(2, 3, 0, 1, 4).reshape(kv * hpk * rows, dim)
     row_block = pl.BlockSpec((rows, dim), lambda i: (i, 0))
     kv_block = pl.BlockSpec((1, padded, dim), lambda i: (i // hpk, 0, 0))

time: 152 us -> 146 us (0.961)
  local copies, waits for them, and re-layouts: 15.4 us -> 12.8 us
  Pallas kernels: 16.8 us -> 14.4 us
    convert_element_type x1, local copies, waits for them, and re-layouts: 4.12 us -> 1.26 us  [attend(): keep = keep.reshape(rows, padded).astype(jnp.bfloat16)]
    pallas_call x1, Pallas kernels: 16.8 us -> 14.4 us  [attend(): pl.pallas_call(functools.partial(attend_kernel, scale), grid=(kv * hpk,),...]
  transfers between devices with their start and end apart: 2 -> 2, of which waited for: 1 -> 2; matrix products, arithmetic and copies ran while one was open for 10% -> 7% of each run, Pallas kernels for 0% -> 0%
where the time goes in v7:
time: 146 us; the launch traced here: 145 us
  blocking collectives  69.1 us (47%)
  starting transfers between devices  26.4 us (18%)
  Pallas kernels  14.4 us (10%)
  waiting for transfers between devices  14 us (10%)
  local copies, waits for them, and re-layouts  12.8 us (9%)
  other arithmetic  7.97 us (5%)
    all_gather x2, blocking collectives, gather_rows(): return lax.all_gather(block, 'sx', axis=0, tiled=True)  20.7 us
    all_to_all x1, blocking collectives, local(): blocks = lax.all_to_all(terms, 'tp', 0, 0, tiled=True)  20.2 us
    all_to_all x1, blocking collectives, gather_rows(): block = lax.all_to_all(copies, 'sz', 0, 0, tiled=True)  18 us
    all_to_all x1, starting transfers between devices, gather_rows(): block = lax.all_to_all(copies, 'sz', 0, 0, tiled=True)  15.7 us
    pallas_call x1, Pallas kernels, attend(): pl.pallas_call(functools.partial(attend_kernel, scale), grid=(kv * hpk,),...  14.4 us
    all_to_all x1, waiting for transfers between devices, local(): received = lax.all_to_all(packed, 'sz', 0, 0, tiled=True)  12.7 us
    all_to_all x1, starting transfers between devices, local(): received = lax.all_to_all(packed, 'sz', 0, 0, tiled=True)  10.6 us
    all_to_all x1, blocking collectives, local(): lax.all_to_all(packed, 'sx', 0, 0, tiled=True).astype(jnp.float32)  10.2 us
  transfers between devices with their start and end apart: 2, of which 2 were waited for; matrix products, arithmetic and copies ran while one was open for 7% of the time, Pallas kernels for 0%

profile of v7, /device:TPU:1, one launch (start us, length us, event | category | flops | bytes accessed | tf_op | source)
XLA Modules:
  0.0 145.3 jit_solution(5622313233351690054)
XLA Ops:
  0.0 1.4 broadcast_in_dim.23
  1.4 15.7 %all-to-all-start = ((bf16[16,1,4,1024]{3,2,1,0:T(4,128)(2,1)}), bf16[16,1,4,1024]{3,2,1,0:T(4,128)(2,1)S(1)}, u32[]{:S(2)}, u32[]{:S(2)}) async-start(bf16[16,1,4,1024]{3,2,1,0:T(4,128)(2,1)} %broadcast_in_dim.23), calls=%async_computation | async-start | bytes 262144 | tf_op jit(solution)/shard_map/all_to_all | solution.py:23
  17.2 0.7 iota_compare_fusion.2
  17.9 0.8 select_reduce_fusion
  18.8 0.8 broadcast_reduce_fusion.1
  19.6 0.7 broadcast_multiply_fusion
  20.2 0.7 broadcast_compare_fusion
  21.3 0.7 iota_compare_fusion.1
  22.1 0.1 and.62
  22.2 0.3 and.63
  22.5 0.2 and.66
  22.7 0.2 and.67
  22.9 0.7 sub.34
  23.7 0.1 and_and_fusion
  23.9 0.2 broadcast_in_dim.27
  24.2 0.4 broadcast_in_dim.24
  24.5 0.8 pad_add_fusion
  25.4 0.8 pad_convert_fusion
  26.2 0.2 copy-done.1
  26.5 1.3 reshape.365.keep_ref
  27.9 1.3 all-to-all-done
  29.2 10.2 %all-gather = bf16[64,1,4,1024]{3,2,1,0:T(4,128)(2,1)S(1)} all-gather(bf16[16,1,4,1024]{3,2,1,0:T(4,128)(2,1)S(1)} %all-to-all-done), channel_id=2, replica_groups=mesh['sx'=4,'sz'=16,'tp'=8] {'sx'}, dimensions={0}, use_global_device_ids=true | all-gather | bytes 655360 | tf_op jit(solution)/shard_map/all_gather | solution.py:25
  39.4 0.2 reshape.368
  39.7 0.4 copy.39
  40.1 14.4 %shard_map.136 = (f32[2048,128]{1,0:T(8,128)S(1)}, f32[2048,128]{1,0:T(8,128)S(1)}, f32[2048,128]{1,0:T(8,128)S(1)}) custom-call(bf16[2048,128]{1,0:T(8,128)(2,1)S(1)} %bitcast.64, bf16[1,2688,128]{2,1,0:T(8,128)(2,1)S(1)} %fusion.9.k_ref, bf16[1,2688,128]{2,1,0:T(8,128)(2,1)S(1)} %fusion.12.v_ref, bf16[256,2688]{1,0:T(8,128)(2,1)} %reshape.365.keep_ref), custom_call_target="tpu_custom_call" | custom-call | tf_op jit(solution)/shard_map/pallas_call | solution.py:59
  54.5 0.6 slice_reduce_fusion
  55.1 0.3 reshape_squeeze.6
  55.5 0.1 copy.42
  55.6 0.6 copy.57
  56.2 0.2 reshape_reshape.6
  56.4 0.3 reshape_squeeze.7
  57.3 0.3 mul.91
  57.7 0.2 mul.92
  58.0 0.2 concatenate.35
  58.2 10.2 %all_to_all.29 = bf16[4,16,1,4160]{3,1,2,0:T(8,128)(2,1)S(1)} all-to-all(bf16[4,16,1,4160]{3,1,2,0:T(8,128)(2,1)S(1)} %bitcast.69), channel_id=1, replica_groups=mesh['sx'=4,'sz'=16,'tp'=8] {'sx'}, dimensions={0} | all-to-all | bytes 1064960 | tf_op jit(solution)/shard_map/all_to_all | solution.py:180
  68.6 0.3 mul.96
  68.9 0.2 mul.97
  69.3 0.3 reshape.363
  69.5 1.8 %concatenate.36 = f32[16,1,4160]{2,1,0:T(1,128)} concatenate(f32[16,1,4096]{2,1,0:T(1,128)S(1)} %reshape.363, f32[16,1,32]{2,1,0:T(1,128)S(1)} %bitcast.78, f32[16,1,32]{2,1,0:T(1,128)S(1)} %bitcast.79), dimensions={2} | concatenate | bytes 532480 | tf_op jit(solution)/shard_map/concatenate | solution.py:182
  71.3 10.6 %all-to-all-start.2 = ((f32[16,1,4160]{2,1,0:T(1,128)}), f32[16,1,4160]{2,1,0:T(1,128)S(1)}, u32[]{:S(2)}, u32[]{:S(2)}) async-start(f32[16,1,4160]{2,1,0:T(1,128)} %concatenate.36), calls=%async_computation.2 | async-start | bytes 540672 | tf_op jit(solution)/shard_map/all_to_all | solution.py:183
  82.0 0.2 convert_reduce_fusion
  82.2 12.7 %all-to-all-done.2 = f32[16,1,4160]{2,1,0:T(1,128)S(1)} async-done(((f32[16,1,4160]{2,1,0:T(1,128)}), f32[16,1,4160]{2,1,0:T(1,128)S(1)}, u32[]{:S(2)}, u32[]{:S(2)}) %all-to-all-start.2) | async-done | bytes 266272 | tf_op jit(solution)/shard_map/all_to_all | solution.py:183
  95.3 0.3 fusion.14
  95.7 18.0 %all_to_all.30 = bf16[16,4,1024]{2,1,0:T(4,128)(2,1)S(1)} all-to-all(bf16[16,4,1024]{2,1,0:T(4,128)(2,1)S(1)} %broadcast_in_dim.28), channel_id=1, replica_groups=mesh['sx'=4,'sz'=16,'tp'=8] {'sz'}, dimensions={0} | all-to-all | bytes 262144 | tf_op jit(solution)/shard_map/all_to_all | solution.py:23
  113.7 10.5 %all_gather.7 = bf16[256,1024]{1,0:T(8,128)(2,1)S(1)} all-gather(bf16[64,1024]{1,0:T(8,128)(2,1)S(1)} %reshape.364), channel_id=1, replica_groups=mesh['sx'=4,'sz'=16,'tp'=8] {'sx'}, dimensions={0}, use_global_device_ids=true | all-gather | bytes 655360 | tf_op jit(solution)/shard_map/all_gather | solution.py:25
  124.2 0.3 fusion.20
  124.5 20.2 %all_to_all.31 = f32[8,32,128]{2,1,0:T(8,128)S(1)} all-to-all(f32[8,32,128]{2,1,0:T(8,128)S(1)} %bitcast.73), channel_id=1, replica_groups=mesh['sx'=4,'sz'=16,'tp'=8] {'tp'}, dimensions={0} | all-to-all | bytes 262144 | tf_op jit(solution)/shard_map/all_to_all | solution.py:195
  144.7 0.6 reduce_sum.62
  (56 shorter events, 2.7 us)
Async XLA Ops:
  0.0 124.2 %copy-start = (bf16[1024,128]{1,0:T(8,128)(2,1)S(1)}, bf16[1024,128]{1,0:T(8,128)(2,1)}, u32[]{:S(2)}) copy-start(bf16[1024,128]{1,0:T(8,128)(2,1)} %param.21) | copy-start | bytes 786436
  1.4 27.7 %all-to-all-start = ((bf16[16,1,4,1024]{3,2,1,0:T(4,128)(2,1)}), bf16[16,1,4,1024]{3,2,1,0:T(4,128)(2,1)S(1)}, u32[]{:S(2)}, u32[]{:S(2)}) async-start(bf16[16,1,4,1024]{3,2,1,0:T(4,128)(2,1)} %broadcast_in_dim.23), calls=%async_computation | async-start | bytes 262144 | tf_op jit(solution)/shard_map/all_to_all | solution.py:23
  25.4 1.0 copy-start.1
  25.4 1.1 copy-start.3
  25.4 1.1 copy-start.6
  26.5 1.3 copy-start.2
  26.5 1.3 copy-start.4
  26.5 1.3 copy-start.7
  69.3 12.7 %copy-start.5 = (s32[64,4]{0,1:T(4,128)S(1)}, s32[64,4]{0,1:T(4,128)}, u32[]{:S(2)}) copy-start(s32[64,4]{0,1:T(4,128)} %param.27) | copy-start | bytes 3076
  71.3 23.5 %all-to-all-start.2 = ((f32[16,1,4160]{2,1,0:T(1,128)}), f32[16,1,4160]{2,1,0:T(1,128)S(1)}, u32[]{:S(2)}, u32[]{:S(2)}) async-start(f32[16,1,4160]{2,1,0:T(1,128)} %concatenate.36), calls=%async_computation.2 | async-start | bytes 540672 | tf_op jit(solution)/shard_map/all_to_all | solution.py:183

commit v8 on v7

--- a/solution.py
+++ b/solution.py
@@ -46,27 +46,31 @@
     requests, new, kv, hpk, dim = query_all.shape
     n_keys = keys.shape[0]
     padded = -(-n_keys // 128) * 128
-    rows = requests * new
+    rows = requests * new * hpk
+    block = 256 if rows % 256 == 0 else rows
+    steps = rows // block
     pad = ((0, padded - n_keys), (0, 0), (0, 0))
     keys_t = jnp.pad(keys, pad).transpose(1, 0, 2)
     values_t = jnp.pad(values, pad).transpose(1, 0, 2)
-    keep = jnp.pad(key_mask, ((0, 0), (0, 0), (0, padded - n_keys)))
-    keep = keep.reshape(rows, padded).astype(jnp.bfloat16)
-    q_rows = query_all.transpose(2, 3, 0, 1, 4).reshape(kv * hpk * rows, dim)
-    row_block = pl.BlockSpec((rows, dim), lambda i: (i, 0))
-    kv_block = pl.BlockSpec((1, padded, dim), lambda i: (i // hpk, 0, 0))
-    stat = jax.ShapeDtypeStruct((kv * hpk * rows, dim), jnp.float32)
+    keep = jnp.pad(key_mask, ((0, 0), (0, 0), (0, padded - n_keys))).astype(jnp.bfloat16)
+    keep = jnp.broadcast_to(keep[:, :, None, :], (requests, new, hpk, padded))
+    keep = keep.reshape(rows, padded)
+    q_rows = query_all.transpose(2, 0, 1, 3, 4).reshape(kv * rows, dim)
+    row_block = pl.BlockSpec((block, dim), lambda i: (i, 0))
+    kv_block = pl.BlockSpec((1, padded, dim), lambda i: (i // steps, 0, 0))
+    keep_block = pl.BlockSpec((block, padded), lambda i: (i % steps, 0))
+    stat = jax.ShapeDtypeStruct((kv * rows, dim), jnp.float32)
     out, peak, total = pl.pallas_call(
         functools.partial(attend_kernel, scale),
-        grid=(kv * hpk,),
-        in_specs=[row_block, kv_block, kv_block, pl.BlockSpec((rows, padded), lambda i: (0, 0))],
+        grid=(kv * steps,),
+        in_specs=[row_block, kv_block, kv_block, keep_block],
         out_specs=[row_block, row_block, row_block],
         out_shape=[stat, stat, stat],
         compiler_params=pltpu.CompilerParams(vmem_limit_bytes=48 * 1024 * 1024),
     )(q_rows, keys_t, values_t, keep)
-    out = out.reshape(kv, hpk, requests, new, dim).transpose(2, 3, 0, 1, 4)
-    peak = peak[:, 0].reshape(kv, hpk, requests, new).transpose(2, 3, 0, 1)
-    total = total[:, 0].reshape(kv, hpk, requests, new).transpose(2, 3, 0, 1)
+    out = out.reshape(kv, requests, new, hpk, dim).transpose(1, 2, 0, 3, 4)
+    peak = peak[:, 0].reshape(kv, requests, new, hpk).transpose(1, 2, 0, 3)
+    total = total[:, 0].reshape(kv, requests, new, hpk).transpose(1, 2, 0, 3)
     return out, peak, total
 
 

time: 146 us -> 149 us (1.021)
  local copies, waits for them, and re-layouts: 12.8 us -> 15 us
  starting transfers between devices: 26.4 us -> 24.8 us
    broadcast_in_dim x0 -> x1, local copies, waits for them, and re-layouts: none -> 4.83 us  [attend(): keep = jnp.broadcast_to(keep[:, :, None, :], (requests, new, hpk, padded))]
    all_to_all x1, starting transfers between devices: 10.6 us -> 9.1 us  [local(): received = lax.all_to_all(packed, 'sz', 0, 0, tiled=True)]
  transfers between devices with their start and end apart: 2 -> 2, of which waited for: 2 -> 2; matrix products, arithmetic and copies ran while one was open for 7% -> 6% of each run, Pallas kernels for 0% -> 0%
where the time goes in v8:
time: 149 us; the launch traced here: 148 us
  blocking collectives  70 us (47%)
  starting transfers between devices  24.8 us (17%)
  waiting for transfers between devices  15.3 us (10%)
  local copies, waits for them, and re-layouts  15 us (10%)
  Pallas kernels  14.4 us (10%)
  other arithmetic  7.98 us (5%)
    all_gather x2, blocking collectives, gather_rows(): return lax.all_gather(block, 'sx', axis=0, tiled=True)  21.3 us
    all_to_all x1, blocking collectives, local(): blocks = lax.all_to_all(terms, 'tp', 0, 0, tiled=True)  20.2 us
    all_to_all x1, blocking collectives, gather_rows(): block = lax.all_to_all(copies, 'sz', 0, 0, tiled=True)  18 us
    all_to_all x1, starting transfers between devices, gather_rows(): block = lax.all_to_all(copies, 'sz', 0, 0, tiled=True)  15.7 us
    pallas_call x1, Pallas kernels, attend(): pl.pallas_call(functools.partial(attend_kernel, scale), grid=(kv * steps,...  14.4 us
    all_to_all x1, waiting for transfers between devices, local(): received = lax.all_to_all(packed, 'sz', 0, 0, tiled=True)  12.6 us
    all_to_all x1, blocking collectives, local(): lax.all_to_all(packed, 'sx', 0, 0, tiled=True).astype(jnp.float32)  10.6 us
    all_to_all x1, starting transfers between devices, local(): received = lax.all_to_all(packed, 'sz', 0, 0, tiled=True)  9.1 us
  transfers between devices with their start and end apart: 2, of which 2 were waited for; matrix products, arithmetic and copies ran while one was open for 6% of the time, Pallas kernels for 0%

profile of v8, /device:TPU:1, one launch (start us, length us, event | category | flops | bytes accessed | tf_op | source)
XLA Modules:
  0.0 148.1 jit_solution(12885938211903239390)
XLA Ops:
  0.0 1.4 broadcast_in_dim.25
  1.4 15.7 %all-to-all-start = ((bf16[16,1,4,1024]{3,2,1,0:T(4,128)(2,1)}), bf16[16,1,4,1024]{3,2,1,0:T(4,128)(2,1)S(1)}, u32[]{:S(2)}, u32[]{:S(2)}) async-start(bf16[16,1,4,1024]{3,2,1,0:T(4,128)(2,1)} %broadcast_in_dim.25), calls=%async_computation | async-start | bytes 262144 | tf_op jit(solution)/shard_map/all_to_all | solution.py:23
  17.2 0.7 iota_compare_fusion.2
  17.9 0.8 select_reduce_fusion
  18.8 0.8 broadcast_reduce_fusion.1
  19.5 0.7 broadcast_multiply_fusion
  20.2 0.7 broadcast_compare_fusion
  21.0 0.1 copy.17
  21.3 0.7 iota_compare_fusion.1
  22.1 0.1 and.62
  22.2 0.3 and.63
  22.5 0.2 and.66
  22.7 0.2 and.67
  22.9 0.7 sub.34
  23.7 0.1 and_and_fusion
  23.8 0.1 compare_and_fusion
  23.9 0.2 broadcast_in_dim.29
  24.2 0.4 broadcast_in_dim.26
  24.6 0.8 pad_add_fusion
  25.7 0.8 pad_convert_fusion
  26.5 2.7 %all-to-all-done = bf16[16,1,4,1024]{3,2,1,0:T(4,128)(2,1)S(1)} async-done(((bf16[16,1,4,1024]{3,2,1,0:T(4,128)(2,1)}), bf16[16,1,4,1024]{3,2,1,0:T(4,128)(2,1)S(1)}, u32[]{:S(2)}, u32[]{:S(2)}) %all-to-all-start) | async-done | bytes 131104 | tf_op jit(solution)/shard_map/all_to_all | solution.py:23
  29.1 11.0 %all-gather = bf16[64,1,4,1024]{3,2,1,0:T(4,128)(2,1)} all-gather(bf16[16,1,4,1024]{3,2,1,0:T(4,128)(2,1)S(1)} %all-to-all-done), channel_id=2, replica_groups=mesh['sx'=4,'sz'=16,'tp'=8] {'sx'}, dimensions={0}, use_global_device_ids=true | all-gather | bytes 655360 | tf_op jit(solution)/shard_map/all_gather | solution.py:25
  40.1 1.2 reshape_transpose_reshape.3.q_ref
  41.3 4.8 %broadcast_in_dim.30 = bf16[64,4,8,2688]{3,2,1,0:T(8,128)(2,1)} broadcast(bf16[64,4,2688]{2,1,0:T(4,128)(2,1)S(1)} %pad_convert_fusion), dimensions={0,1,3} | broadcast | bytes 12386304 | tf_op jit(solution)/shard_map/broadcast_in_dim | solution.py:56
  46.2 14.4 %shard_map.136 = (f32[2048,128]{1,0:T(8,128)S(1)}, f32[2048,128]{1,0:T(8,128)S(1)}, f32[2048,128]{1,0:T(8,128)S(1)}) custom-call(bf16[2048,128]{1,0:T(8,128)(2,1)S(1)} %reshape_transpose_reshape.3.q_ref, bf16[1,2688,128]{2,1,0:T(8,128)(2,1)S(1)} %fusion.9.k_ref, bf16[1,2688,128]{2,1,0:T(8,128)(2,1)S(1)} %fusion.12.v_ref, bf16[2048,2688]{1,0:T(8,128)(2,1)} %bitcast.39), custom_call_target="tpu_custom_call" | custom-call | tf_op jit(solution)/shard_map/pallas_call | solution.py:63
  60.6 0.6 slice_reduce_fusion
  61.3 0.2 reshape_reshape_transpose_reshape.3
  61.6 0.3 mul.91
  62.0 0.2 mul.92
  62.2 0.1 fusion.13
  62.3 0.2 concatenate.35
  62.5 10.6 %all_to_all.29 = bf16[4,16,1,4160]{3,1,2,0:T(8,128)(2,1)S(1)} all-to-all(bf16[4,16,1,4160]{3,1,2,0:T(8,128)(2,1)S(1)} %concatenate.35), channel_id=1, replica_groups=mesh['sx'=4,'sz'=16,'tp'=8] {'sx'}, dimensions={0} | all-to-all | bytes 1064960 | tf_op jit(solution)/shard_map/all_to_all | solution.py:184
  73.3 0.3 mul.96
  73.6 0.2 mul.97
  73.8 0.1 fusion.6
  73.9 0.3 reshape.342
  74.2 1.8 %concatenate.36 = f32[16,1,4160]{2,1,0:T(1,128)} concatenate(f32[16,1,4096]{2,1,0:T(1,128)S(1)} %reshape.342, f32[16,1,32]{2,1,0:T(1,128)S(1)} %bitcast.46, f32[16,1,32]{2,1,0:T(1,128)S(1)} %bitcast.47), dimensions={2} | concatenate | bytes 532480 | tf_op jit(solution)/shard_map/concatenate | solution.py:186
  76.0 9.1 %all-to-all-start.2 = ((f32[16,1,4160]{2,1,0:T(1,128)}), f32[16,1,4160]{2,1,0:T(1,128)S(1)}, u32[]{:S(2)}, u32[]{:S(2)}) async-start(f32[16,1,4160]{2,1,0:T(1,128)} %concatenate.36), calls=%async_computation.2 | async-start | bytes 540672 | tf_op jit(solution)/shard_map/all_to_all | solution.py:187
  85.1 0.2 convert_reduce_fusion
  85.3 12.6 %all-to-all-done.2 = f32[16,1,4160]{2,1,0:T(1,128)S(1)} async-done(((f32[16,1,4160]{2,1,0:T(1,128)}), f32[16,1,4160]{2,1,0:T(1,128)S(1)}, u32[]{:S(2)}, u32[]{:S(2)}) %all-to-all-start.2) | async-done | bytes 266272 | tf_op jit(solution)/shard_map/all_to_all | solution.py:187
  97.9 0.1 fusion.18
  98.2 0.1 mul.101
  98.3 0.3 fusion.14
  98.7 18.0 %all_to_all.30 = bf16[16,4,1024]{2,1,0:T(4,128)(2,1)S(1)} all-to-all(bf16[16,4,1024]{2,1,0:T(4,128)(2,1)S(1)} %broadcast_in_dim.31), channel_id=1, replica_groups=mesh['sx'=4,'sz'=16,'tp'=8] {'sz'}, dimensions={0} | all-to-all | bytes 262144 | tf_op jit(solution)/shard_map/all_to_all | solution.py:23
  116.7 10.4 %all_gather.7 = bf16[256,1024]{1,0:T(8,128)(2,1)S(1)} all-gather(bf16[64,1024]{1,0:T(8,128)(2,1)S(1)} %reshape.343), channel_id=1, replica_groups=mesh['sx'=4,'sz'=16,'tp'=8] {'sx'}, dimensions={0}, use_global_device_ids=true | all-gather | bytes 655360 | tf_op jit(solution)/shard_map/all_gather | solution.py:25
  127.1 0.3 fusion.19
  127.4 20.2 %all_to_all.31 = f32[8,32,128]{2,1,0:T(8,128)S(1)} all-to-all(f32[8,32,128]{2,1,0:T(8,128)S(1)} %bitcast.41), channel_id=1, replica_groups=mesh['sx'=4,'sz'=16,'tp'=8] {'tp'}, dimensions={0} | all-to-all | bytes 262144 | tf_op jit(solution)/shard_map/all_to_all | solution.py:199
  147.5 0.6 reduce_sum.62
  (46 shorter events, 1.5 us)
Async XLA Ops:
  0.0 127.1 %copy-start = (bf16[1024,128]{1,0:T(8,128)(2,1)S(1)}, bf16[1024,128]{1,0:T(8,128)(2,1)}, u32[]{:S(2)}) copy-start(bf16[1024,128]{1,0:T(8,128)(2,1)} %param.21) | copy-start | bytes 786436
  1.4 27.7 %all-to-all-start = ((bf16[16,1,4,1024]{3,2,1,0:T(4,128)(2,1)}), bf16[16,1,4,1024]{3,2,1,0:T(4,128)(2,1)S(1)}, u32[]{:S(2)}, u32[]{:S(2)}) async-start(bf16[16,1,4,1024]{3,2,1,0:T(4,128)(2,1)} %broadcast_in_dim.25), calls=%async_computation | async-start | bytes 262144 | tf_op jit(solution)/shard_map/all_to_all | solution.py:23
  22.7 2.8 %copy-start.1 = (bf16[8,192,128]{2,1,0:T(8,128)(2,1)S(1)}, bf16[8,192,128]{2,1,0:T(8,128)(2,1)}, u32[]{:S(2)}) copy-start(bf16[8,192,128]{2,1,0:T(8,128)(2,1)} %param.17) | copy-start | bytes 1179652
  22.7 2.8 %copy-start.3 = (bf16[16,64,128]{2,1,0:T(8,128)(2,1)S(1)}, bf16[16,64,128]{2,1,0:T(8,128)(2,1)}, u32[]{:S(2)}) copy-start(bf16[16,64,128]{2,1,0:T(8,128)(2,1)} %param.19) | copy-start | bytes 786436
  22.7 2.8 %copy-start.6 = (bf16[1,4,128]{2,1,0:T(4,128)(2,1)S(1)}, bf16[1,4,128]{2,1,0:T(4,128)(2,1)}, u32[]{:S(2)}) copy-start(bf16[1,4,128]{2,1,0:T(4,128)(2,1)} %param.15) | copy-start | bytes 3076
  24.6 1.0 copy-start.2
  24.6 1.1 copy-start.4
  24.6 1.1 copy-start.7
  73.9 11.2 %copy-start.5 = (s32[64,4]{0,1:T(4,128)S(1)}, s32[64,4]{0,1:T(4,128)}, u32[]{:S(2)}) copy-start(s32[64,4]{0,1:T(4,128)} %param.27) | copy-start | bytes 3076
  76.0 21.9 %all-to-all-start.2 = ((f32[16,1,4160]{2,1,0:T(1,128)}), f32[16,1,4160]{2,1,0:T(1,128)S(1)}, u32[]{:S(2)}, u32[]{:S(2)}) async-start(f32[16,1,4160]{2,1,0:T(1,128)} %concatenate.36), calls=%async_computation.2 | async-start | bytes 540672 | tf_op jit(solution)/shard_map/all_to_all | solution.py:187

commit v9 on v8

--- a/solution.py
+++ b/solution.py
@@ -31,6 +31,9 @@
     )
     scores = scores * scale
     keep = keep_ref[...] > 0.5
+    pairs, n_keys = keep.shape
+    heads = scores.shape[0] // pairs
+    keep = jnp.broadcast_to(keep[:, None, :], (pairs, heads, n_keys)).reshape(pairs * heads, n_keys)
     masked = jnp.where(keep, scores, NEG)
     peak = jnp.max(masked, axis=1, keepdims=True)
     weights = jnp.exp(masked - jnp.maximum(peak, 0.5 * NEG))
@@ -53,12 +56,11 @@
     keys_t = jnp.pad(keys, pad).transpose(1, 0, 2)
     values_t = jnp.pad(values, pad).transpose(1, 0, 2)
     keep = jnp.pad(key_mask, ((0, 0), (0, 0), (0, padded - n_keys))).astype(jnp.bfloat16)
-    keep = jnp.broadcast_to(keep[:, :, None, :], (requests, new, hpk, padded))
-    keep = keep.reshape(rows, padded)
+    keep = keep.reshape(requests * new, padded)
     q_rows = query_all.transpose(2, 0, 1, 3, 4).reshape(kv * rows, dim)
     row_block = pl.BlockSpec((block, dim), lambda i: (i, 0))
     kv_block = pl.BlockSpec((1, padded, dim), lambda i: (i // steps, 0, 0))
-    keep_block = pl.BlockSpec((block, padded), lambda i: (i % steps, 0))
+    keep_block = pl.BlockSpec((block // hpk, padded), lambda i: (i % steps, 0))
     stat = jax.ShapeDtypeStruct((kv * rows, dim), jnp.float32)
     out, peak, total = pl.pallas_call(
         functools.partial(attend_kernel, scale),

time: 149 us -> 146 us (0.980)
  local copies, waits for them, and re-layouts: 15 us -> 10.5 us
  Pallas kernels: 14.4 us -> 16.9 us
  starting transfers between devices: 24.8 us -> 26.4 us
    broadcast_in_dim x1 -> x0, local copies, waits for them, and re-layouts: 4.83 us -> none  [attend(): keep = jnp.broadcast_to(keep[:, :, None, :], (requests, new, hpk, padded))]
    pallas_call x1, Pallas kernels: 14.4 us -> 16.9 us  [attend(): pl.pallas_call(functools.partial(attend_kernel, scale), grid=(kv * steps,...]
    all_to_all x1, starting transfers between devices: 9.1 us -> 10.7 us  [local(): received = lax.all_to_all(packed, 'sz', 0, 0, tiled=True)]
  transfers between devices with their start and end apart: 2 -> 2, of which waited for: 2 -> 2; matrix products, arithmetic and copies ran while one was open for 6% -> 7% of each run, Pallas kernels for 0% -> 0%
where the time goes in v9:
time: 146 us
  blocking collectives  69.1 us (47%)
  starting transfers between devices  26.4 us (18%)
  Pallas kernels  16.9 us (12%)
  waiting for transfers between devices  14 us (10%)
  local copies, waits for them, and re-layouts  10.5 us (7%)
  other arithmetic  7.98 us (5%)
    all_gather x2, blocking collectives, gather_rows(): return lax.all_gather(block, 'sx', axis=0, tiled=True)  20.7 us
    all_to_all x1, blocking collectives, local(): blocks = lax.all_to_all(terms, 'tp', 0, 0, tiled=True)  20.2 us
    all_to_all x1, blocking collectives, gather_rows(): block = lax.all_to_all(copies, 'sz', 0, 0, tiled=True)  18 us
    pallas_call x1, Pallas kernels, attend(): pl.pallas_call(functools.partial(attend_kernel, scale), grid=(kv * steps,...  16.9 us
    all_to_all x1, starting transfers between devices, gather_rows(): block = lax.all_to_all(copies, 'sz', 0, 0, tiled=True)  15.7 us
    all_to_all x1, waiting for transfers between devices, local(): received = lax.all_to_all(packed, 'sz', 0, 0, tiled=True)  12.7 us
    all_to_all x1, starting transfers between devices, local(): received = lax.all_to_all(packed, 'sz', 0, 0, tiled=True)  10.7 us
    all_to_all x1, blocking collectives, local(): lax.all_to_all(packed, 'sx', 0, 0, tiled=True).astype(jnp.float32)  10.2 us
  transfers between devices with their start and end apart: 2, of which 2 were waited for; matrix products, arithmetic and copies ran while one was open for 7% of the time, Pallas kernels for 0%

profile of v9, /device:TPU:1, one launch (start us, length us, event | category | flops | bytes accessed | tf_op | source)
XLA Modules:
  0.0 145.5 jit_solution(2951130849337665017)
XLA Ops:
  0.0 1.4 broadcast_in_dim.23
  1.4 15.7 %all-to-all-start = ((bf16[16,1,4,1024]{3,2,1,0:T(4,128)(2,1)}), bf16[16,1,4,1024]{3,2,1,0:T(4,128)(2,1)S(1)}, u32[]{:S(2)}, u32[]{:S(2)}) async-start(bf16[16,1,4,1024]{3,2,1,0:T(4,128)(2,1)} %broadcast_in_dim.23), calls=%async_computation | async-start | bytes 262144 | tf_op jit(solution)/shard_map/all_to_all | solution.py:23
  17.2 0.7 iota_compare_fusion.2
  17.9 0.8 select_reduce_fusion
  18.8 0.8 broadcast_reduce_fusion.1
  19.6 0.7 broadcast_multiply_fusion
  20.2 0.7 broadcast_compare_fusion
  21.0 0.1 copy.17
  21.3 0.7 iota_compare_fusion.1
  22.1 0.1 and.62
  22.2 0.3 and.63
  22.5 0.2 and.66
  22.7 0.2 and.67
  22.9 0.7 sub.34
  23.7 0.1 and_and_fusion
  23.8 0.1 compare_and_fusion
  23.9 0.2 broadcast_in_dim.27
  24.2 0.4 broadcast_in_dim.24
  24.5 0.8 pad_add_fusion
  25.4 0.8 pad_convert_fusion
  26.2 0.2 copy-done.1
  26.5 1.3 reshape.347.keep_ref
  27.9 1.3 all-to-all-done
  29.2 10.2 %all-gather = bf16[64,1,4,1024]{3,2,1,0:T(4,128)(2,1)S(1)} all-gather(bf16[16,1,4,1024]{3,2,1,0:T(4,128)(2,1)S(1)} %all-to-all-done), channel_id=2, replica_groups=mesh['sx'=4,'sz'=16,'tp'=8] {'sx'}, dimensions={0}, use_global_device_ids=true | all-gather | bytes 655360 | tf_op jit(solution)/shard_map/all_gather | solution.py:25
  39.4 0.2 reshape_transpose_reshape.3.q_ref
  39.6 16.9 %shard_map.136 = (f32[2048,128]{1,0:T(8,128)S(1)}, f32[2048,128]{1,0:T(8,128)S(1)}, f32[2048,128]{1,0:T(8,128)S(1)}) custom-call(bf16[2048,128]{1,0:T(8,128)(2,1)S(1)} %reshape_transpose_reshape.3.q_ref, bf16[1,2688,128]{2,1,0:T(8,128)(2,1)S(1)} %fusion.9.k_ref, bf16[1,2688,128]{2,1,0:T(8,128)(2,1)S(1)} %fusion.12.v_ref, bf16[256,2688]{1,0:T(8,128)(2,1)} %reshape.347.keep_ref), custom_call_target="tpu_custom_call" | custom-call | tf_op jit(solution)/shard_map/pallas_call | solution.py:65
  56.5 0.6 slice_reduce_fusion
  57.3 0.2 reshape_reshape_transpose_reshape.3
  57.6 0.3 mul.91
  57.9 0.2 mul.92
  58.1 0.1 fusion.13
  58.2 0.2 concatenate.35
  58.5 10.2 %all_to_all.29 = bf16[4,16,1,4160]{3,1,2,0:T(8,128)(2,1)S(1)} all-to-all(bf16[4,16,1,4160]{3,1,2,0:T(8,128)(2,1)S(1)} %concatenate.35), channel_id=1, replica_groups=mesh['sx'=4,'sz'=16,'tp'=8] {'sx'}, dimensions={0} | all-to-all | bytes 1064960 | tf_op jit(solution)/shard_map/all_to_all | solution.py:186
  68.8 0.3 mul.96
  69.1 0.2 mul.97
  69.5 0.3 reshape.344
  69.7 1.8 %concatenate.36 = f32[16,1,4160]{2,1,0:T(1,128)} concatenate(f32[16,1,4096]{2,1,0:T(1,128)S(1)} %reshape.344, f32[16,1,32]{2,1,0:T(1,128)S(1)} %bitcast.44, f32[16,1,32]{2,1,0:T(1,128)S(1)} %bitcast.45), dimensions={2} | concatenate | bytes 532480 | tf_op jit(solution)/shard_map/concatenate | solution.py:188
  71.5 10.7 %all-to-all-start.2 = ((f32[16,1,4160]{2,1,0:T(1,128)}), f32[16,1,4160]{2,1,0:T(1,128)S(1)}, u32[]{:S(2)}, u32[]{:S(2)}) async-start(f32[16,1,4160]{2,1,0:T(1,128)} %concatenate.36), calls=%async_computation.2 | async-start | bytes 540672 | tf_op jit(solution)/shard_map/all_to_all | solution.py:189
  82.2 0.2 convert_reduce_fusion
  82.4 12.7 %all-to-all-done.2 = f32[16,1,4160]{2,1,0:T(1,128)S(1)} async-done(((f32[16,1,4160]{2,1,0:T(1,128)}), f32[16,1,4160]{2,1,0:T(1,128)S(1)}, u32[]{:S(2)}, u32[]{:S(2)}) %all-to-all-start.2) | async-done | bytes 266272 | tf_op jit(solution)/shard_map/all_to_all | solution.py:189
  95.1 0.1 fusion.18
  95.4 0.1 mul.101
  95.5 0.3 fusion.14
  95.9 18.0 %all_to_all.30 = bf16[16,4,1024]{2,1,0:T(4,128)(2,1)S(1)} all-to-all(bf16[16,4,1024]{2,1,0:T(4,128)(2,1)S(1)} %broadcast_in_dim.28), channel_id=1, replica_groups=mesh['sx'=4,'sz'=16,'tp'=8] {'sz'}, dimensions={0} | all-to-all | bytes 262144 | tf_op jit(solution)/shard_map/all_to_all | solution.py:23
  113.9 10.5 %all_gather.7 = bf16[256,1024]{1,0:T(8,128)(2,1)S(1)} all-gather(bf16[64,1024]{1,0:T(8,128)(2,1)S(1)} %reshape.345), channel_id=1, replica_groups=mesh['sx'=4,'sz'=16,'tp'=8] {'sx'}, dimensions={0}, use_global_device_ids=true | all-gather | bytes 655360 | tf_op jit(solution)/shard_map/all_gather | solution.py:25
  124.4 0.3 fusion.19
  124.7 20.2 %all_to_all.31 = f32[8,32,128]{2,1,0:T(8,128)S(1)} all-to-all(f32[8,32,128]{2,1,0:T(8,128)S(1)} %bitcast.39), channel_id=1, replica_groups=mesh['sx'=4,'sz'=16,'tp'=8] {'tp'}, dimensions={0} | all-to-all | bytes 262144 | tf_op jit(solution)/shard_map/all_to_all | solution.py:201
  144.9 0.6 reduce_sum.62
  (46 shorter events, 1.5 us)
Async XLA Ops:
  0.0 124.4 %copy-start = (bf16[1024,128]{1,0:T(8,128)(2,1)S(1)}, bf16[1024,128]{1,0:T(8,128)(2,1)}, u32[]{:S(2)}) copy-start(bf16[1024,128]{1,0:T(8,128)(2,1)} %param.21) | copy-start | bytes 786436
  1.4 27.7 %all-to-all-start = ((bf16[16,1,4,1024]{3,2,1,0:T(4,128)(2,1)}), bf16[16,1,4,1024]{3,2,1,0:T(4,128)(2,1)S(1)}, u32[]{:S(2)}, u32[]{:S(2)}) async-start(bf16[16,1,4,1024]{3,2,1,0:T(4,128)(2,1)} %broadcast_in_dim.23), calls=%async_computation | async-start | bytes 262144 | tf_op jit(solution)/shard_map/all_to_all | solution.py:23
  25.4 1.0 copy-start.1
  25.4 1.1 copy-start.3
  25.4 1.1 copy-start.6
  26.5 1.3 copy-start.2
  26.5 1.3 copy-start.4
  26.5 1.3 copy-start.7
  69.4 12.7 %copy-start.5 = (s32[64,4]{0,1:T(4,128)S(1)}, s32[64,4]{0,1:T(4,128)}, u32[]{:S(2)}) copy-start(s32[64,4]{0,1:T(4,128)} %param.27) | copy-start | bytes 3076
  71.5 23.6 %all-to-all-start.2 = ((f32[16,1,4160]{2,1,0:T(1,128)}), f32[16,1,4160]{2,1,0:T(1,128)S(1)}, u32[]{:S(2)}, u32[]{:S(2)}) async-start(f32[16,1,4160]{2,1,0:T(1,128)} %concatenate.36), calls=%async_computation.2 | async-start | bytes 540672 | tf_op jit(solution)/shard_map/all_to_all | solution.py:189

commit v10 on v9

--- a/solution.py
+++ b/solution.py
@@ -185,8 +185,8 @@
     packed = packed.reshape(outer, inner, req_dev, width)
     received = lax.all_to_all(packed, "sx", 0, 0, tiled=True).astype(jnp.float32)
     stage_out, stage_peak, stage_total = merge(received, n_out, n_stat)
-    packed = jnp.concatenate([stage_out, stage_peak, stage_total], axis=-1)
-    received = lax.all_to_all(packed, "sz", 0, 0, tiled=True)
+    packed = jnp.concatenate([stage_out, stage_peak, stage_total], axis=-1).astype(jnp.bfloat16)
+    received = lax.all_to_all(packed, "sz", 0, 0, tiled=True).astype(jnp.float32)
     final_out, _, final_total = merge(received, n_out, n_stat)
     final_out = final_out.reshape(req_dev, NEW, kv_local, HPK, HEAD_DIM)
     final_total = final_total.reshape(req_dev, NEW, kv_local, HPK)

time: 146 us -> 145 us (level)
  blocking collectives: 69.1 us -> 67.2 us
    all_to_all x1, blocking collectives: 18 us -> 16 us  [gather_rows(): block = lax.all_to_all(copies, 'sz', 0, 0, tiled=True)]
where the time goes in v10:
time: 145 us; the launch traced here: 144 us
  blocking collectives  67.2 us (46%)
  starting transfers between devices  25.8 us (18%)
  Pallas kernels  16.9 us (12%)
  waiting for transfers between devices  13.7 us (9%)
  local copies, waits for them, and re-layouts  10.9 us (8%)
  other arithmetic  9.09 us (6%)
    all_gather x2, blocking collectives, gather_rows(): return lax.all_gather(block, 'sx', axis=0, tiled=True)  20.7 us
    all_to_all x1, blocking collectives, local(): blocks = lax.all_to_all(terms, 'tp', 0, 0, tiled=True)  20.2 us
    pallas_call x1, Pallas kernels, attend(): pl.pallas_call(functools.partial(attend_kernel, scale), grid=(kv * steps,...  16.9 us
    all_to_all x1, blocking collectives, gather_rows(): block = lax.all_to_all(copies, 'sz', 0, 0, tiled=True)  16 us
    all_to_all x1, starting transfers between devices, gather_rows(): block = lax.all_to_all(copies, 'sz', 0, 0, tiled=True)  15.7 us
    all_to_all x1, waiting for transfers between devices, local(): lax.all_to_all(packed, 'sz', 0, 0, tiled=True).astype(jnp.float32)  11.8 us
    all_to_all x1, blocking collectives, local(): lax.all_to_all(packed, 'sx', 0, 0, tiled=True).astype(jnp.float32)  10.2 us
    all_to_all x1, starting transfers between devices, local(): lax.all_to_all(packed, 'sz', 0, 0, tiled=True).astype(jnp.float32)  10 us
  transfers between devices with their start and end apart: 2, of which 2 were waited for; matrix products, arithmetic and copies ran while one was open for 7% of the time, Pallas kernels for 0%

profile of v10, /device:TPU:1, one launch (start us, length us, event | category | flops | bytes accessed | tf_op | source)
XLA Modules:
  0.0 144.2 jit_solution(14699195079878000140)
XLA Ops:
  0.0 1.4 %broadcast_in_dim.23 = bf16[16,1,4,1024]{3,2,1,0:T(4,128)(2,1)} broadcast(bf16[4,1024]{1,0:T(4,128)(2,1)} %bitcast.53), dimensions={2,3} | broadcast | bytes 139264 | tf_op jit(solution)/shard_map/broadcast_in_dim | solution.py:22
  1.4 15.7 %all-to-all-start = ((bf16[16,1,4,1024]{3,2,1,0:T(4,128)(2,1)}), bf16[16,1,4,1024]{3,2,1,0:T(4,128)(2,1)S(1)}, u32[]{:S(2)}, u32[]{:S(2)}) async-start(bf16[16,1,4,1024]{3,2,1,0:T(4,128)(2,1)} %broadcast_in_dim.23), calls=%async_computation | async-start | bytes 262144 | tf_op jit(solution)/shard_map/all_to_all | solution.py:23
  17.2 0.7 broadcast_reduce_fusion.1
  18.0 0.7 iota_compare_fusion.2
  18.7 0.8 select_reduce_fusion
  19.7 0.1 and.62
  19.9 0.3 and.63
  20.1 0.7 broadcast_compare_fusion
  20.8 0.1 copy.20
  20.9 0.7 iota_compare_fusion.1
  21.6 0.2 and.66
  21.8 0.2 and.67
  22.0 0.7 broadcast_multiply_fusion
  23.0 0.1 and_and_fusion
  23.3 0.4 broadcast_in_dim.24
  23.7 0.2 broadcast_in_dim.27
  23.9 0.8 pad_add_fusion
  24.8 0.8 pad_convert_fusion
  25.6 0.2 copy-done.1
  25.9 1.3 reshape.399.keep_ref
  27.3 1.9 %all-to-all-done = bf16[16,1,4,1024]{3,2,1,0:T(4,128)(2,1)S(1)} async-done(((bf16[16,1,4,1024]{3,2,1,0:T(4,128)(2,1)}), bf16[16,1,4,1024]{3,2,1,0:T(4,128)(2,1)S(1)}, u32[]{:S(2)}, u32[]{:S(2)}) %all-to-all-start) | async-done | bytes 131104 | tf_op jit(solution)/shard_map/all_to_all | solution.py:23
  29.2 10.2 %all-gather = bf16[64,1,4,1024]{3,2,1,0:T(4,128)(2,1)S(1)} all-gather(bf16[16,1,4,1024]{3,2,1,0:T(4,128)(2,1)S(1)} %all-to-all-done), channel_id=2, replica_groups=mesh['sx'=4,'sz'=16,'tp'=8] {'sx'}, dimensions={0}, use_global_device_ids=true | all-gather | bytes 655360 | tf_op jit(solution)/shard_map/all_gather | solution.py:25
  39.4 0.2 reshape_transpose_reshape.3.q_ref
  39.6 16.9 %shard_map.136 = (f32[2048,128]{1,0:T(8,128)S(1)}, f32[2048,128]{1,0:T(8,128)S(1)}, f32[2048,128]{1,0:T(8,128)S(1)}) custom-call(bf16[2048,128]{1,0:T(8,128)(2,1)S(1)} %reshape_transpose_reshape.3.q_ref, bf16[1,2688,128]{2,1,0:T(8,128)(2,1)S(1)} %fusion.9.k_ref, bf16[1,2688,128]{2,1,0:T(8,128)(2,1)S(1)} %fusion.12.v_ref, bf16[256,2688]{1,0:T(8,128)(2,1)} %reshape.399.keep_ref), custom_call_target="tpu_custom_call" | custom-call | tf_op jit(solution)/shard_map/pallas_call | solution.py:65
  56.5 0.6 slice_reduce_fusion
  57.4 0.3 mul.91
  57.7 0.2 mul.92
  57.9 0.2 reshape_reshape_transpose_reshape.3
  58.1 0.9 fusion.13
  59.0 1.1 concatenate.50
  60.1 10.2 %all_to_all.29 = bf16[4,16,1,4160]{3,1,2,0:T(8,128)(2,1)S(1)} all-to-all(bf16[4,16,1,4160]{3,1,2,0:T(8,128)(2,1)S(1)} %concatenate.50), channel_id=1, replica_groups=mesh['sx'=4,'sz'=16,'tp'=8] {'sx'}, dimensions={0} | all-to-all | bytes 1064960 | tf_op jit(solution)/shard_map/all_to_all | solution.py:186
  70.5 0.3 mul.96
  70.9 0.2 mul.97
  71.3 0.5 broadcast.166
  71.8 0.7 reduce.22
  72.5 0.8 reshape.415
  73.3 10.0 %all-to-all-start.2 = ((bf16[16,2,2080]{2,1,0:T(2,128)(2,1)}), bf16[16,2,2080]{2,1,0:T(2,128)(2,1)S(1)}, u32[]{:S(2)}, u32[]{:S(2)}) async-start(bf16[16,2,2080]{2,1,0:T(2,128)(2,1)} %reshape.415), calls=%async_computation.2 | async-start | bytes 278528 | tf_op jit(solution)/shard_map/all_to_all | solution.py:189
  83.3 0.2 convert_reduce_fusion
  83.5 11.8 %all-to-all-done.2 = bf16[16,2,2080]{2,1,0:T(2,128)(2,1)S(1)} async-done(((bf16[16,2,2080]{2,1,0:T(2,128)(2,1)}), bf16[16,2,2080]{2,1,0:T(2,128)(2,1)S(1)}, u32[]{:S(2)}, u32[]{:S(2)}) %all-to-all-start.2) | async-done | bytes 133152 | tf_op jit(solution)/shard_map/all_to_all | solution.py:189
  95.3 0.2 reshape.416
  95.5 0.3 convert_element_type.91
  95.9 0.1 mul.101
  96.0 0.3 fusion.14
  96.6 16.0 %all_to_all.30 = bf16[16,4,1024]{2,1,0:T(4,128)(2,1)S(1)} all-to-all(bf16[16,4,1024]{2,1,0:T(4,128)(2,1)S(1)} %broadcast_in_dim.28), channel_id=1, replica_groups=mesh['sx'=4,'sz'=16,'tp'=8] {'sz'}, dimensions={0} | all-to-all | bytes 262144 | tf_op jit(solution)/shard_map/all_to_all | solution.py:23
  112.7 10.5 %all_gather.7 = bf16[256,1024]{1,0:T(8,128)(2,1)S(1)} all-gather(bf16[64,1024]{1,0:T(8,128)(2,1)S(1)} %reshape.397), channel_id=1, replica_groups=mesh['sx'=4,'sz'=16,'tp'=8] {'sx'}, dimensions={0}, use_global_device_ids=true | all-gather | bytes 655360 | tf_op jit(solution)/shard_map/all_gather | solution.py:25
  123.1 0.3 fusion.19
  123.4 20.2 %all_to_all.31 = f32[8,32,128]{2,1,0:T(8,128)S(1)} all-to-all(f32[8,32,128]{2,1,0:T(8,128)S(1)} %bitcast.46), channel_id=1, replica_groups=mesh['sx'=4,'sz'=16,'tp'=8] {'tp'}, dimensions={0} | all-to-all | bytes 262144 | tf_op jit(solution)/shard_map/all_to_all | solution.py:201
  143.6 0.6 reduce_sum.59
  (53 shorter events, 1.9 us)
Async XLA Ops:
  0.0 123.1 %copy-start = (bf16[1024,128]{1,0:T(8,128)(2,1)S(1)}, bf16[1024,128]{1,0:T(8,128)(2,1)}, u32[]{:S(2)}) copy-start(bf16[1024,128]{1,0:T(8,128)(2,1)} %param.21) | copy-start | bytes 786436
  0.0 23.0 %copy-start.8 = (s32[64]{0:T(128)S(1)}, s32[64]{0:T(128)}, u32[]{:S(2)}) copy-start(s32[64]{0:T(128)} %param.24) | copy-start | bytes 772
  1.4 27.7 %all-to-all-start = ((bf16[16,1,4,1024]{3,2,1,0:T(4,128)(2,1)}), bf16[16,1,4,1024]{3,2,1,0:T(4,128)(2,1)S(1)}, u32[]{:S(2)}, u32[]{:S(2)}) async-start(bf16[16,1,4,1024]{3,2,1,0:T(4,128)(2,1)} %broadcast_in_dim.23), calls=%async_computation | async-start | bytes 262144 | tf_op jit(solution)/shard_map/all_to_all | solution.py:23
  24.8 1.0 copy-start.1
  24.8 1.1 copy-start.3
  24.8 1.1 copy-start.6
  25.9 1.3 copy-start.2
  25.9 1.3 copy-start.4
  25.9 1.3 copy-start.7
  71.1 12.2 %copy-start.5 = (s32[64,4]{0,1:T(4,128)S(1)}, s32[64,4]{0,1:T(4,128)}, u32[]{:S(2)}) copy-start(s32[64,4]{0,1:T(4,128)} %param.27) | copy-start | bytes 3076
  73.3 22.0 %all-to-all-start.2 = ((bf16[16,2,2080]{2,1,0:T(2,128)(2,1)}), bf16[16,2,2080]{2,1,0:T(2,128)(2,1)S(1)}, u32[]{:S(2)}, u32[]{:S(2)}) async-start(bf16[16,2,2080]{2,1,0:T(2,128)(2,1)} %reshape.415), calls=%async_computation.2 | async-start | bytes 278528 | tf_op jit(solution)/shard_map/all_to_all | solution.py:189

commit v11 on v10

--- a/solution.py
+++ b/solution.py
@@ -50,7 +50,7 @@
     n_keys = keys.shape[0]
     padded = -(-n_keys // 128) * 128
     rows = requests * new * hpk
-    block = 256 if rows % 256 == 0 else rows
+    block = 512 if rows % 512 == 0 else rows
     steps = rows // block
     pad = ((0, padded - n_keys), (0, 0), (0, 0))
     keys_t = jnp.pad(keys, pad).transpose(1, 0, 2)

time: 145 us -> 146 us (level)
  no operation moved by 1% of the time
where the time goes in v11:
time: 146 us; the launch traced here: 145 us
  blocking collectives  67.2 us (46%)
  starting transfers between devices  25.8 us (18%)
  Pallas kernels  18.1 us (12%)
  waiting for transfers between devices  13.7 us (9%)
  local copies, waits for them, and re-layouts  10.9 us (7%)
  other arithmetic  9.09 us (6%)
    all_gather x2, blocking collectives, gather_rows(): return lax.all_gather(block, 'sx', axis=0, tiled=True)  20.7 us
    all_to_all x1, blocking collectives, local(): blocks = lax.all_to_all(terms, 'tp', 0, 0, tiled=True)  20.2 us
    pallas_call x1, Pallas kernels, attend(): pl.pallas_call(functools.partial(attend_kernel, scale), grid=(kv * steps,...  18.1 us
    all_to_all x1, blocking collectives, gather_rows(): block = lax.all_to_all(copies, 'sz', 0, 0, tiled=True)  16 us
    all_to_all x1, starting transfers between devices, gather_rows(): block = lax.all_to_all(copies, 'sz', 0, 0, tiled=True)  15.7 us
    all_to_all x1, waiting for transfers between devices, local(): lax.all_to_all(packed, 'sz', 0, 0, tiled=True).astype(jnp.float32)  11.8 us
    all_to_all x1, blocking collectives, local(): lax.all_to_all(packed, 'sx', 0, 0, tiled=True).astype(jnp.float32)  10.2 us
    all_to_all x1, starting transfers between devices, local(): lax.all_to_all(packed, 'sz', 0, 0, tiled=True).astype(jnp.float32)  10 us
  transfers between devices with their start and end apart: 2, of which 2 were waited for; matrix products, arithmetic and copies ran while one was open for 7% of the time, Pallas kernels for 0%

profile of v11, /device:TPU:1, one launch (start us, length us, event | category | flops | bytes accessed | tf_op | source)
XLA Modules:
  0.0 145.5 jit_solution(7314079937001385188)
XLA Ops:
  0.0 1.4 broadcast_in_dim.23
  1.4 15.7 %all-to-all-start = ((bf16[16,1,4,1024]{3,2,1,0:T(4,128)(2,1)}), bf16[16,1,4,1024]{3,2,1,0:T(4,128)(2,1)S(1)}, u32[]{:S(2)}, u32[]{:S(2)}) async-start(bf16[16,1,4,1024]{3,2,1,0:T(4,128)(2,1)} %broadcast_in_dim.23), calls=%async_computation | async-start | bytes 262144 | tf_op jit(solution)/shard_map/all_to_all | solution.py:23
  17.2 0.7 broadcast_reduce_fusion.1
  18.0 0.7 iota_compare_fusion.2
  18.7 0.8 select_reduce_fusion
  19.7 0.1 and.62
  19.9 0.3 and.63
  20.1 0.7 broadcast_compare_fusion
  20.8 0.1 copy.20
  20.9 0.7 iota_compare_fusion.1
  21.6 0.2 and.66
  21.8 0.2 and.67
  22.0 0.7 broadcast_multiply_fusion
  23.0 0.1 and_and_fusion
  23.3 0.4 broadcast_in_dim.24
  23.7 0.2 broadcast_in_dim.27
  23.9 0.8 pad_add_fusion
  24.8 0.8 pad_convert_fusion
  25.6 0.2 copy-done.1
  25.9 1.3 reshape.399.keep_ref
  27.3 1.9 %all-to-all-done = bf16[16,1,4,1024]{3,2,1,0:T(4,128)(2,1)S(1)} async-done(((bf16[16,1,4,1024]{3,2,1,0:T(4,128)(2,1)}), bf16[16,1,4,1024]{3,2,1,0:T(4,128)(2,1)S(1)}, u32[]{:S(2)}, u32[]{:S(2)}) %all-to-all-start) | async-done | bytes 131104 | tf_op jit(solution)/shard_map/all_to_all | solution.py:23
  29.2 10.2 %all-gather = bf16[64,1,4,1024]{3,2,1,0:T(4,128)(2,1)S(1)} all-gather(bf16[16,1,4,1024]{3,2,1,0:T(4,128)(2,1)S(1)} %all-to-all-done), channel_id=2, replica_groups=mesh['sx'=4,'sz'=16,'tp'=8] {'sx'}, dimensions={0}, use_global_device_ids=true | all-gather | bytes 655360 | tf_op jit(solution)/shard_map/all_gather | solution.py:25
  39.4 0.2 reshape_transpose_reshape.3.q_ref
  39.6 18.1 %shard_map.136 = (f32[2048,128]{1,0:T(8,128)S(1)}, f32[2048,128]{1,0:T(8,128)S(1)}, f32[2048,128]{1,0:T(8,128)S(1)}) custom-call(bf16[2048,128]{1,0:T(8,128)(2,1)S(1)} %reshape_transpose_reshape.3.q_ref, bf16[1,2688,128]{2,1,0:T(8,128)(2,1)S(1)} %fusion.9.k_ref, bf16[1,2688,128]{2,1,0:T(8,128)(2,1)S(1)} %fusion.12.v_ref, bf16[256,2688]{1,0:T(8,128)(2,1)} %reshape.399.keep_ref), custom_call_target="tpu_custom_call" | custom-call | tf_op jit(solution)/shard_map/pallas_call | solution.py:65
  57.7 0.6 slice_reduce_fusion
  58.6 0.3 mul.91
  58.9 0.2 mul.92
  59.1 0.2 reshape_reshape_transpose_reshape.3
  59.3 0.9 fusion.13
  60.2 1.1 concatenate.50
  61.4 10.2 %all_to_all.29 = bf16[4,16,1,4160]{3,1,2,0:T(8,128)(2,1)S(1)} all-to-all(bf16[4,16,1,4160]{3,1,2,0:T(8,128)(2,1)S(1)} %concatenate.50), channel_id=1, replica_groups=mesh['sx'=4,'sz'=16,'tp'=8] {'sx'}, dimensions={0} | all-to-all | bytes 1064960 | tf_op jit(solution)/shard_map/all_to_all | solution.py:186
  71.7 0.3 mul.96
  72.1 0.2 mul.97
  72.5 0.5 broadcast.166
  73.0 0.7 reduce.22
  73.7 0.8 reshape.415
  74.5 10.0 %all-to-all-start.2 = ((bf16[16,2,2080]{2,1,0:T(2,128)(2,1)}), bf16[16,2,2080]{2,1,0:T(2,128)(2,1)S(1)}, u32[]{:S(2)}, u32[]{:S(2)}) async-start(bf16[16,2,2080]{2,1,0:T(2,128)(2,1)} %reshape.415), calls=%async_computation.2 | async-start | bytes 278528 | tf_op jit(solution)/shard_map/all_to_all | solution.py:189
  84.5 0.2 convert_reduce_fusion
  84.7 11.8 %all-to-all-done.2 = bf16[16,2,2080]{2,1,0:T(2,128)(2,1)S(1)} async-done(((bf16[16,2,2080]{2,1,0:T(2,128)(2,1)}), bf16[16,2,2080]{2,1,0:T(2,128)(2,1)S(1)}, u32[]{:S(2)}, u32[]{:S(2)}) %all-to-all-start.2) | async-done | bytes 133152 | tf_op jit(solution)/shard_map/all_to_all | solution.py:189
  96.5 0.2 reshape.416
  96.7 0.3 convert_element_type.91
  97.1 0.1 mul.101
  97.2 0.3 fusion.14
  97.8 16.0 %all_to_all.30 = bf16[16,4,1024]{2,1,0:T(4,128)(2,1)S(1)} all-to-all(bf16[16,4,1024]{2,1,0:T(4,128)(2,1)S(1)} %broadcast_in_dim.28), channel_id=1, replica_groups=mesh['sx'=4,'sz'=16,'tp'=8] {'sz'}, dimensions={0} | all-to-all | bytes 262144 | tf_op jit(solution)/shard_map/all_to_all | solution.py:23
  113.9 10.5 %all_gather.7 = bf16[256,1024]{1,0:T(8,128)(2,1)S(1)} all-gather(bf16[64,1024]{1,0:T(8,128)(2,1)S(1)} %reshape.397), channel_id=1, replica_groups=mesh['sx'=4,'sz'=16,'tp'=8] {'sx'}, dimensions={0}, use_global_device_ids=true | all-gather | bytes 655360 | tf_op jit(solution)/shard_map/all_gather | solution.py:25
  124.4 0.3 fusion.19
  124.7 20.2 %all_to_all.31 = f32[8,32,128]{2,1,0:T(8,128)S(1)} all-to-all(f32[8,32,128]{2,1,0:T(8,128)S(1)} %bitcast.46), channel_id=1, replica_groups=mesh['sx'=4,'sz'=16,'tp'=8] {'tp'}, dimensions={0} | all-to-all | bytes 262144 | tf_op jit(solution)/shard_map/all_to_all | solution.py:201
  144.9 0.6 reduce_sum.59
  (53 shorter events, 1.9 us)
Async XLA Ops:
  0.0 124.4 %copy-start = (bf16[1024,128]{1,0:T(8,128)(2,1)S(1)}, bf16[1024,128]{1,0:T(8,128)(2,1)}, u32[]{:S(2)}) copy-start(bf16[1024,128]{1,0:T(8,128)(2,1)} %param.21) | copy-start | bytes 786436
  0.0 23.0 %copy-start.8 = (s32[64]{0:T(128)S(1)}, s32[64]{0:T(128)}, u32[]{:S(2)}) copy-start(s32[64]{0:T(128)} %param.24) | copy-start | bytes 772
  1.4 27.7 %all-to-all-start = ((bf16[16,1,4,1024]{3,2,1,0:T(4,128)(2,1)}), bf16[16,1,4,1024]{3,2,1,0:T(4,128)(2,1)S(1)}, u32[]{:S(2)}, u32[]{:S(2)}) async-start(bf16[16,1,4,1024]{3,2,1,0:T(4,128)(2,1)} %broadcast_in_dim.23), calls=%async_computation | async-start | bytes 262144 | tf_op jit(solution)/shard_map/all_to_all | solution.py:23
  24.8 1.0 copy-start.1
  24.8 1.1 copy-start.3
  24.8 1.1 copy-start.6
  25.9 1.3 copy-start.2
  25.9 1.3 copy-start.4
  25.9 1.3 copy-start.7
  72.3 12.2 %copy-start.5 = (s32[64,4]{0,1:T(4,128)S(1)}, s32[64,4]{0,1:T(4,128)}, u32[]{:S(2)}) copy-start(s32[64,4]{0,1:T(4,128)} %param.27) | copy-start | bytes 3076
  74.5 22.0 %all-to-all-start.2 = ((bf16[16,2,2080]{2,1,0:T(2,128)(2,1)}), bf16[16,2,2080]{2,1,0:T(2,128)(2,1)S(1)}, u32[]{:S(2)}, u32[]{:S(2)}) async-start(bf16[16,2,2080]{2,1,0:T(2,128)(2,1)} %reshape.415), calls=%async_computation.2 | async-start | bytes 278528 | tf_op jit(solution)/shard_map/all_to_all | solution.py:189

commit v12 on v10

--- a/solution.py
+++ b/solution.py
@@ -198,7 +198,8 @@
     attention = gather_rows(attention)
     terms = jnp.dot(attention, out_weight, preferred_element_type=jnp.float32)
     n_tp = lax.axis_size("tp")
-    blocks = lax.all_to_all(terms, "tp", 0, 0, tiled=True)
+    blocks = lax.all_to_all(terms.astype(jnp.bfloat16), "tp", 0, 0, tiled=True)
+    blocks = blocks.astype(jnp.float32)
     blocks = blocks.reshape((n_tp, blocks.shape[0] // n_tp) + blocks.shape[1:])
     return jnp.sum(blocks, axis=0).astype(jnp.bfloat16)
 

time: 145 us -> 144 us (level)
  no operation moved by 1% of the time
where the time goes in v12:
time: 144 us
  blocking collectives  66.8 us (46%)
  starting transfers between devices  25.8 us (18%)
  Pallas kernels  16.9 us (12%)
  waiting for transfers between devices  13.7 us (10%)
  local copies, waits for them, and re-layouts  10.9 us (8%)
  other arithmetic  9.09 us (6%)
    all_gather x2, blocking collectives, gather_rows(): return lax.all_gather(block, 'sx', axis=0, tiled=True)  20.7 us
    all_to_all x1, blocking collectives, local(): blocks = lax.all_to_all(terms.astype(jnp.bfloat16), 'tp', 0, 0, tiled=True)  19.8 us
    pallas_call x1, Pallas kernels, attend(): pl.pallas_call(functools.partial(attend_kernel, scale), grid=(kv * steps,...  16.9 us
    all_to_all x1, blocking collectives, gather_rows(): block = lax.all_to_all(copies, 'sz', 0, 0, tiled=True)  16 us
    all_to_all x1, starting transfers between devices, gather_rows(): block = lax.all_to_all(copies, 'sz', 0, 0, tiled=True)  15.7 us
    all_to_all x1, waiting for transfers between devices, local(): lax.all_to_all(packed, 'sz', 0, 0, tiled=True).astype(jnp.float32)  11.8 us
    all_to_all x1, blocking collectives, local(): lax.all_to_all(packed, 'sx', 0, 0, tiled=True).astype(jnp.float32)  10.2 us
    all_to_all x1, starting transfers between devices, local(): lax.all_to_all(packed, 'sz', 0, 0, tiled=True).astype(jnp.float32)  10 us
  transfers between devices with their start and end apart: 2, of which 2 were waited for; matrix products, arithmetic and copies ran while one was open for 7% of the time, Pallas kernels for 0%

profile of v12, /device:TPU:1, one launch (start us, length us, event | category | flops | bytes accessed | tf_op | source)
XLA Modules:
  0.0 143.9 jit_solution(4780791891713216997)
XLA Ops:
  0.0 1.4 %broadcast_in_dim.23 = bf16[16,1,4,1024]{3,2,1,0:T(4,128)(2,1)} broadcast(bf16[4,1024]{1,0:T(4,128)(2,1)} %bitcast.53), dimensions={2,3} | broadcast | bytes 139264 | tf_op jit(solution)/shard_map/broadcast_in_dim | solution.py:22
  1.4 15.7 %all-to-all-start = ((bf16[16,1,4,1024]{3,2,1,0:T(4,128)(2,1)}), bf16[16,1,4,1024]{3,2,1,0:T(4,128)(2,1)S(1)}, u32[]{:S(2)}, u32[]{:S(2)}) async-start(bf16[16,1,4,1024]{3,2,1,0:T(4,128)(2,1)} %broadcast_in_dim.23), calls=%async_computation | async-start | bytes 262144 | tf_op jit(solution)/shard_map/all_to_all | solution.py:23
  17.2 0.7 broadcast_reduce_fusion.1
  18.0 0.7 iota_compare_fusion.2
  18.7 0.8 select_reduce_fusion
  19.7 0.1 and.62
  19.9 0.3 and.63
  20.1 0.7 broadcast_compare_fusion
  20.8 0.1 copy.20
  20.9 0.7 iota_compare_fusion.1
  21.6 0.2 and.66
  21.8 0.2 and.67
  22.0 0.7 broadcast_multiply_fusion
  23.0 0.1 and_and_fusion
  23.3 0.4 broadcast_in_dim.24
  23.7 0.2 broadcast_in_dim.27
  23.9 0.8 pad_add_fusion
  24.8 0.8 pad_convert_fusion
  25.6 0.2 copy-done.1
  25.9 1.3 reshape.398.keep_ref
  27.3 1.9 %all-to-all-done = bf16[16,1,4,1024]{3,2,1,0:T(4,128)(2,1)S(1)} async-done(((bf16[16,1,4,1024]{3,2,1,0:T(4,128)(2,1)}), bf16[16,1,4,1024]{3,2,1,0:T(4,128)(2,1)S(1)}, u32[]{:S(2)}, u32[]{:S(2)}) %all-to-all-start) | async-done | bytes 131104 | tf_op jit(solution)/shard_map/all_to_all | solution.py:23
  29.2 10.2 %all-gather = bf16[64,1,4,1024]{3,2,1,0:T(4,128)(2,1)S(1)} all-gather(bf16[16,1,4,1024]{3,2,1,0:T(4,128)(2,1)S(1)} %all-to-all-done), channel_id=2, replica_groups=mesh['sx'=4,'sz'=16,'tp'=8] {'sx'}, dimensions={0}, use_global_device_ids=true | all-gather | bytes 655360 | tf_op jit(solution)/shard_map/all_gather | solution.py:25
  39.4 0.2 reshape_transpose_reshape.3.q_ref
  39.6 16.9 %shard_map.136 = (f32[2048,128]{1,0:T(8,128)S(1)}, f32[2048,128]{1,0:T(8,128)S(1)}, f32[2048,128]{1,0:T(8,128)S(1)}) custom-call(bf16[2048,128]{1,0:T(8,128)(2,1)S(1)} %reshape_transpose_reshape.3.q_ref, bf16[1,2688,128]{2,1,0:T(8,128)(2,1)S(1)} %fusion.9.k_ref, bf16[1,2688,128]{2,1,0:T(8,128)(2,1)S(1)} %fusion.12.v_ref, bf16[256,2688]{1,0:T(8,128)(2,1)} %reshape.398.keep_ref), custom_call_target="tpu_custom_call" | custom-call | tf_op jit(solution)/shard_map/pallas_call | solution.py:65
  56.5 0.6 slice_reduce_fusion
  57.4 0.3 mul.91
  57.7 0.2 mul.92
  57.9 0.2 reshape_reshape_transpose_reshape.3
  58.1 0.9 fusion.13
  59.0 1.1 concatenate.50
  60.1 10.2 %all_to_all.29 = bf16[4,16,1,4160]{3,1,2,0:T(8,128)(2,1)S(1)} all-to-all(bf16[4,16,1,4160]{3,1,2,0:T(8,128)(2,1)S(1)} %concatenate.50), channel_id=1, replica_groups=mesh['sx'=4,'sz'=16,'tp'=8] {'sx'}, dimensions={0} | all-to-all | bytes 1064960 | tf_op jit(solution)/shard_map/all_to_all | solution.py:186
  70.5 0.3 mul.96
  70.9 0.2 mul.97
  71.3 0.5 broadcast.166
  71.8 0.7 reduce.22
  72.5 0.8 reshape.414
  73.3 10.0 %all-to-all-start.2 = ((bf16[16,2,2080]{2,1,0:T(2,128)(2,1)}), bf16[16,2,2080]{2,1,0:T(2,128)(2,1)S(1)}, u32[]{:S(2)}, u32[]{:S(2)}) async-start(bf16[16,2,2080]{2,1,0:T(2,128)(2,1)} %reshape.414), calls=%async_computation.2 | async-start | bytes 278528 | tf_op jit(solution)/shard_map/all_to_all | solution.py:189
  83.3 0.2 convert_reduce_fusion
  83.5 11.8 %all-to-all-done.2 = bf16[16,2,2080]{2,1,0:T(2,128)(2,1)S(1)} async-done(((bf16[16,2,2080]{2,1,0:T(2,128)(2,1)}), bf16[16,2,2080]{2,1,0:T(2,128)(2,1)S(1)}, u32[]{:S(2)}, u32[]{:S(2)}) %all-to-all-start.2) | async-done | bytes 133152 | tf_op jit(solution)/shard_map/all_to_all | solution.py:189
  95.3 0.2 reshape.415
  95.5 0.3 convert_element_type.94
  95.9 0.1 mul.101
  96.0 0.3 fusion.14
  96.6 16.0 %all_to_all.30 = bf16[16,4,1024]{2,1,0:T(4,128)(2,1)S(1)} all-to-all(bf16[16,4,1024]{2,1,0:T(4,128)(2,1)S(1)} %broadcast_in_dim.28), channel_id=1, replica_groups=mesh['sx'=4,'sz'=16,'tp'=8] {'sz'}, dimensions={0} | all-to-all | bytes 262144 | tf_op jit(solution)/shard_map/all_to_all | solution.py:23
  112.7 10.5 %all_gather.7 = bf16[256,1024]{1,0:T(8,128)(2,1)S(1)} all-gather(bf16[64,1024]{1,0:T(8,128)(2,1)S(1)} %reshape.396), channel_id=1, replica_groups=mesh['sx'=4,'sz'=16,'tp'=8] {'sx'}, dimensions={0}, use_global_device_ids=true | all-gather | bytes 655360 | tf_op jit(solution)/shard_map/all_gather | solution.py:25
  123.1 0.3 convolution_convert_fusion
  123.4 19.8 %all_to_all.31 = bf16[8,32,128]{2,1,0:T(8,128)(2,1)S(1)} all-to-all(bf16[8,32,128]{2,1,0:T(8,128)(2,1)S(1)} %bitcast.50), channel_id=1, replica_groups=mesh['sx'=4,'sz'=16,'tp'=8] {'tp'}, dimensions={0} | all-to-all | bytes 131072 | tf_op jit(solution)/shard_map/all_to_all | solution.py:201
  143.2 0.6 reduce_sum.62
  (53 shorter events, 1.9 us)
Async XLA Ops:
  0.0 123.1 %copy-start = (bf16[1024,128]{1,0:T(8,128)(2,1)S(1)}, bf16[1024,128]{1,0:T(8,128)(2,1)}, u32[]{:S(2)}) copy-start(bf16[1024,128]{1,0:T(8,128)(2,1)} %param.21) | copy-start | bytes 786436
  0.0 23.0 %copy-start.8 = (s32[64]{0:T(128)S(1)}, s32[64]{0:T(128)}, u32[]{:S(2)}) copy-start(s32[64]{0:T(128)} %param.24) | copy-start | bytes 772
  1.4 27.7 %all-to-all-start = ((bf16[16,1,4,1024]{3,2,1,0:T(4,128)(2,1)}), bf16[16,1,4,1024]{3,2,1,0:T(4,128)(2,1)S(1)}, u32[]{:S(2)}, u32[]{:S(2)}) async-start(bf16[16,1,4,1024]{3,2,1,0:T(4,128)(2,1)} %broadcast_in_dim.23), calls=%async_computation | async-start | bytes 262144 | tf_op jit(solution)/shard_map/all_to_all | solution.py:23
  24.8 1.0 copy-start.1
  24.8 1.1 copy-start.3
  24.8 1.1 copy-start.6
  25.9 1.3 copy-start.2
  25.9 1.3 copy-start.4
  25.9 1.3 copy-start.7
  71.1 12.2 %copy-start.5 = (s32[64,4]{0,1:T(4,128)S(1)}, s32[64,4]{0,1:T(4,128)}, u32[]{:S(2)}) copy-start(s32[64,4]{0,1:T(4,128)} %param.27) | copy-start | bytes 3076
  73.3 22.0 %all-to-all-start.2 = ((bf16[16,2,2080]{2,1,0:T(2,128)(2,1)}), bf16[16,2,2080]{2,1,0:T(2,128)(2,1)S(1)}, u32[]{:S(2)}, u32[]{:S(2)}) async-start(bf16[16,2,2080]{2,1,0:T(2,128)(2,1)} %reshape.414), calls=%async_computation.2 | async-start | bytes 278528 | tf_op jit(solution)/shard_map/all_to_all | solution.py:189
